TPU v7x, 32 devices: a whole 2x2x4 slice. The times are simulated.
32 devices in a mesh: rep: 2 (over x), tm: 8 (over z, y), mp: 2 (over core).
Axes of the slice: x: 2, y: 2, z: 4, core: 2. Of those that a mesh axis runs over, the one named last changes fastest.
Arguments:
- inputs: bfloat16 [8, 1024, 1024], P('rep', 'tm'), parts along dimension 0, may hold values from -6 to 6
- resets: int32 [8, 1024], P('rep', 'tm'), parts along dimension 0, may hold values 0 or 1
- actions: int32 [8, 8, 128, 4], P('rep', None, 'tm'), parts along dimension 0, may hold values from 0 to 17
- in_proj: bfloat16 [1024, 1024], P(None, 'mp'), may hold values from -0.1875 to 0.1875
- decay_rates: float32 [1024], replicated, may hold values from 0.00024414062 to 0.03
- readout_w: bfloat16 [1024, 1024], P('mp'), may hold values from -0.1875 to 0.1875
- norm_gain: float32 [1024], replicated, may hold values from 0.1 to 1.9
- w_hidden: bfloat16 [1024, 1024], P(None, 'mp'), may hold values from -0.1875 to 0.1875
- action_embed: bfloat16 [18, 1024], P(None, 'mp'), may hold values from -6 to 6
- w_out: bfloat16 [1024, 1024], P('mp'), may hold values from -0.1875 to 0.1875
Outputs:
- predicted: bfloat16 [8, 8, 128, 4, 1024], P('rep', None, 'tm', None, 'mp'), parts along dimension 0
There are 2 independent parts, one for each index of `rep`. A program takes and returns all parts, laid end to end along the dimension named above; an argument that names none is the same for every part. Nothing has to cross between parts.
All inputs are finite; a program needn't handle non-finite values. No bound on the sum of `resets` on one device may be relied on, other than what follows from the above.
Results may differ from a plain program's by a relative error of at most 0.015.
Values may be sent and summed in bfloat16 or wider, within the bound.
No kernel may reach another device: no remote copies, remote signals or barrier semaphores. Data moves between devices by JAX's collectives and lax.ppermute only.
A program may use at most 64 MiB of HBM per device.

v0:
```python
import jax
import jax.numpy as jnp
from jax import lax
from jax.sharding import PartitionSpec as P


def carried_in(value, axis, join, neutral):
    count, mine = (lax.axis_size(axis), lax.axis_index(axis))
    pieces = jax.tree.map(lambda part: lax.all_gather(part, axis), value)
    total = jax.tree.map(
        lambda part, zero: jnp.full_like(part, 0) + jnp.asarray(zero, part.dtype), value, neutral
    )

    def hop(position, total):
        longer = join(total, jax.tree.map(lambda part: part[position], pieces))
        return jax.tree.map(lambda new, old: jnp.where(position < mine, new, old), longer, total)

    return lax.fori_loop(0, count - 1, hop, total)


def shortened(value):

    def short(part):
        return part.astype(jnp.bfloat16) if part.dtype == jnp.float32 else part

    return jax.tree.map(short, value)


def combine(earlier, later):
    return (earlier[0] * later[0], later[0] * earlier[1] + later[1])


def hidden_units(features, norm_gain, w_hidden, action_embed, picked):
    mean_sq = jnp.mean(features * features, axis=-1, keepdims=True)
    normed = (features * lax.rsqrt(mean_sq + 1e-06) * norm_gain).astype(jnp.bfloat16)
    table_ids = jnp.arange(action_embed.shape[0], dtype=jnp.int32)
    one_hot = (picked[:, None] == table_ids[None, :]).astype(jnp.bfloat16)
    pre_act = jnp.dot(normed, w_hidden, preferred_element_type=jnp.float32) + jnp.dot(
        one_hot, action_embed, preferred_element_type=jnp.float32
    )
    return jax.nn.silu(pre_act).astype(jnp.bfloat16)


def per_device(
    inputs,
    resets,
    actions,
    in_proj,
    decay_rates,
    readout_w,
    norm_gain,
    w_hidden,
    action_embed,
    w_out,
):
    mp_index = lax.axis_index("mp")
    width_part = in_proj.shape[1]
    local_rates = lax.dynamic_slice_in_dim(decay_rates, mp_index * width_part, width_part)
    decays = jnp.exp(-local_rates)
    scaling = jnp.sqrt(1.0 - decays * decays)
    batch, steps, width = inputs.shape
    driven = (
        jnp.dot(
            inputs.reshape(batch * steps, width), in_proj, preferred_element_type=jnp.float32
        ).reshape(batch, steps, width_part)
        * scaling
    )
    keep_mask = (1 - resets).astype(jnp.float32)
    gates = keep_mask[:, :, None] * decays
    cumulative, local_states = lax.associative_scan(combine, (gates, driven), axis=1)
    identity = (
        jnp.ones((batch, width_part), jnp.float32),
        jnp.zeros((batch, width_part), jnp.float32),
    )
    entering = carried_in((cumulative[:, -1], local_states[:, -1]), "tm", combine, identity)
    carry_state = entering[1]
    corrected = local_states + cumulative * carry_state[:, None, :]
    posterior = lax.all_to_all(
        shortened(corrected.reshape(batch, 1, steps, width_part)),
        "tm",
        split_axis=2,
        concat_axis=1,
        tiled=True,
    )
    seqs, blocks, sub_steps, horizon = actions.shape
    rows = seqs * blocks * sub_steps
    current = posterior.reshape(rows, width_part)
    action_rows = actions.reshape(rows, horizon)
    outputs = []
    for step in range(horizon):
        features = lax.psum(
            jnp.dot(
                current.astype(jnp.bfloat16), readout_w, preferred_element_type=jnp.float32
            ).astype(jnp.bfloat16),
            "mp",
        ).astype(jnp.float32)
        hidden = hidden_units(features, norm_gain, w_hidden, action_embed, action_rows[:, step])
        guessed = lax.psum_scatter(
            jnp.dot(hidden, w_out, preferred_element_type=jnp.float32).astype(jnp.bfloat16),
            "mp",
            scatter_dimension=1,
            tiled=True,
        )
        outputs.append(guessed)
        if step < horizon - 1:
            full_guess = lax.all_gather(guessed, "mp", axis=1, tiled=True)
            current = decays * current + scaling * jnp.dot(
                full_guess, in_proj, preferred_element_type=jnp.float32
            )
    result = jnp.stack(outputs, axis=1)
    return result.reshape(seqs, blocks, sub_steps, horizon, result.shape[2])


def solution(mesh):
    in_specs = (
        P("rep", "tm", None),
        P("rep", "tm"),
        P("rep", None, "tm", None),
        P(None, "mp"),
        P(),
        P("mp", None),
        P(),
        P(None, "mp"),
        P(None, "mp"),
        P("mp", None),
    )
    out_specs = P("rep", None, "tm", None, "mp")
    return jax.shard_map(
        per_device, mesh=mesh, in_specs=in_specs, out_specs=out_specs, check_vma=False
    )
```

profile of v0, /device:TPU:0, one launch (start us, length us, event | category | flops | bytes accessed | tf_op | source)
XLA Modules:
  0.0 339.0 jit_solution(1014321069220786846)
XLA Ops:
  8.8 1.5 slice.219
  10.3 2.2 convolution_multiply_fusion.3
  12.6 1.5 slice.268
  14.1 1.5 slice.222
  15.6 1.5 slice.221
  17.1 1.4 multiply_add_fusion
  25.9 1.2 fusion.36
  29.0 2.0 pad.98
  31.0 4.3 %pad.99 = f32[4,128,512]{2,1,0:T(8,128)} pad(f32[4,64,512]{2,1,0:T(8,128)} %add.272, f32[]{:T(128)} %constant.52.clone.1), padding=0_0_0x1_0_1x0_0_0 | pad | bytes 1572868 | tf_op jit(solution)/shard_map/pad | solution.py:70
  36.2 32.4 %all-gather.1 = f32[32,1,512]{2,1,0:T(1,128)S(1)} all-gather(f32[4,1,512]{2,1,0:T(1,128)S(1)} %slice_add_fusion), channel_id=3, replica_groups=mesh['rep'=2,'tm'=8,'mp'=2] {'tm'}, dimensions={0}, use_global_device_ids=true | all-gather | bytes 73728 | tf_op jit(solution)/shard_map/all_gather | solution.py:9
  68.7 4.3 %pad.113 = f32[4,128,512]{2,1,0:T(8,128)} pad(f32[4,64,512]{2,1,0:T(8,128)} %add.280, f32[]{:T(128)} %constant.52.clone.1), padding=0_0_0x1_0_1x0_0_0 | pad | bytes 1572868 | tf_op jit(solution)/shard_map/pad | solution.py:70
  73.8 30.7 %all-gather = f32[32,1,512]{2,1,0:T(1,128)S(1)} all-gather(f32[4,1,512]{2,1,0:T(1,128)S(1)} %slice_add_fusion.1), channel_id=2, replica_groups=mesh['rep'=2,'tm'=8,'mp'=2] {'tm'}, dimensions={0}, use_global_device_ids=true | all-gather | bytes 73728 | tf_op jit(solution)/shard_map/all_gather | solution.py:9
  105.0 2.0 fusion.35
  107.5 15.5 %all_to_all.4 = bf16[4,1,128,512]{3,0,1,2:T(4,128)(2,1)S(1)} all-to-all(bf16[4,1,128,512]{3,0,1,2:T(4,128)(2,1)S(1)} %copy.20), channel_id=1, replica_groups=mesh['rep'=2,'tm'=8,'mp'=2] {'tm'}, dimensions={2} | all-to-all | bytes 1048576 | tf_op jit(solution)/shard_map/all_to_all | solution.py:78
  123.9 1.7 convolution_convert_fusion.7
  125.7 18.4 %all-reduce.33.cloned.1.call-done = bf16[512,1024]{1,0:T(8,128)(2,1)} async-done(((bf16[512,1024]{1,0:T(8,128)(2,1)}), bf16[512,1024]{1,0:T(8,128)(2,1)}) %all-reduce.33.cloned.1.call-update) | async-done | bytes 1048592 | tf_op jit(solution)/shard_map/psum | solution.py:91
  144.1 1.5 fusion.1
  145.7 3.0 fusion.23
  148.6 3.7 %convolution_convert_fusion.6 = bf16[512,1024]{1,0:T(8,128)(2,1)} fusion(bf16[512,1024]{1,0:T(8,128)(2,1)} %param.21, f32[512,512]{1,0:T(8,128)} %fusion.23, bf16[18,512]{1,0:T(8,128)(2,1)S(1)} %copy-done.16, s32[512]{0:T(512)S(1)} %bitcast.91), kind=kOutput, calls=%fused_computation.30 | convolution fusion | flops 548414464 | bytes 3166208 | tf_op jit(solution)/shard_map/dot_general | solution.py:99
  152.4 9.7 %reduce-scatter.5.cloned.1.call-done = bf16[512,512]{1,0:T(8,128)(2,1)} async-done(((bf16[512,1024]{1,0:T(8,128)(2,1)}), bf16[512,512]{1,0:T(8,128)(2,1)}) %reduce-scatter.5.cloned.1.call-update) | async-done | bytes 524304 | tf_op jit(solution)/shard_map/reduce_scatter | solution.py:98
  162.1 11.7 %all-gather.6.cloned.1.call-done = bf16[512,1024]{1,0:T(8,128)(2,1)} async-done(((bf16[512,512]{1,0:T(8,128)(2,1)}), bf16[512,1024]{1,0:T(8,128)(2,1)}) %all-gather.6.cloned.1.call-update) | async-done | bytes 1048592 | tf_op jit(solution)/shard_map/all_gather | solution.py:106
  173.9 2.1 fusion.15
  175.9 1.7 convolution_convert_fusion.5
  177.9 20.5 %all-reduce.35.cloned.1.call-done = bf16[512,1024]{1,0:T(8,128)(2,1)} async-done(((bf16[512,1024]{1,0:T(8,128)(2,1)}), bf16[512,1024]{1,0:T(8,128)(2,1)}) %all-reduce.35.cloned.1.call-update) | async-done | bytes 1048592 | tf_op jit(solution)/shard_map/psum | solution.py:91
  198.4 1.5 fusion.4
  199.9 3.0 fusion.21
  202.9 3.6 %convolution_convert_fusion.4 = bf16[512,1024]{1,0:T(8,128)(2,1)} fusion(bf16[512,1024]{1,0:T(8,128)(2,1)} %param.21, f32[512,512]{1,0:T(8,128)} %fusion.21, bf16[18,512]{1,0:T(8,128)(2,1)S(1)} %copy-done.16, s32[512]{0:T(512)S(1)} %bitcast.90), kind=kOutput, calls=%fused_computation.28 | convolution fusion | flops 548414464 | bytes 3166208 | tf_op jit(solution)/shard_map/dot_general | solution.py:99
  206.5 9.7 %reduce-scatter.7.cloned.1.call-done = bf16[512,512]{1,0:T(8,128)(2,1)} async-done(((bf16[512,1024]{1,0:T(8,128)(2,1)}), bf16[512,512]{1,0:T(8,128)(2,1)}) %reduce-scatter.7.cloned.1.call-update) | async-done | bytes 524304 | tf_op jit(solution)/shard_map/reduce_scatter | solution.py:98
  216.3 11.6 %all-gather.8.cloned.1.call-done = bf16[512,1024]{1,0:T(8,128)(2,1)} async-done(((bf16[512,512]{1,0:T(8,128)(2,1)}), bf16[512,1024]{1,0:T(8,128)(2,1)}) %all-gather.8.cloned.1.call-update) | async-done | bytes 1048592 | tf_op jit(solution)/shard_map/all_gather | solution.py:106
  227.9 2.2 fusion.14
  230.1 1.7 convolution_convert_fusion.3
  231.9 20.7 %all-reduce.37.cloned.1.call-done = bf16[512,1024]{1,0:T(8,128)(2,1)} async-done(((bf16[512,1024]{1,0:T(8,128)(2,1)}), bf16[512,1024]{1,0:T(8,128)(2,1)}) %all-reduce.37.cloned.1.call-update) | async-done | bytes 1048592 | tf_op jit(solution)/shard_map/psum | solution.py:91
  252.6 1.5 fusion.7
  254.1 3.0 fusion.19
  257.1 3.7 %convolution_convert_fusion.2 = bf16[512,1024]{1,0:T(8,128)(2,1)} fusion(bf16[512,1024]{1,0:T(8,128)(2,1)} %param.21, f32[512,512]{1,0:T(8,128)} %fusion.19, bf16[18,512]{1,0:T(8,128)(2,1)S(1)} %copy-done.16, s32[512]{0:T(512)S(1)} %bitcast.89), kind=kOutput, calls=%fused_computation.26 | convolution fusion | flops 548414464 | bytes 3166208 | tf_op jit(solution)/shard_map/dot_general | solution.py:99
  260.8 9.7 %reduce-scatter.9.cloned.1.call-done = bf16[512,512]{1,0:T(8,128)(2,1)} async-done(((bf16[512,1024]{1,0:T(8,128)(2,1)}), bf16[512,512]{1,0:T(8,128)(2,1)}) %reduce-scatter.9.cloned.1.call-update) | async-done | bytes 524304 | tf_op jit(solution)/shard_map/reduce_scatter | solution.py:98
  270.6 11.7 %all-gather.10.cloned.1.call-done = bf16[512,1024]{1,0:T(8,128)(2,1)} async-done(((bf16[512,512]{1,0:T(8,128)(2,1)}), bf16[512,1024]{1,0:T(8,128)(2,1)}) %all-gather.10.cloned.1.call-update) | async-done | bytes 1048592 | tf_op jit(solution)/shard_map/all_gather | solution.py:106
  282.3 3.5 %convolution_convert_fusion.1 = bf16[512,1024]{1,0:T(8,128)(2,1)} fusion(bf16[512,1024]{1,0:T(8,128)(2,1)S(1)} %copy-done, bf16[512,1024]{1,0:T(8,128)(2,1)} %all-gather.10.cloned.1.call-done, bf16[1024,512]{1,0:T(8,128)(2,1)S(1)} %copy-done.8, f32[512,512]{1,0:T(8,128)S(1)} %fusion.14, f32[512]{0:T(512)S(1)} %get-tuple-element.128, ...), kind=kOutput, calls=%fused_computation.25 | convolution fusion | flops 1075314688 | bytes 5246976 | tf_op jit(solution)/shard_map/dot_general | solution.py:92
  285.8 20.7 %all-reduce.39.cloned.1.call-done = bf16[512,1024]{1,0:T(8,128)(2,1)} async-done(((bf16[512,1024]{1,0:T(8,128)(2,1)}), bf16[512,1024]{1,0:T(8,128)(2,1)}) %all-reduce.39.cloned.1.call-update) | async-done | bytes 1048592 | tf_op jit(solution)/shard_map/psum | solution.py:91
  306.5 1.5 fusion.10
  308.0 3.0 fusion.17
  311.0 3.7 %convolution_convert_fusion = bf16[512,1024]{1,0:T(8,128)(2,1)} fusion(bf16[512,1024]{1,0:T(8,128)(2,1)} %param.21, f32[512,512]{1,0:T(8,128)} %fusion.17, bf16[18,512]{1,0:T(8,128)(2,1)S(1)} %copy-done.16, s32[512]{0:T(512)S(1)} %bitcast.88), kind=kOutput, calls=%fused_computation.24 | convolution fusion | flops 548414464 | bytes 3166208 | tf_op jit(solution)/shard_map/dot_general | solution.py:99
  314.7 1.0 copy.23
  315.7 2.1 copy.24
  317.8 2.0 copy.25
  319.9 4.5 %reduce-scatter.11.cloned.1.call-done = bf16[512,512]{1,0:T(8,128)(2,1)} async-done(((bf16[512,1024]{1,0:T(8,128)(2,1)}), bf16[512,512]{1,0:T(8,128)(2,1)}) %reduce-scatter.11.cloned.1.call-update) | async-done | bytes 524304 | tf_op jit(solution)/shard_map/reduce_scatter | solution.py:98
  324.4 2.2 copy.26
  326.6 5.9 %pad_maximum_fusion = bf16[4,8,16,4,512]{4,3,2,1,0:T(4,128)(2,1)} fusion(bf16[4,8,16,1,512]{4,3,2,1,0:T(2,128)(2,1)S(1)} %copy.26, bf16[4,8,16,1,512]{4,3,2,1,0:T(2,128)(2,1)S(1)} %copy-done.1, bf16[4,8,16,1,512]{4,3,2,1,0:T(2,128)(2,1)S(1)} %copy.24, bf16[4,8,16,1,512]{4,3,2,1,0:T(2,128)(2,1)S(1)} %copy.23), kind=kLoop, calls=%fused_computation.23 | loop fusion | flops 8388608 | bytes 4194304 | tf_op jit(solution)/shard_map/stack | solution.py:110
  (179 shorter events, 15.7 us)
Async XLA Ops:
  6.5 117.3 %copy-start = (bf16[512,1024]{1,0:T(8,128)(2,1)S(1)}, bf16[512,1024]{1,0:T(8,128)(2,1)}, u32[]{:S(2)}) copy-start(bf16[512,1024]{1,0:T(8,128)(2,1)} %param.17) | copy-start | bytes 3145732
  6.5 137.6 %all-reduce.33.cloned.1.call-start = ((), (), s32[]{:S(2)}) async-start(), calls=%async_computation.5 | async-start | bytes 2097152 | tf_op jit(solution)/shard_map/psum | solution.py:91
  22.4 1.0 copy-start.9
  24.1 1.8 copy-start.4
  24.1 1.8 copy-start.5
  27.1 1.0 copy-start.6
  123.1 0.8 copy-start.10
  123.1 2.5 copy-start.11
  123.8 21.8 %copy-start.12 = (bf16[1024,512]{1,0:T(8,128)(2,1)S(1)}, bf16[1024,512]{1,0:T(8,128)(2,1)}, u32[]{:S(2)}) copy-start(bf16[1024,512]{1,0:T(8,128)(2,1)} %param.19) | copy-start | bytes 3145732
  123.9 21.8 %copy-start.17 = (f32[1024]{0:T(1024)S(1)}, f32[1024]{0:T(1024)}, u32[]{:S(2)}) copy-start(f32[1024]{0:T(1024)} %param.18) | copy-start | bytes 12292
  125.6 36.5 %reduce-scatter.5.cloned.1.call-start = ((), (), s32[]{:S(2)}) async-start(), calls=%async_computation.6 | async-start | bytes 1572864 | tf_op jit(solution)/shard_map/reduce_scatter | solution.py:98
  145.6 3.0 copy-start.16
  148.6 25.2 %copy-start.7 = (bf16[1024,512]{1,0:T(8,128)(2,1)S(1)}, bf16[1024,512]{1,0:T(8,128)(2,1)}, u32[]{:S(2)}) copy-start(bf16[1024,512]{1,0:T(8,128)(2,1)} %param.15) | copy-start | bytes 3145732
  152.3 21.5 %all-gather.6.cloned.1.call-start = ((), (), s32[]{:S(2)}) async-start(), calls=%async_computation.7 | async-start | bytes 1572864 | tf_op jit(solution)/shard_map/all_gather | solution.py:106
  162.1 36.3 %all-reduce.35.cloned.1.call-start = ((), (), s32[]{:S(2)}) async-start(), calls=%async_computation.8 | async-start | bytes 2097152 | tf_op jit(solution)/shard_map/psum | solution.py:91
  175.9 24.0 %copy-start.13 = (bf16[1024,512]{1,0:T(8,128)(2,1)S(1)}, bf16[1024,512]{1,0:T(8,128)(2,1)}, u32[]{:S(2)}) copy-start(bf16[1024,512]{1,0:T(8,128)(2,1)} %param.19) | copy-start | bytes 3145732
  177.7 38.6 %reduce-scatter.7.cloned.1.call-start = ((), (), s32[]{:S(2)}) async-start(), calls=%async_computation.9 | async-start | bytes 1572864 | tf_op jit(solution)/shard_map/reduce_scatter | solution.py:98
  206.5 21.4 %all-gather.8.cloned.1.call-start = ((), (), s32[]{:S(2)}) async-start(), calls=%async_computation.10 | async-start | bytes 1572864 | tf_op jit(solution)/shard_map/all_gather | solution.py:106
  216.3 36.3 %all-reduce.37.cloned.1.call-start = ((), (), s32[]{:S(2)}) async-start(), calls=%async_computation.11 | async-start | bytes 2097152 | tf_op jit(solution)/shard_map/psum | solution.py:91
  230.1 24.0 %copy-start.14 = (bf16[1024,512]{1,0:T(8,128)(2,1)S(1)}, bf16[1024,512]{1,0:T(8,128)(2,1)}, u32[]{:S(2)}) copy-start(bf16[1024,512]{1,0:T(8,128)(2,1)} %param.19) | copy-start | bytes 3145732
  231.8 38.7 %reduce-scatter.9.cloned.1.call-start = ((), (), s32[]{:S(2)}) async-start(), calls=%async_computation.12 | async-start | bytes 1572864 | tf_op jit(solution)/shard_map/reduce_scatter | solution.py:98
  257.1 25.2 %copy-start.8 = (bf16[1024,512]{1,0:T(8,128)(2,1)S(1)}, bf16[1024,512]{1,0:T(8,128)(2,1)}, u32[]{:S(2)}) copy-start(bf16[1024,512]{1,0:T(8,128)(2,1)} %param.15) | copy-start | bytes 3145732
  260.8 21.5 %all-gather.10.cloned.1.call-start = ((), (), s32[]{:S(2)}) async-start(), calls=%async_computation.13 | async-start | bytes 1572864 | tf_op jit(solution)/shard_map/all_gather | solution.py:106
  270.5 36.0 %all-reduce.39.cloned.1.call-start = ((), (), s32[]{:S(2)}) async-start(), calls=%async_computation.14 | async-start | bytes 2097152 | tf_op jit(solution)/shard_map/psum | solution.py:91
  285.7 22.3 %copy-start.15 = (bf16[1024,512]{1,0:T(8,128)(2,1)S(1)}, bf16[1024,512]{1,0:T(8,128)(2,1)}, u32[]{:S(2)}) copy-start(bf16[1024,512]{1,0:T(8,128)(2,1)} %param.19) | copy-start | bytes 3145732
  285.8 38.6 %reduce-scatter.11.cloned.1.call-start = ((), (), s32[]{:S(2)}) async-start(), calls=%async_computation.15 | async-start | bytes 1572864 | tf_op jit(solution)/shard_map/reduce_scatter | solution.py:98
  311.0 3.7 %copy-start.2 = (bf16[512,512]{1,0:T(8,128)(2,1)S(1)}, bf16[512,512]{1,0:T(8,128)(2,1)}, u32[]{:S(2)}) copy-start(bf16[512,512]{1,0:T(8,128)(2,1)} %reduce-scatter.5.cloned.1.call-done) | copy-start | bytes 1572868
  314.7 3.2 copy-start.3
  324.4 2.2 copy-start.1
Sparse Core Ops, SparseCore 0:
  125.7 18.4 all-reduce.32
  152.5 9.5 reduce-scatter.4
  163.6 10.1 all-gather.5
  177.8 20.5 all-reduce.34
  206.6 9.5 reduce-scatter.6
  217.6 10.1 all-gather.7
  232.0 20.5 all-reduce.36
  260.9 9.5 reduce-scatter.8
  272.1 10.1 all-gather.9
  285.9 20.5 all-reduce.38
  314.8 9.5 reduce-scatter.10
where the time goes:
time: 340 us; the launch traced here: 339 us
  waiting for transfers between devices  149 us (44%)
  blocking collectives  78.5 us (23%)
  matrix products  41.5 us (12%)
  local copies, waits for them, and re-layouts  31.1 us (9%)
  other arithmetic  24 us (7%)
  between operations  14.1 us (4%)
    psum x4, waiting for transfers between devices, per_device(): lax.psum(jnp.dot(current.astype(jnp.bfloat16), readout_w, preferred_eleme...  80.3 us
    all_gather x2, blocking collectives, carried_in(): pieces = jax.tree.map(lambda part: lax.all_gather(part, axis), value)  63 us
    all_gather x3, waiting for transfers between devices, per_device(): full_guess = lax.all_gather(guessed, 'mp', axis=1, tiled=True)  35 us
    reduce_scatter x4, waiting for transfers between devices, per_device(): lax.psum_scatter(jnp.dot(hidden, w_out, preferred_element_type=jnp.float3...  33.6 us
    all_to_all x1, blocking collectives, per_device(): lax.all_to_all(shortened(corrected.reshape(batch, 1, steps, width_part)),...  15.5 us
    dot_general x4, matrix products, per_device(): jnp.dot(hidden, w_out, preferred_element_type=jnp.float32)  14.6 us
    pad x24, local copies, waits for them, and re-layouts, per_device(): lax.associative_scan(combine, (gates, driven), axis=1)  12.2 us
    dot_general x4, matrix products, hidden_units(): jnp.dot(normed, w_hidden, preferred_element_type=jnp.float32)  11.8 us
  transfers between devices with their start and end apart: 11, of which 11 were waited for; matrix products, arithmetic and copies ran while one was open for 2% of the time, Pallas kernels for 0%

commit v1 on v0

v1 whole, which is shorter than its diff:
```python
import jax
import jax.numpy as jnp
from jax import lax
from jax.experimental import pallas as pl
from jax.experimental.pallas import tpu as pltpu
from jax.sharding import PartitionSpec as P


def _scan_kernel(x_ref, g_ref, o_ref):
    nb, steps, width = x_ref.shape

    def body(t, states):
        row = pl.ds(t, 1)
        new = []
        for b in range(nb):
            h = g_ref[b, row, :] * states[b] + x_ref[b, row, :]
            o_ref[b, row, :] = h
            new.append(h)
        return tuple(new)

    start = tuple(jnp.zeros((1, width), jnp.float32) for _ in range(nb))
    lax.fori_loop(0, steps, body, start, unroll=8)


def local_scan(driven, gates):
    size = driven.size
    return pl.pallas_call(
        _scan_kernel,
        out_shape=jax.ShapeDtypeStruct(driven.shape, jnp.float32),
        in_specs=[pl.BlockSpec(memory_space=pltpu.VMEM)] * 2,
        out_specs=pl.BlockSpec(memory_space=pltpu.VMEM),
        cost_estimate=pl.CostEstimate(flops=2 * size, bytes_accessed=12 * size, transcendentals=0),
    )(driven, gates)


def per_device(
    inputs,
    resets,
    actions,
    in_proj,
    decay_rates,
    readout_w,
    norm_gain,
    w_hidden,
    action_embed,
    w_out,
):
    m = lax.axis_index("mp")
    d = lax.axis_index("tm")
    ntm = lax.axis_size("tm")
    swap = [(0, 1), (1, 0)]

    def partner(x):
        return lax.ppermute(x, "mp", swap)

    half = in_proj.shape[1]
    ip_o = partner(in_proj)
    r_o = partner(readout_w)
    wh_o = partner(w_hidden)
    wo_o = partner(w_out)
    emb_o = partner(action_embed)
    ip = jnp.concatenate([in_proj, ip_o], axis=1)
    wh = jnp.concatenate([w_hidden, wh_o], axis=1)
    wo = jnp.concatenate([w_out, wo_o], axis=0)
    emb = jnp.concatenate([action_embed, emb_o], axis=1)

    rates = jnp.concatenate(
        [
            lax.dynamic_slice_in_dim(decay_rates, m * half, half),
            lax.dynamic_slice_in_dim(decay_rates, (1 - m) * half, half),
        ]
    )
    decays = jnp.exp(-rates)
    scaling = jnp.sqrt(1.0 - decays * decays)
    width = decays.shape[0]

    seqs, steps, feat = inputs.shape
    bh = seqs // 2
    x = lax.dynamic_slice_in_dim(inputs, m * bh, bh, 0)
    driven = (
        jnp.dot(x.reshape(bh * steps, feat), ip, preferred_element_type=jnp.float32).reshape(
            bh, steps, width
        )
        * scaling
    )
    my_resets = lax.dynamic_slice_in_dim(resets, m * bh, bh, 0)
    keep = (1 - my_resets).astype(jnp.float32)
    gates = keep[:, :, None] * decays
    local = local_scan(driven, gates)

    positions = lax.broadcasted_iota(jnp.int32, my_resets.shape, 1)
    first = jnp.min(jnp.where(my_resets != 0, positions, steps), axis=1).astype(jnp.float32)
    payload = jnp.concatenate(
        [local[:, -1, :], jnp.broadcast_to(first[:, None], (bh, 128))], axis=1
    )
    gathered = lax.all_gather(payload, "tm")
    ends = gathered[:, :, :width]
    firsts = gathered[:, :, width]

    sub = steps // ntm
    send = local.astype(jnp.bfloat16).reshape(bh, ntm, sub, width)
    recv = lax.all_to_all(send, "tm", split_axis=1, concat_axis=1, tiled=True)

    nblocks = gathered.shape[0]
    whole_block = decays ** steps
    gain = jnp.where(firsts >= steps, 1.0, 0.0)[:, :, None] * whole_block
    total = ends
    offset = 1
    while offset < nblocks:
        gain_prev = jnp.concatenate([jnp.ones_like(gain[:offset]), gain[:-offset]], axis=0)
        total_prev = jnp.concatenate([jnp.zeros_like(total[:offset]), total[:-offset]], axis=0)
        total = gain * total_prev + total
        gain = gain * gain_prev
        offset *= 2
    carry = jnp.concatenate([jnp.zeros_like(total[:1]), total[:-1]], axis=0)

    t_glob = d * sub + lax.broadcasted_iota(jnp.int32, (sub,), 0)
    powers = decays[None, :] ** (t_glob[:, None] + 1).astype(jnp.float32)
    alive = t_glob[None, None, :].astype(jnp.float32) < jnp.swapaxes(firsts, 0, 1)[:, :, None]
    cum = jnp.where(alive[..., None], powers[None, None], 0.0)
    posterior = recv.astype(jnp.float32) + cum * jnp.swapaxes(carry, 0, 1)[:, :, None, :]

    _, blocks, _, horizon = actions.shape
    rows = bh * blocks * sub
    current = posterior.reshape(rows, width)
    my_actions = lax.dynamic_slice_in_dim(actions, m * bh, bh, 0).reshape(rows, horizon)
    table_ids = jnp.arange(emb.shape[0], dtype=jnp.int32)
    kept, given = [], []
    for step in range(horizon):
        rounded = current.astype(jnp.bfloat16)
        features = jnp.dot(
            rounded[:, :half], readout_w, preferred_element_type=jnp.float32
        ).astype(jnp.bfloat16).astype(jnp.float32) + jnp.dot(
            rounded[:, half:], r_o, preferred_element_type=jnp.float32
        ).astype(jnp.bfloat16).astype(jnp.float32)
        mean_sq = jnp.mean(features * features, axis=-1, keepdims=True)
        normed = (features * lax.rsqrt(mean_sq + 1e-06) * norm_gain).astype(jnp.bfloat16)
        one_hot = (my_actions[:, step][:, None] == table_ids[None, :]).astype(jnp.bfloat16)
        pre_act = jnp.dot(normed, wh, preferred_element_type=jnp.float32) + jnp.dot(
            one_hot, emb, preferred_element_type=jnp.float32
        )
        hidden = jax.nn.silu(pre_act).astype(jnp.bfloat16)
        guessed = jnp.dot(hidden, wo, preferred_element_type=jnp.float32).astype(jnp.bfloat16)
        kept.append(lax.dynamic_slice_in_dim(guessed, m * half, half, 1))
        given.append(partner(lax.dynamic_slice_in_dim(guessed, (1 - m) * half, half, 1)))
        if step < horizon - 1:
            current = decays * current + scaling * jnp.dot(
                guessed, ip, preferred_element_type=jnp.float32
            )
    mine = jnp.stack(kept, axis=1).reshape(bh, blocks, sub, horizon, half)
    theirs = jnp.stack(given, axis=1).reshape(bh, blocks, sub, horizon, half)
    first_half = jnp.where(m == 0, mine, theirs)
    second_half = jnp.where(m == 0, theirs, mine)
    return jnp.concatenate([first_half, second_half], axis=0)


def solution(mesh):
    in_specs = (
        P("rep", "tm", None),
        P("rep", "tm"),
        P("rep", None, "tm", None),
        P(None, "mp"),
        P(),
        P("mp", None),
        P(),
        P(None, "mp"),
        P(None, "mp"),
        P("mp", None),
    )
    out_specs = P("rep", None, "tm", None, "mp")
    return jax.shard_map(
        per_device, mesh=mesh, in_specs=in_specs, out_specs=out_specs, check_vma=False
    )
```

time: 340 us -> 127 us (0.37)
  waiting for transfers between devices: 149 us -> 6.8 us
  blocking collectives: 78.5 us -> 31.9 us
  other arithmetic: 24 us -> 5.87 us
  between operations: 14.1 us -> 0.38 us
  local copies, waits for them, and re-layouts: 31.1 us -> 22.2 us
  starting transfers between devices: 0.59 us -> 8.05 us
  matrix products: 41.5 us -> 47.5 us
    psum x4 -> x0, waiting for transfers between devices: 80.3 us -> none  [per_device(): lax.psum(jnp.dot(current.astype(jnp.bfloat16), readout_w, preferred_eleme...]
    all_gather x3 -> x0, waiting for transfers between devices: 35 us -> none  [per_device(): full_guess = lax.all_gather(guessed, 'mp', axis=1, tiled=True)]
    reduce_scatter x4 -> x0, waiting for transfers between devices: 33.6 us -> none  [per_device(): lax.psum_scatter(jnp.dot(hidden, w_out, preferred_element_type=jnp.float3...]
    all_gather x2 -> x1, blocking collectives: 63 us -> 31.9 us  [per_device(): gathered = lax.all_gather(payload, 'tm')]
    all_to_all x1 -> x0, blocking collectives: 15.5 us -> none  [per_device(): lax.all_to_all(shortened(corrected.reshape(batch, 1, steps, width_part)),...]
    pad x24 -> x0, local copies, waits for them, and re-layouts: 12.2 us -> none  [per_device(): lax.associative_scan(combine, (gates, driven), axis=1)]
    concatenate x0 -> x5, local copies, waits for them, and re-layouts: none -> 9.28 us  [the longest x1 3.27 us: per_device(): return jnp.concatenate([first_half, second_half], axis=0)]
    slice x45 -> x8, local copies, waits for them, and re-layouts: 8.92 us -> 0.97 us  [the longest x1 0.85 us: per_device(): local[:, -1, :]]
  transfers between devices with their start and end apart: 11 -> 10, of which waited for: 11 -> 5; matrix products, arithmetic and copies ran while one was open for 2% -> 20% of each run, Pallas kernels for 0% -> 3%
where the time goes in v1:
time: 127 us; the launch traced here: 126 us
  matrix products  47.5 us (37%)
  blocking collectives  31.9 us (25%)
  local copies, waits for them, and re-layouts  22.2 us (17%)
  starting transfers between devices  8.05 us (6%)
  waiting for transfers between devices  6.8 us (5%)
  other arithmetic  5.87 us (5%)
  Pallas kernels  3.16 us (2%)
    all_gather x1, blocking collectives, per_device(): gathered = lax.all_gather(payload, 'tm')  31.9 us
    dot_general x4, matrix products, per_device(): jnp.dot(hidden, wo, preferred_element_type=jnp.float32).astype(jnp.bfloat16)  19.3 us
    dot_general x4, matrix products, per_device(): jnp.dot(rounded[:, half:], r_o, preferred_element_type=jnp.float32)  10.9 us
    dot_general x3, matrix products, per_device(): jnp.dot(guessed, ip, preferred_element_type=jnp.float32)  8.52 us
    dynamic_slice x4, local copies, waits for them, and re-layouts, per_device(): kept.append(lax.dynamic_slice_in_dim(guessed, m * half, half, 1))  6.38 us
    all_to_all x1, starting transfers between devices, per_device(): recv = lax.all_to_all(send, 'tm', split_axis=1, concat_axis=1, tiled=True)  5.52 us
    dot_general x4, matrix products, per_device(): jnp.dot(one_hot, emb, preferred_element_type=jnp.float32)  5.38 us
    all_to_all x1, waiting for transfers between devices, per_device(): recv = lax.all_to_all(send, 'tm', split_axis=1, concat_axis=1, tiled=True)  4.94 us
  transfers between devices with their start and end apart: 10, of which 5 were waited for; matrix products, arithmetic and copies ran while one was open for 20% of the time, Pallas kernels for 3%

profile of v1, /device:TPU:0, one launch (start us, length us, event | category | flops | bytes accessed | tf_op | source)
XLA Modules:
  0.0 125.9 jit_solution(2131900124612781710)
XLA Ops:
  0.0 0.5 collective-permute-start.4
  0.6 0.4 collective-permute-start.2
  1.1 0.4 collective-permute-start.1
  1.5 2.4 %constant_dynamic-update-slice_fusion.7 = bf16[1024,1024]{1,0:T(8,128)(2,1)} fusion(bf16[512,1024]{1,0:T(8,128)(2,1)} %param.19), kind=kLoop, calls=%fused_computation.107 | loop fusion | bytes 2097152
  3.9 1.1 constant_dynamic-update-slice_fusion.3
  5.6 1.1 broadcast_multiply_fusion.g_ref
  6.9 1.3 %fusion.50 = f32[256,1024]{1,0:T(8,128)} fusion(bf16[18,1024]{1,0:T(8,128)(2,1)S(1)} %constant_dynamic-update-slice_fusion.4, s32[256]{0:T(256)S(1)} %bitcast.75), kind=kOutput, calls=%fused_computation.86 | convolution fusion | flops 9441792 | bytes 1086464 | tf_op jit(solution)/shard_map/dot_general | solution.py:139
  8.2 1.3 %fusion.48 = f32[256,1024]{1,0:T(8,128)} fusion(bf16[18,1024]{1,0:T(8,128)(2,1)S(1)} %constant_dynamic-update-slice_fusion.4, s32[256]{0:T(256)S(1)} %bitcast.74), kind=kOutput, calls=%fused_computation.84 | convolution fusion | flops 9441792 | bytes 1086464 | tf_op jit(solution)/shard_map/dot_general | solution.py:139
  9.5 1.4 %fusion.47 = f32[256,1024]{1,0:T(8,128)} fusion(bf16[18,1024]{1,0:T(8,128)(2,1)S(1)} %constant_dynamic-update-slice_fusion.4, s32[256]{0:T(256)S(1)} %bitcast.73), kind=kOutput, calls=%fused_computation.83 | convolution fusion | flops 9441792 | bytes 1086464 | tf_op jit(solution)/shard_map/dot_general | solution.py:139
  10.9 1.3 %fusion.49 = f32[256,1024]{1,0:T(8,128)} fusion(bf16[18,1024]{1,0:T(8,128)(2,1)S(1)} %constant_dynamic-update-slice_fusion.4, s32[256]{0:T(256)S(1)} %bitcast.72), kind=kOutput, calls=%fused_computation.85 | convolution fusion | flops 9441792 | bytes 1086464 | tf_op jit(solution)/shard_map/dot_general | solution.py:139
  12.3 1.4 %constant_dynamic-update-slice_fusion = bf16[1024,1024]{1,0:T(8,128)(2,1)S(1)} fusion(bf16[1024,1024]{1,0:T(8,128)(2,1)S(1)} %constant_dynamic-update-slice_fusion.1, bf16[1024,512]{1,0:T(8,128)(2,1)} %collective-permute-done), kind=kLoop, calls=%fused_computation.100 | loop fusion | bytes 2097152 | tf_op jit(solution)/shard_map/concatenate | solution.py:62
  13.7 1.7 %fusion.2.x_ref = f32[2,128,1024]{2,1,0:T(8,128)} fusion(bf16[1024,1024]{1,0:T(8,128)(2,1)S(1)} %constant_dynamic-update-slice_fusion, f32[1024]{0:T(1024)S(1)} %get-tuple-element.26, bf16[4,128,1024]{2,1,0:T(8,128)(2,1)S(1)} %copy-done, s32[]{:T(128)S(6)} %select_n.45), kind=kOutput, calls=%fused_computation.3 | convolution fusion | flops 537133056 | bytes 3674116 | tf_op jit(solution)/shard_map/dot_general | solution.py:81
  15.4 3.2 %shard_map.100 = f32[2,128,1024]{2,1,0:T(8,128)} custom-call(f32[2,128,1024]{2,1,0:T(8,128)} %fusion.2.x_ref, f32[2,128,1024]{2,1,0:T(8,128)} %broadcast_multiply_fusion.g_ref), custom_call_target="tpu_custom_call" | custom-call | flops 524288 | bytes 3145728 | tf_op jit(solution)/shard_map/pallas_call | solution.py:27
  18.6 0.8 slice.85
  19.5 31.9 %all-gather.1 = f32[8,2,1152]{2,1,0:T(2,128)S(1)} all-gather(f32[1,2,1152]{2,1,0:T(2,128)S(1)} %maximum_bitcast_fusion), channel_id=2, replica_groups=mesh['rep'=2,'tm'=8,'mp'=2] {'tm'}, dimensions={0}, use_global_device_ids=true | all-gather | bytes 82944 | tf_op jit(solution)/shard_map/all_gather | solution.py:96
  51.4 1.3 %convert_element_type.133 = bf16[2,128,1024]{2,1,0:T(8,128)(2,1)S(1)} convert(f32[2,128,1024]{2,1,0:T(8,128)} %shard_map.100) | non-fusion elementwise | flops 262144 | bytes 1572864 | tf_op jit(solution)/shard_map/convert_element_type | solution.py:101
  52.8 0.9 copy.25
  53.6 5.5 %all-to-all-start = ((bf16[2,8,16,1024]{3,2,0,1:T(8,128)(2,1)}), bf16[2,8,16,1024]{3,2,0,1:T(8,128)(2,1)}, u32[]{:S(2)}, u32[]{:S(2)}) async-start(bf16[2,8,16,1024]{3,2,0,1:T(8,128)(2,1)} %copy.25), calls=%async_computation | async-start | bytes 1048576 | tf_op jit(solution)/shard_map/all_to_all | solution.py:102
  59.9 2.3 %constant_dynamic-update-slice_fusion.6 = bf16[1024,1024]{1,0:T(8,128)(2,1)} fusion(bf16[1024,1024]{1,0:T(8,128)(2,1)} %constant_dynamic-update-slice_fusion.7, bf16[512,1024]{1,0:T(8,128)(2,1)} %collective-permute-done.4), kind=kLoop, calls=%fused_computation.106 | loop fusion | bytes 2097152 | tf_op jit(solution)/shard_map/concatenate | solution.py:64
  62.2 2.4 %constant_dynamic-update-slice_fusion.2 = bf16[1024,1024]{1,0:T(8,128)(2,1)} fusion(bf16[1024,1024]{1,0:T(8,128)(2,1)} %constant_dynamic-update-slice_fusion.3, bf16[1024,512]{1,0:T(8,128)(2,1)} %collective-permute-done.2), kind=kLoop, calls=%fused_computation.102 | loop fusion | bytes 2097152 | tf_op jit(solution)/shard_map/concatenate | solution.py:63
  64.6 4.9 %all-to-all-done = bf16[2,8,16,1024]{3,2,0,1:T(8,128)(2,1)} async-done(((bf16[2,8,16,1024]{3,2,0,1:T(8,128)(2,1)}), bf16[2,8,16,1024]{3,2,0,1:T(8,128)(2,1)}, u32[]{:S(2)}, u32[]{:S(2)}) %all-to-all-start) | async-done | bytes 524320 | tf_op jit(solution)/shard_map/all_to_all | solution.py:102
  69.5 1.2 multiply_add_fusion.1
  71.0 1.1 bitcast_multiply_fusion
  72.3 0.4 fusion.17
  72.8 2.7 %multiply_reduce_fusion.3 = (f32[256]{0:T(256)S(1)}, f32[256,1024]{1,0:T(8,128)}) fusion(f32[256,1024]{1,0:T(8,128)S(1)} %fusion.17, bf16[512,1024]{1,0:T(8,128)(2,1)} %collective-permute-done.1, bf16[256,1024]{1,0:T(8,128)(2,1)S(1)} %bitcast_convert_fusion), kind=kOutput, calls=%fused_computation.53 | convolution fusion | flops 269745920 | bytes 3408896 | tf_op jit(solution)/shard_map/dot_general | solution.py:133
  75.5 5.1 %convolution_convert_fusion.11 = bf16[256,1024]{1,0:T(8,128)(2,1)} fusion(bf16[1024,1024]{1,0:T(8,128)(2,1)} %constant_dynamic-update-slice_fusion.6, f32[256,1024]{1,0:T(8,128)} %fusion.47, bf16[1024,1024]{1,0:T(8,128)(2,1)} %constant_dynamic-update-slice_fusion.2, f32[256,1024]{1,0:T(8,128)} %get-tuple-element.33, f32[1024]{0:T(1024)S(1)} %copy-done.14, ...), kind=kOutput, calls=%fused_computation.35 | convolution fusion | flops 1076363264 | bytes 6820864 | tf_op jit(solution)/shard_map/dot_general | solution.py:143
  80.6 1.8 %constant_dynamic-slice_fusion.7 = (bf16[256,512]{1,0:T(8,128)(2,1)S(1)}, bf16[256,512]{1,0:T(8,128)(2,1)}) fusion(bf16[256,1024]{1,0:T(8,128)(2,1)} %convolution_convert_fusion.11, s32[]{:T(128)S(6)} %select_n.46, s32[]{:T(128)S(6)} %select_n.47), kind=kLoop, calls=%fused_computation.123 | loop fusion | bytes 1048584 | tf_op jit(solution)/shard_map/dynamic_slice | solution.py:144
  82.4 3.1 %fusion.66 = (bf16[256,1024]{1,0:T(8,128)(2,1)S(1)}, f32[256,1024]{1,0:T(8,128)}) fusion(f32[256,1024]{1,0:T(8,128)} %bitcast_multiply_fusion, bf16[256,1024]{1,0:T(8,128)(2,1)} %convolution_convert_fusion.11, bf16[1024,1024]{1,0:T(8,128)(2,1)S(1)} %constant_dynamic-update-slice_fusion, f32[1024]{0:T(1024)S(1)} %get-tuple-element.26), kind=kOutput, calls=%fused_computation.144 | convolution fusion | flops 537657344 | bytes 5246976 | tf_op jit(solution)/shard_map/dot_general | solution.py:147
  85.5 0.4 fusion.14
  85.9 2.7 %multiply_reduce_fusion.2 = (f32[256]{0:T(256)S(1)}, f32[256,1024]{1,0:T(8,128)}) fusion(f32[256,1024]{1,0:T(8,128)S(1)} %fusion.14, bf16[512,1024]{1,0:T(8,128)(2,1)} %collective-permute-done.1, bf16[256,1024]{1,0:T(8,128)(2,1)S(1)} %get-tuple-element.34), kind=kOutput, calls=%fused_computation.50 | convolution fusion | flops 269745920 | bytes 3408896 | tf_op jit(solution)/shard_map/dot_general | solution.py:133
  88.7 5.1 %convolution_convert_fusion.10 = bf16[256,1024]{1,0:T(8,128)(2,1)} fusion(bf16[1024,1024]{1,0:T(8,128)(2,1)} %constant_dynamic-update-slice_fusion.6, f32[256,1024]{1,0:T(8,128)} %fusion.48, bf16[1024,1024]{1,0:T(8,128)(2,1)} %constant_dynamic-update-slice_fusion.2, f32[256,1024]{1,0:T(8,128)} %get-tuple-element.37, f32[256]{0:T(256)S(1)} %add_rsqrt_fusion.2, ...), kind=kOutput, calls=%fused_computation.34 | convolution fusion | flops 1076363264 | bytes 6820864 | tf_op jit(solution)/shard_map/dot_general | solution.py:143
  93.8 1.9 %constant_dynamic-slice_fusion.6 = (bf16[256,512]{1,0:T(8,128)(2,1)}, bf16[256,512]{1,0:T(8,128)(2,1)}) fusion(bf16[256,1024]{1,0:T(8,128)(2,1)} %convolution_convert_fusion.10, s32[]{:T(128)S(6)} %select_n.46, s32[]{:T(128)S(6)} %select_n.47), kind=kLoop, calls=%fused_computation.122 | loop fusion | bytes 1048584 | tf_op jit(solution)/shard_map/dynamic_slice | solution.py:144
  95.8 3.2 %fusion.67 = (bf16[256,1024]{1,0:T(8,128)(2,1)S(1)}, f32[256,1024]{1,0:T(8,128)}) fusion(bf16[256,1024]{1,0:T(8,128)(2,1)} %convolution_convert_fusion.10, bf16[1024,1024]{1,0:T(8,128)(2,1)S(1)} %constant_dynamic-update-slice_fusion, f32[1024]{0:T(1024)S(1)} %get-tuple-element.26, f32[256,1024]{1,0:T(8,128)} %get-tuple-element.35, ...), kind=kOutput, calls=%fused_computation.145 | convolution fusion | flops 537919488 | bytes 5251072 | tf_op jit(solution)/shard_map/dot_general | solution.py:147
  98.9 0.4 fusion.11
  99.4 2.6 %multiply_reduce_fusion.1 = (f32[256]{0:T(256)S(1)}, f32[256,1024]{1,0:T(8,128)}) fusion(f32[256,1024]{1,0:T(8,128)S(1)} %fusion.11, bf16[512,1024]{1,0:T(8,128)(2,1)} %collective-permute-done.1, bf16[256,1024]{1,0:T(8,128)(2,1)S(1)} %get-tuple-element.38), kind=kOutput, calls=%fused_computation.46 | convolution fusion | flops 269745920 | bytes 3408896 | tf_op jit(solution)/shard_map/dot_general | solution.py:133
  102.0 5.1 %convolution_convert_fusion.9 = bf16[256,1024]{1,0:T(8,128)(2,1)} fusion(bf16[1024,1024]{1,0:T(8,128)(2,1)} %constant_dynamic-update-slice_fusion.6, f32[256,1024]{1,0:T(8,128)} %fusion.49, bf16[1024,1024]{1,0:T(8,128)(2,1)} %constant_dynamic-update-slice_fusion.2, f32[256,1024]{1,0:T(8,128)} %get-tuple-element.41, f32[256]{0:T(256)S(1)} %add_rsqrt_fusion.1, ...), kind=kOutput, calls=%fused_computation.33 | convolution fusion | flops 1076363264 | bytes 6820864 | tf_op jit(solution)/shard_map/dot_general | solution.py:143
  107.1 1.9 %constant_dynamic-slice_fusion.5 = (bf16[256,512]{1,0:T(8,128)(2,1)}, bf16[256,512]{1,0:T(8,128)(2,1)}) fusion(bf16[256,1024]{1,0:T(8,128)(2,1)} %convolution_convert_fusion.9, s32[]{:T(128)S(6)} %select_n.46, s32[]{:T(128)S(6)} %select_n.47), kind=kLoop, calls=%fused_computation.121 | loop fusion | bytes 1048584 | tf_op jit(solution)/shard_map/dynamic_slice | solution.py:144
  109.0 2.2 %add_convert_fusion = bf16[256,1024]{1,0:T(8,128)(2,1)S(1)} fusion(f32[256,1024]{1,0:T(8,128)} %get-tuple-element.39, bf16[256,1024]{1,0:T(8,128)(2,1)} %convolution_convert_fusion.9, bf16[1024,1024]{1,0:T(8,128)(2,1)S(1)} %constant_dynamic-update-slice_fusion, f32[1024]{0:T(1024)S(1)} %get-tuple-element.26, f32[1024]{0:T(1024)S(1)} %get-tuple-element.27), kind=kOutput, calls=%fused_computation.43 | convolution fusion | flops 537919488 | bytes 4202496 | tf_op jit(solution)/shard_map/dot_general | solution.py:147
  111.3 0.4 fusion.8
  111.7 2.8 %multiply_reduce_fusion = (f32[256]{0:T(256)S(1)}, f32[256,1024]{1,0:T(8,128)}) fusion(f32[256,1024]{1,0:T(8,128)S(1)} %fusion.8, bf16[512,1024]{1,0:T(8,128)(2,1)} %collective-permute-done.1, bf16[256,1024]{1,0:T(8,128)(2,1)S(1)} %add_convert_fusion), kind=kOutput, calls=%fused_computation.42 | convolution fusion | flops 269745920 | bytes 3408896 | tf_op jit(solution)/shard_map/dot_general | solution.py:133
  114.5 4.0 %convolution_convert_fusion.8 = bf16[256,1024]{1,0:T(8,128)(2,1)S(1)} fusion(bf16[1024,1024]{1,0:T(8,128)(2,1)} %constant_dynamic-update-slice_fusion.6, f32[256,1024]{1,0:T(8,128)S(1)} %copy-done.7, bf16[1024,1024]{1,0:T(8,128)(2,1)} %constant_dynamic-update-slice_fusion.2, f32[256,1024]{1,0:T(8,128)} %get-tuple-element.43, f32[256]{0:T(256)S(1)} %add_rsqrt_fusion, ...), kind=kOutput, calls=%fused_computation.32 | convolution fusion | flops 1076363264 | bytes 6820864 | tf_op jit(solution)/shard_map/dot_general | solution.py:143
  118.5 0.7 constant_dynamic-slice_fusion.4
  119.3 0.5 collective-permute-start.7
  119.8 0.5 collective-permute-start.5
  120.3 0.7 collective-permute-done.8
  121.0 0.4 collective-permute-done.7
  121.4 0.4 collective-permute-done.6
  122.6 3.3 %copy.32 = bf16[4,8,16,4,512]{4,3,2,1,0:T(4,128)(2,1)} copy(bf16[4,8,16,4,512]{4,2,1,0,3:T(8,128)(2,1)S(1)} %pad_maximum_fusion) | data formatting | bytes 4194304 | tf_op jit(solution)/shard_map/concatenate | solution.py:154
  (79 shorter events, 3.0 us)
Async XLA Ops:
  0.0 13.7 %copy-start = (bf16[4,128,1024]{2,1,0:T(8,128)(2,1)S(1)}, bf16[4,128,1024]{2,1,0:T(8,128)(2,1)}, u32[]{:S(2)}) copy-start(bf16[4,128,1024]{2,1,0:T(8,128)(2,1)} %param.10) | copy-start | bytes 3145732
  0.0 3.9 %copy-start.9 = (bf16[1024,512]{1,0:T(8,128)(2,1)S(1)}, bf16[1024,512]{1,0:T(8,128)(2,1)}, u32[]{:S(2)}) copy-start(bf16[1024,512]{1,0:T(8,128)(2,1)} %param.17) | copy-start | bytes 3145732
  0.0 59.9 %collective-permute-start.4 = (bf16[512,1024]{1,0:T(8,128)(2,1)}, bf16[512,1024]{1,0:T(8,128)(2,1)}, u32[]{:S(2)}, u32[]{:S(2)}) collective-permute-start(bf16[512,1024]{1,0:T(8,128)(2,1)} %param.19), channel_id=1, source_target_pairs={{0,1},{1,0},{2,3},{3,2},{4,5},{5,4},{6,7},{7,6},{8,9},{9,8},{10,11... | collective-permute-start | bytes 3145736 | tf_op jit(solution)/shard_map/ppermute | solution.py:54
  0.5 6.4 %collective-permute-start.3 = (bf16[18,512]{1,0:T(8,128)(2,1)}, bf16[18,512]{1,0:T(8,128)(2,1)S(1)}, u32[]{:S(2)}, u32[]{:S(2)}) collective-permute-start(bf16[18,512]{1,0:T(8,128)(2,1)} %param.18), channel_id=1, source_target_pairs={{0,1},{1,0},{2,3},{3,2},{4,5},{5,4},{6,7},{7,6},{8,9},{9,8},{10,11... | collective-permute-start | bytes 55304 | tf_op jit(solution)/shard_map/ppermute | solution.py:54
  0.6 61.6 %collective-permute-start.2 = (bf16[1024,512]{1,0:T(8,128)(2,1)}, bf16[1024,512]{1,0:T(8,128)(2,1)}, u32[]{:S(2)}, u32[]{:S(2)}) collective-permute-start(bf16[1024,512]{1,0:T(8,128)(2,1)} %param.17), channel_id=1, source_target_pairs={{0,1},{1,0},{2,3},{3,2},{4,5},{5,4},{6,7},{7,6},{8,9},{9,8},{10,11... | collective-permute-start | bytes 3145736 | tf_op jit(solution)/shard_map/ppermute | solution.py:54
  1.0 11.3 %collective-permute-start = (bf16[1024,512]{1,0:T(8,128)(2,1)}, bf16[1024,512]{1,0:T(8,128)(2,1)}, u32[]{:S(2)}, u32[]{:S(2)}) collective-permute-start(bf16[1024,512]{1,0:T(8,128)(2,1)} %param.13), channel_id=1, source_target_pairs={{0,1},{1,0},{2,3},{3,2},{4,5},{5,4},{6,7},{7,6},{8,9},{9,8},{10,11... | collective-permute-start | bytes 3145736 | tf_op jit(solution)/shard_map/ppermute | solution.py:54
  1.1 71.7 %collective-permute-start.1 = (bf16[512,1024]{1,0:T(8,128)(2,1)}, bf16[512,1024]{1,0:T(8,128)(2,1)}, u32[]{:S(2)}, u32[]{:S(2)}) collective-permute-start(bf16[512,1024]{1,0:T(8,128)(2,1)} %param.15), channel_id=1, source_target_pairs={{0,1},{1,0},{2,3},{3,2},{4,5},{5,4},{6,7},{7,6},{8,9},{9,8},{10,11... | collective-permute-start | bytes 3145736 | tf_op jit(solution)/shard_map/ppermute | solution.py:54
  1.5 3.5 %copy-start.8 = (bf16[1024,512]{1,0:T(8,128)(2,1)S(1)}, bf16[1024,512]{1,0:T(8,128)(2,1)}, u32[]{:S(2)}) copy-start(bf16[1024,512]{1,0:T(8,128)(2,1)} %param.13) | copy-start | bytes 3145732
  3.9 1.3 %copy-start.11 = (s32[4,8,16,4]{2,3,1,0:T(4,128)S(1)}, s32[4,8,16,4]{2,3,1,0:T(4,128)}, u32[]{:S(2)}) copy-start(s32[4,8,16,4]{2,3,1,0:T(4,128)} %param.12) | copy-start | bytes 24580
  3.9 1.5 %copy-start.13 = (s32[4,128]{1,0:T(4,128)S(1)}, s32[4,128]{1,0:T(4,128)}, u32[]{:S(2)}) copy-start(s32[4,128]{1,0:T(4,128)} %param.11) | copy-start | bytes 6148
  3.9 1.6 %copy-start.12 = (f32[1024]{0:T(1024)S(1)}, f32[1024]{0:T(1024)}, u32[]{:S(2)}) copy-start(f32[1024]{0:T(1024)} %param.14) | copy-start | bytes 12292
  5.0 1.8 %copy-start.10 = (bf16[18,512]{1,0:T(8,128)(2,1)S(1)}, bf16[18,512]{1,0:T(8,128)(2,1)}, u32[]{:S(2)}) copy-start(bf16[18,512]{1,0:T(8,128)(2,1)} %param.18) | copy-start | bytes 55300
  53.6 15.9 %all-to-all-start = ((bf16[2,8,16,1024]{3,2,0,1:T(8,128)(2,1)}), bf16[2,8,16,1024]{3,2,0,1:T(8,128)(2,1)}, u32[]{:S(2)}, u32[]{:S(2)}) async-start(bf16[2,8,16,1024]{3,2,0,1:T(8,128)(2,1)} %copy.25), calls=%async_computation | async-start | bytes 1048576 | tf_op jit(solution)/shard_map/all_to_all | solution.py:102
  70.9 1.4 %copy-start.1 = (bf16[512,1024]{1,0:T(8,128)(2,1)S(1)}, bf16[512,1024]{1,0:T(8,128)(2,1)}, u32[]{:S(2)}) copy-start(bf16[512,1024]{1,0:T(8,128)(2,1)} %param.15) | copy-start | bytes 3145732
  72.8 2.8 %copy-start.14 = (f32[1024]{0:T(1024)S(1)}, f32[1024]{0:T(1024)}, u32[]{:S(2)}) copy-start(f32[1024]{0:T(1024)} %param.16) | copy-start | bytes 12292
  82.3 3.2 %copy-start.2 = (bf16[512,1024]{1,0:T(8,128)(2,1)S(1)}, bf16[512,1024]{1,0:T(8,128)(2,1)}, u32[]{:S(2)}) copy-start(bf16[512,1024]{1,0:T(8,128)(2,1)} %param.15) | copy-start | bytes 3145732
  95.8 3.2 %copy-start.3 = (bf16[512,1024]{1,0:T(8,128)(2,1)S(1)}, bf16[512,1024]{1,0:T(8,128)(2,1)}, u32[]{:S(2)}) copy-start(bf16[512,1024]{1,0:T(8,128)(2,1)} %param.15) | copy-start | bytes 3145732
  109.0 2.2 %copy-start.4 = (bf16[512,1024]{1,0:T(8,128)(2,1)S(1)}, bf16[512,1024]{1,0:T(8,128)(2,1)}, u32[]{:S(2)}) copy-start(bf16[512,1024]{1,0:T(8,128)(2,1)} %param.15) | copy-start | bytes 3145732
  111.7 2.8 %copy-start.7 = (f32[256,1024]{1,0:T(8,128)S(1)}, f32[256,1024]{1,0:T(8,128)}, u32[]{:S(2)}) copy-start(f32[256,1024]{1,0:T(8,128)} %fusion.50) | copy-start | bytes 3145732
  114.5 7.7 %copy-start.5 = (bf16[256,512]{1,0:T(8,128)(2,1)S(1)}, bf16[256,512]{1,0:T(8,128)(2,1)}, u32[]{:S(2)}) copy-start(bf16[256,512]{1,0:T(8,128)(2,1)} %get-tuple-element.9) | copy-start | bytes 786436
  114.5 7.6 %copy-start.6 = (bf16[256,512]{1,0:T(8,128)(2,1)S(1)}, bf16[256,512]{1,0:T(8,128)(2,1)}, u32[]{:S(2)}) copy-start(bf16[256,512]{1,0:T(8,128)(2,1)} %get-tuple-element.11) | copy-start | bytes 786436
  119.3 1.7 %collective-permute-start.8 = (bf16[256,512]{1,0:T(8,128)(2,1)}, bf16[256,512]{1,0:T(8,128)(2,1)S(1)}, u32[]{:S(2)}, u32[]{:S(2)}) collective-permute-start(bf16[256,512]{1,0:T(8,128)(2,1)} %get-tuple-element.14), channel_id=1, source_target_pairs={{0,1},{1,0},{2,3},{3,2},{4,5},{5,4},{6,7},{7,6},{8,9},{9,8},{10,11... | collective-permute-start | bytes 786440 | tf_op jit(solution)/shard_map/ppermute | solution.py:54
  119.3 2.1 %collective-permute-start.7 = (bf16[256,512]{1,0:T(8,128)(2,1)}, bf16[256,512]{1,0:T(8,128)(2,1)S(1)}, u32[]{:S(2)}, u32[]{:S(2)}) collective-permute-start(bf16[256,512]{1,0:T(8,128)(2,1)} %get-tuple-element.12), channel_id=1, source_target_pairs={{0,1},{1,0},{2,3},{3,2},{4,5},{5,4},{6,7},{7,6},{8,9},{9,8},{10,11... | collective-permute-start | bytes 786440 | tf_op jit(solution)/shard_map/ppermute | solution.py:54
  119.8 2.0 %collective-permute-start.6 = (bf16[256,512]{1,0:T(8,128)(2,1)}, bf16[256,512]{1,0:T(8,128)(2,1)S(1)}, u32[]{:S(2)}, u32[]{:S(2)}) collective-permute-start(bf16[256,512]{1,0:T(8,128)(2,1)} %get-tuple-element.10), channel_id=1, source_target_pairs={{0,1},{1,0},{2,3},{3,2},{4,5},{5,4},{6,7},{7,6},{8,9},{9,8},{10,11... | collective-permute-start | bytes 786440 | tf_op jit(solution)/shard_map/ppermute | solution.py:54
  119.8 2.4 %collective-permute-start.5 = (bf16[256,512]{1,0:T(8,128)(2,1)}, bf16[256,512]{1,0:T(8,128)(2,1)S(1)}, u32[]{:S(2)}, u32[]{:S(2)}) collective-permute-start(bf16[256,512]{1,0:T(8,128)(2,1)} %get-tuple-element.8), channel_id=1, source_target_pairs={{0,1},{1,0},{2,3},{3,2},{4,5},{5,4},{6,7},{7,6},{8,9},{9,8},{10,11... | collective-permute-start | bytes 786440 | tf_op jit(solution)/shard_map/ppermute | solution.py:54

commit v2 on v1

--- a/solution.py
+++ b/solution.py
@@ -31,6 +31,19 @@
         out_specs=pl.BlockSpec(memory_space=pltpu.VMEM),
         cost_estimate=pl.CostEstimate(flops=2 * size, bytes_accessed=12 * size, transcendentals=0),
     )(driven, gates)
+
+
+def gather_blocks(value, axis, mine, count):
+    if count & (count - 1):
+        return lax.all_gather(value, axis)
+    held = value[None]
+    shift = 1
+    while shift < count:
+        pairs = [(i, (i + shift) % count) for i in range(count)]
+        held = jnp.concatenate([held, lax.ppermute(held, axis, pairs)], axis=0)
+        shift *= 2
+    order = (mine - jnp.arange(count, dtype=jnp.int32)) % count
+    return jnp.take(held, order, axis=0)
 
 
 def per_device(
@@ -93,7 +106,7 @@
     payload = jnp.concatenate(
         [local[:, -1, :], jnp.broadcast_to(first[:, None], (bh, 128))], axis=1
     )
-    gathered = lax.all_gather(payload, "tm")
+    gathered = gather_blocks(payload, "tm", d, ntm)
     ends = gathered[:, :, :width]
     firsts = gathered[:, :, width]
 

time: 127 us -> 106 us (0.83)
  blocking collectives: 31.9 us -> 0 us
  starting transfers between devices: 8.05 us -> 14.6 us
  waiting for transfers between devices: 6.8 us -> 11 us
    all_gather x1 -> x0, blocking collectives: 31.9 us -> none  [per_device(): gathered = lax.all_gather(payload, 'tm')]
    ppermute x0 -> x3, waiting for transfers between devices: none -> 9.15 us  [gather_blocks(): held = jnp.concatenate([held, lax.ppermute(held, axis, pairs)], axis=0)]
    ppermute x0 -> x3, starting transfers between devices: none -> 7.09 us  [gather_blocks(): held = jnp.concatenate([held, lax.ppermute(held, axis, pairs)], axis=0)]
    all_to_all x1, waiting for transfers between devices: 4.94 us -> 0.01 us  [per_device(): recv = lax.all_to_all(send, 'tm', split_axis=1, concat_axis=1, tiled=True)]
  transfers between devices with their start and end apart: 10 -> 13, of which waited for: 5 -> 6; matrix products, arithmetic and copies ran while one was open for 20% -> 25% of each run, Pallas kernels for 3% -> 3%
where the time goes in v2:
time: 106 us
  matrix products  47.5 us (45%)
  local copies, waits for them, and re-layouts  22.8 us (22%)
  starting transfers between devices  14.6 us (14%)
  waiting for transfers between devices  11 us (10%)
  other arithmetic  6.1 us (6%)
  Pallas kernels  3.13 us (3%)
    dot_general x4, matrix products, per_device(): jnp.dot(hidden, wo, preferred_element_type=jnp.float32).astype(jnp.bfloat16)  19.2 us
    dot_general x4, matrix products, per_device(): jnp.dot(rounded[:, half:], r_o, preferred_element_type=jnp.float32)  10.9 us
    ppermute x3, waiting for transfers between devices, gather_blocks(): held = jnp.concatenate([held, lax.ppermute(held, axis, pairs)], axis=0)  9.15 us
    dot_general x3, matrix products, per_device(): jnp.dot(guessed, ip, preferred_element_type=jnp.float32)  8.54 us
    ppermute x3, starting transfers between devices, gather_blocks(): held = jnp.concatenate([held, lax.ppermute(held, axis, pairs)], axis=0)  7.09 us
    dynamic_slice x4, local copies, waits for them, and re-layouts, per_device(): kept.append(lax.dynamic_slice_in_dim(guessed, m * half, half, 1))  6.34 us
    dot_general x4, matrix products, per_device(): jnp.dot(one_hot, emb, preferred_element_type=jnp.float32)  5.43 us
    all_to_all x1, starting transfers between devices, per_device(): recv = lax.all_to_all(send, 'tm', split_axis=1, concat_axis=1, tiled=True)  4.87 us
  transfers between devices with their start and end apart: 13, of which 6 were waited for; matrix products, arithmetic and copies ran while one was open for 25% of the time, Pallas kernels for 3%

profile of v2, /device:TPU:0, one launch (start us, length us, event | category | flops | bytes accessed | tf_op | source)
XLA Modules:
  0.0 105.6 jit_solution(7108837316866180942)
XLA Ops:
  0.0 0.6 collective-permute-start.7
  0.6 0.4 collective-permute-start.5
  1.6 2.4 %constant_dynamic-update-slice_fusion.7 = bf16[1024,1024]{1,0:T(8,128)(2,1)} fusion(bf16[512,1024]{1,0:T(8,128)(2,1)} %param.19), kind=kLoop, calls=%fused_computation.112 | loop fusion | bytes 2097152
  4.0 1.1 %constant_dynamic-update-slice_fusion.3 = bf16[1024,1024]{1,0:T(8,128)(2,1)} fusion(bf16[1024,512]{1,0:T(8,128)(2,1)S(1)} %copy-done.9), kind=kLoop, calls=%fused_computation.108 | loop fusion | bytes 2097152
  5.7 1.2 %broadcast_multiply_fusion.g_ref = f32[2,128,1024]{2,1,0:T(8,128)} fusion(f32[1024]{0:T(1024)S(1)} %get-tuple-element.27, f32[2,128]{1,0:T(2,128)S(1)} %get-tuple-element.31), kind=kLoop, calls=%fused_computation.70 | loop fusion | flops 262144 | bytes 1053696 | tf_op jit(solution)/shard_map/mul | solution.py:101
  7.1 1.3 %fusion.50 = f32[256,1024]{1,0:T(8,128)} fusion(bf16[18,1024]{1,0:T(8,128)(2,1)S(1)} %constant_dynamic-update-slice_fusion.4, s32[256]{0:T(256)S(1)} %bitcast.77), kind=kOutput, calls=%fused_computation.87 | convolution fusion | flops 9441792 | bytes 1086464 | tf_op jit(solution)/shard_map/dot_general | solution.py:152
  8.4 1.3 %fusion.48 = f32[256,1024]{1,0:T(8,128)} fusion(bf16[18,1024]{1,0:T(8,128)(2,1)S(1)} %constant_dynamic-update-slice_fusion.4, s32[256]{0:T(256)S(1)} %bitcast.76), kind=kOutput, calls=%fused_computation.85 | convolution fusion | flops 9441792 | bytes 1086464 | tf_op jit(solution)/shard_map/dot_general | solution.py:152
  9.7 1.4 %fusion.47 = f32[256,1024]{1,0:T(8,128)} fusion(bf16[18,1024]{1,0:T(8,128)(2,1)S(1)} %constant_dynamic-update-slice_fusion.4, s32[256]{0:T(256)S(1)} %bitcast.75), kind=kOutput, calls=%fused_computation.84 | convolution fusion | flops 9441792 | bytes 1086464 | tf_op jit(solution)/shard_map/dot_general | solution.py:152
  11.1 1.4 %constant_dynamic-update-slice_fusion = bf16[1024,1024]{1,0:T(8,128)(2,1)S(1)} fusion(bf16[1024,1024]{1,0:T(8,128)(2,1)S(1)} %constant_dynamic-update-slice_fusion.1, bf16[1024,512]{1,0:T(8,128)(2,1)} %collective-permute-done), kind=kLoop, calls=%fused_computation.105 | loop fusion | bytes 2097152 | tf_op jit(solution)/shard_map/concatenate | solution.py:75
  12.5 1.7 %fusion.2.x_ref = f32[2,128,1024]{2,1,0:T(8,128)} fusion(bf16[1024,1024]{1,0:T(8,128)(2,1)S(1)} %constant_dynamic-update-slice_fusion, f32[1024]{0:T(1024)S(1)} %get-tuple-element.26, bf16[4,128,1024]{2,1,0:T(8,128)(2,1)S(1)} %copy-done, s32[]{:T(128)S(6)} %select_n.83), kind=kOutput, calls=%fused_computation.4 | convolution fusion | flops 537133056 | bytes 3674116 | tf_op jit(solution)/shard_map/dot_general | solution.py:94
  14.3 3.1 %shard_map.100 = f32[2,128,1024]{2,1,0:T(8,128)} custom-call(f32[2,128,1024]{2,1,0:T(8,128)} %fusion.2.x_ref, f32[2,128,1024]{2,1,0:T(8,128)} %broadcast_multiply_fusion.g_ref), custom_call_target="tpu_custom_call" | custom-call | flops 524288 | bytes 3145728 | tf_op jit(solution)/shard_map/pallas_call | solution.py:27
  17.4 0.8 slice.87
  18.3 2.6 %collective-permute-start.1 = (f32[1,2,1152]{2,1,0:T(2,128)S(1)}, f32[1,2,1152]{2,1,0:T(2,128)S(1)}, u32[]{:S(2)}, u32[]{:S(2)}) collective-permute-start(f32[1,2,1152]{2,1,0:T(2,128)S(1)} %maximum_bitcast_fusion), channel_id=1, source_target_pairs={{0,2},{2,4},{4,6},{6,8},{8,10},{10,12},{12,14},{14,0},{1,3},{3,5},... | collective-permute-start | bytes 27656 | tf_op jit(solution)/shard_map/ppermute | solution.py:43
  20.9 1.4 %fusion.49 = f32[256,1024]{1,0:T(8,128)} fusion(bf16[18,1024]{1,0:T(8,128)(2,1)S(1)} %constant_dynamic-update-slice_fusion.4, s32[256]{0:T(256)S(1)} %bitcast.74), kind=kOutput, calls=%fused_computation.86 | convolution fusion | flops 9441792 | bytes 1086464 | tf_op jit(solution)/shard_map/dot_general | solution.py:152
  22.3 1.3 %convert_element_type.133 = bf16[2,128,1024]{2,1,0:T(8,128)(2,1)S(1)} convert(f32[2,128,1024]{2,1,0:T(8,128)} %shard_map.100) | non-fusion elementwise | flops 262144 | bytes 1572864 | tf_op jit(solution)/shard_map/convert_element_type | solution.py:114
  23.6 0.9 copy.25
  24.5 4.9 %all-to-all-start = ((bf16[2,8,16,1024]{3,2,0,1:T(8,128)(2,1)}), bf16[2,8,16,1024]{3,2,0,1:T(8,128)(2,1)}, u32[]{:S(2)}, u32[]{:S(2)}) async-start(bf16[2,8,16,1024]{3,2,0,1:T(8,128)(2,1)} %copy.25), calls=%async_computation | async-start | bytes 1048576 | tf_op jit(solution)/shard_map/all_to_all | solution.py:115
  29.4 2.2 %collective-permute-start.2 = (f32[2,2,1152]{2,1,0:T(2,128)S(1)}, f32[2,2,1152]{2,1,0:T(2,128)S(1)}, u32[]{:S(2)}, u32[]{:S(2)}) collective-permute-start(f32[2,2,1152]{2,1,0:T(2,128)S(1)} %pad_maximum_fusion.5), channel_id=1, source_target_pairs={{0,4},{2,6},{4,8},{6,10},{8,12},{10,14},{12,0},{14,2},{1,5},{3,7},... | collective-permute-start | bytes 55304 | tf_op jit(solution)/shard_map/ppermute | solution.py:43
  31.6 2.3 %constant_dynamic-update-slice_fusion.6 = bf16[1024,1024]{1,0:T(8,128)(2,1)} fusion(bf16[1024,1024]{1,0:T(8,128)(2,1)} %constant_dynamic-update-slice_fusion.7, bf16[512,1024]{1,0:T(8,128)(2,1)} %collective-permute-done.7), kind=kLoop, calls=%fused_computation.111 | loop fusion | bytes 2097152 | tf_op jit(solution)/shard_map/concatenate | solution.py:77
  33.9 8.8 %collective-permute-done.2 = f32[2,2,1152]{2,1,0:T(2,128)S(1)} collective-permute-done((f32[2,2,1152]{2,1,0:T(2,128)S(1)}, f32[2,2,1152]{2,1,0:T(2,128)S(1)}, u32[]{:S(2)}, u32[]{:S(2)}) %collective-permute-start.2) | collective-permute-done | bytes 18464 | tf_op jit(solution)/shard_map/ppermute | solution.py:43
  42.7 2.3 %collective-permute-start.3 = (f32[4,2,1152]{2,1,0:T(2,128)S(1)}, f32[4,2,1152]{2,1,0:T(2,128)S(1)}, u32[]{:S(2)}, u32[]{:S(2)}) collective-permute-start(f32[4,2,1152]{2,1,0:T(2,128)S(1)} %pad_maximum_fusion.4), channel_id=1, source_target_pairs={{0,8},{2,10},{4,12},{6,14},{8,0},{10,2},{12,4},{14,6},{1,9},{3,11}... | collective-permute-start | bytes 110600 | tf_op jit(solution)/shard_map/ppermute | solution.py:43
  44.9 2.4 %constant_dynamic-update-slice_fusion.2 = bf16[1024,1024]{1,0:T(8,128)(2,1)} fusion(bf16[1024,1024]{1,0:T(8,128)(2,1)} %constant_dynamic-update-slice_fusion.3, bf16[1024,512]{1,0:T(8,128)(2,1)} %collective-permute-done.5), kind=kLoop, calls=%fused_computation.107 | loop fusion | bytes 2097152 | tf_op jit(solution)/shard_map/concatenate | solution.py:76
  47.7 0.6 gather_fusion
  49.3 1.2 %multiply_add_fusion.1 = f32[2,8,16,1024]{3,2,0,1:T(8,128)S(1)} fusion(bf16[2,8,16,1024]{3,2,0,1:T(8,128)(2,1)} %all-to-all-done, f32[2,8,1024]{2,0,1:T(2,128)S(1)} %pad_bitcast_fusion, f32[16,1024]{1,0:T(8,128)S(1)} %broadcast_power_fusion, pred[2,8,16]{2,0,1:T(4,128)(4,1)S(1)} %broadcast_compare_fusion), kind=kLoop, calls=%fused_computation.55 | loop fusion | flops 1048576 | bytes 1704192 | tf_op jit(solution)/shard_map/add | solution.py:134
  50.7 1.1 %bitcast_multiply_fusion = f32[256,1024]{1,0:T(8,128)} fusion(f32[2,8,16,1024]{3,2,1,0:T(8,128)S(1)} %copy.30, f32[1024]{0:T(1024)S(1)} %get-tuple-element.27), kind=kLoop, calls=%fused_computation.39 | loop fusion | flops 262144 | bytes 2101248 | tf_op jit(solution)/shard_map/mul | solution.py:160
  52.1 0.4 fusion.17
  52.6 2.7 %multiply_reduce_fusion.3 = (f32[256]{0:T(256)S(1)}, f32[256,1024]{1,0:T(8,128)}) fusion(f32[256,1024]{1,0:T(8,128)S(1)} %fusion.17, bf16[512,1024]{1,0:T(8,128)(2,1)} %collective-permute-done.4, bf16[256,1024]{1,0:T(8,128)(2,1)S(1)} %bitcast_convert_fusion), kind=kOutput, calls=%fused_computation.54 | convolution fusion | flops 269745920 | bytes 3408896 | tf_op jit(solution)/shard_map/dot_general | solution.py:146
  55.3 5.0 %convolution_convert_fusion.11 = bf16[256,1024]{1,0:T(8,128)(2,1)} fusion(bf16[1024,1024]{1,0:T(8,128)(2,1)} %constant_dynamic-update-slice_fusion.6, f32[256,1024]{1,0:T(8,128)} %fusion.47, bf16[1024,1024]{1,0:T(8,128)(2,1)} %constant_dynamic-update-slice_fusion.2, f32[256,1024]{1,0:T(8,128)} %get-tuple-element.33, f32[1024]{0:T(1024)S(1)} %copy-done.14, ...), kind=kOutput, calls=%fused_computation.36 | convolution fusion | flops 1076363264 | bytes 6820864 | tf_op jit(solution)/shard_map/dot_general | solution.py:156
  60.3 1.8 %constant_dynamic-slice_fusion.7 = (bf16[256,512]{1,0:T(8,128)(2,1)S(1)}, bf16[256,512]{1,0:T(8,128)(2,1)}) fusion(bf16[256,1024]{1,0:T(8,128)(2,1)} %convolution_convert_fusion.11, s32[]{:T(128)S(6)} %select_n.84, s32[]{:T(128)S(6)} %select_n.85), kind=kLoop, calls=%fused_computation.131 | loop fusion | bytes 1048584 | tf_op jit(solution)/shard_map/dynamic_slice | solution.py:157
  62.1 3.1 %fusion.69 = (bf16[256,1024]{1,0:T(8,128)(2,1)S(1)}, f32[256,1024]{1,0:T(8,128)}) fusion(f32[256,1024]{1,0:T(8,128)} %bitcast_multiply_fusion, bf16[256,1024]{1,0:T(8,128)(2,1)} %convolution_convert_fusion.11, bf16[1024,1024]{1,0:T(8,128)(2,1)S(1)} %constant_dynamic-update-slice_fusion, f32[1024]{0:T(1024)S(1)} %get-tuple-element.26), kind=kOutput, calls=%fused_computation.162 | convolution fusion | flops 537657344 | bytes 5246976 | tf_op jit(solution)/shard_map/dot_general | solution.py:160
  65.2 0.4 fusion.14
  65.7 2.8 %multiply_reduce_fusion.2 = (f32[256]{0:T(256)S(1)}, f32[256,1024]{1,0:T(8,128)}) fusion(f32[256,1024]{1,0:T(8,128)S(1)} %fusion.14, bf16[512,1024]{1,0:T(8,128)(2,1)} %collective-permute-done.4, bf16[256,1024]{1,0:T(8,128)(2,1)S(1)} %get-tuple-element.34), kind=kOutput, calls=%fused_computation.51 | convolution fusion | flops 269745920 | bytes 3408896 | tf_op jit(solution)/shard_map/dot_general | solution.py:146
  68.4 5.1 %convolution_convert_fusion.10 = bf16[256,1024]{1,0:T(8,128)(2,1)} fusion(bf16[1024,1024]{1,0:T(8,128)(2,1)} %constant_dynamic-update-slice_fusion.6, f32[256,1024]{1,0:T(8,128)} %fusion.48, bf16[1024,1024]{1,0:T(8,128)(2,1)} %constant_dynamic-update-slice_fusion.2, f32[256,1024]{1,0:T(8,128)} %get-tuple-element.37, f32[256]{0:T(256)S(1)} %add_rsqrt_fusion.2, ...), kind=kOutput, calls=%fused_computation.35 | convolution fusion | flops 1076363264 | bytes 6820864 | tf_op jit(solution)/shard_map/dot_general | solution.py:156
  73.5 1.9 %constant_dynamic-slice_fusion.6 = (bf16[256,512]{1,0:T(8,128)(2,1)}, bf16[256,512]{1,0:T(8,128)(2,1)}) fusion(bf16[256,1024]{1,0:T(8,128)(2,1)} %convolution_convert_fusion.10, s32[]{:T(128)S(6)} %select_n.84, s32[]{:T(128)S(6)} %select_n.85), kind=kLoop, calls=%fused_computation.130 | loop fusion | bytes 1048584 | tf_op jit(solution)/shard_map/dynamic_slice | solution.py:157
  75.4 3.2 %fusion.70 = (bf16[256,1024]{1,0:T(8,128)(2,1)S(1)}, f32[256,1024]{1,0:T(8,128)}) fusion(bf16[256,1024]{1,0:T(8,128)(2,1)} %convolution_convert_fusion.10, bf16[1024,1024]{1,0:T(8,128)(2,1)S(1)} %constant_dynamic-update-slice_fusion, f32[1024]{0:T(1024)S(1)} %get-tuple-element.26, f32[256,1024]{1,0:T(8,128)} %get-tuple-element.35, ...), kind=kOutput, calls=%fused_computation.163 | convolution fusion | flops 537919488 | bytes 5251072 | tf_op jit(solution)/shard_map/dot_general | solution.py:160
  78.7 0.4 fusion.11
  79.1 2.6 %multiply_reduce_fusion.1 = (f32[256]{0:T(256)S(1)}, f32[256,1024]{1,0:T(8,128)}) fusion(f32[256,1024]{1,0:T(8,128)S(1)} %fusion.11, bf16[512,1024]{1,0:T(8,128)(2,1)} %collective-permute-done.4, bf16[256,1024]{1,0:T(8,128)(2,1)S(1)} %get-tuple-element.38), kind=kOutput, calls=%fused_computation.47 | convolution fusion | flops 269745920 | bytes 3408896 | tf_op jit(solution)/shard_map/dot_general | solution.py:146
  81.7 5.1 %convolution_convert_fusion.9 = bf16[256,1024]{1,0:T(8,128)(2,1)} fusion(bf16[1024,1024]{1,0:T(8,128)(2,1)} %constant_dynamic-update-slice_fusion.6, f32[256,1024]{1,0:T(8,128)} %fusion.49, bf16[1024,1024]{1,0:T(8,128)(2,1)} %constant_dynamic-update-slice_fusion.2, f32[256,1024]{1,0:T(8,128)} %get-tuple-element.41, f32[256]{0:T(256)S(1)} %add_rsqrt_fusion.1, ...), kind=kOutput, calls=%fused_computation.34 | convolution fusion | flops 1076363264 | bytes 6820864 | tf_op jit(solution)/shard_map/dot_general | solution.py:156
  86.8 1.9 %constant_dynamic-slice_fusion.5 = (bf16[256,512]{1,0:T(8,128)(2,1)}, bf16[256,512]{1,0:T(8,128)(2,1)}) fusion(bf16[256,1024]{1,0:T(8,128)(2,1)} %convolution_convert_fusion.9, s32[]{:T(128)S(6)} %select_n.84, s32[]{:T(128)S(6)} %select_n.85), kind=kLoop, calls=%fused_computation.129 | loop fusion | bytes 1048584 | tf_op jit(solution)/shard_map/dynamic_slice | solution.py:157
  88.7 2.2 %add_convert_fusion = bf16[256,1024]{1,0:T(8,128)(2,1)S(1)} fusion(f32[256,1024]{1,0:T(8,128)} %get-tuple-element.39, bf16[256,1024]{1,0:T(8,128)(2,1)} %convolution_convert_fusion.9, bf16[1024,1024]{1,0:T(8,128)(2,1)S(1)} %constant_dynamic-update-slice_fusion, f32[1024]{0:T(1024)S(1)} %get-tuple-element.26, f32[1024]{0:T(1024)S(1)} %get-tuple-element.27), kind=kOutput, calls=%fused_computation.44 | convolution fusion | flops 537919488 | bytes 4202496 | tf_op jit(solution)/shard_map/dot_general | solution.py:160
  90.9 0.4 fusion.8
  91.4 2.8 %multiply_reduce_fusion = (f32[256]{0:T(256)S(1)}, f32[256,1024]{1,0:T(8,128)}) fusion(f32[256,1024]{1,0:T(8,128)S(1)} %fusion.8, bf16[512,1024]{1,0:T(8,128)(2,1)} %collective-permute-done.4, bf16[256,1024]{1,0:T(8,128)(2,1)S(1)} %add_convert_fusion), kind=kOutput, calls=%fused_computation.43 | convolution fusion | flops 269745920 | bytes 3408896 | tf_op jit(solution)/shard_map/dot_general | solution.py:146
  94.2 4.0 %convolution_convert_fusion.8 = bf16[256,1024]{1,0:T(8,128)(2,1)S(1)} fusion(bf16[1024,1024]{1,0:T(8,128)(2,1)} %constant_dynamic-update-slice_fusion.6, f32[256,1024]{1,0:T(8,128)S(1)} %copy-done.7, bf16[1024,1024]{1,0:T(8,128)(2,1)} %constant_dynamic-update-slice_fusion.2, f32[256,1024]{1,0:T(8,128)} %get-tuple-element.43, f32[256]{0:T(256)S(1)} %add_rsqrt_fusion, ...), kind=kOutput, calls=%fused_computation.33 | convolution fusion | flops 1076363264 | bytes 6820864 | tf_op jit(solution)/shard_map/dot_general | solution.py:156
  98.2 0.7 constant_dynamic-slice_fusion.4
  99.0 0.5 collective-permute-start.10
  99.5 0.5 collective-permute-start.8
  100.0 0.7 collective-permute-done.11
  102.3 3.3 %copy.32 = bf16[4,8,16,4,512]{4,3,2,1,0:T(4,128)(2,1)} copy(bf16[4,8,16,4,512]{4,2,1,0,3:T(8,128)(2,1)S(1)} %pad_maximum_fusion) | data formatting | bytes 4194304 | tf_op jit(solution)/shard_map/concatenate | solution.py:167
  (92 shorter events, 4.8 us)
Async XLA Ops:
  0.0 12.5 %copy-start = (bf16[4,128,1024]{2,1,0:T(8,128)(2,1)S(1)}, bf16[4,128,1024]{2,1,0:T(8,128)(2,1)}, u32[]{:S(2)}) copy-start(bf16[4,128,1024]{2,1,0:T(8,128)(2,1)} %param.10) | copy-start | bytes 3145732
  0.0 3.9 %copy-start.10 = (bf16[18,512]{1,0:T(8,128)(2,1)S(1)}, bf16[18,512]{1,0:T(8,128)(2,1)}, u32[]{:S(2)}) copy-start(bf16[18,512]{1,0:T(8,128)(2,1)} %param.18) | copy-start | bytes 55300
  0.0 3.9 %copy-start.9 = (bf16[1024,512]{1,0:T(8,128)(2,1)S(1)}, bf16[1024,512]{1,0:T(8,128)(2,1)}, u32[]{:S(2)}) copy-start(bf16[1024,512]{1,0:T(8,128)(2,1)} %param.17) | copy-start | bytes 3145732
  0.0 31.6 %collective-permute-start.7 = (bf16[512,1024]{1,0:T(8,128)(2,1)}, bf16[512,1024]{1,0:T(8,128)(2,1)}, u32[]{:S(2)}, u32[]{:S(2)}) collective-permute-start(bf16[512,1024]{1,0:T(8,128)(2,1)} %param.19), channel_id=1, source_target_pairs={{0,1},{1,0},{2,3},{3,2},{4,5},{5,4},{6,7},{7,6},{8,9},{9,8},{10,11... | collective-permute-start | bytes 3145736 | tf_op jit(solution)/shard_map/ppermute | solution.py:67
  0.6 6.5 %collective-permute-start.6 = (bf16[18,512]{1,0:T(8,128)(2,1)}, bf16[18,512]{1,0:T(8,128)(2,1)S(1)}, u32[]{:S(2)}, u32[]{:S(2)}) collective-permute-start(bf16[18,512]{1,0:T(8,128)(2,1)} %param.18), channel_id=1, source_target_pairs={{0,1},{1,0},{2,3},{3,2},{4,5},{5,4},{6,7},{7,6},{8,9},{9,8},{10,11... | collective-permute-start | bytes 55304 | tf_op jit(solution)/shard_map/ppermute | solution.py:67
  0.6 44.3 %collective-permute-start.5 = (bf16[1024,512]{1,0:T(8,128)(2,1)}, bf16[1024,512]{1,0:T(8,128)(2,1)}, u32[]{:S(2)}, u32[]{:S(2)}) collective-permute-start(bf16[1024,512]{1,0:T(8,128)(2,1)} %param.17), channel_id=1, source_target_pairs={{0,1},{1,0},{2,3},{3,2},{4,5},{5,4},{6,7},{7,6},{8,9},{9,8},{10,11... | collective-permute-start | bytes 3145736 | tf_op jit(solution)/shard_map/ppermute | solution.py:67
  1.1 10.1 %collective-permute-start = (bf16[1024,512]{1,0:T(8,128)(2,1)}, bf16[1024,512]{1,0:T(8,128)(2,1)}, u32[]{:S(2)}, u32[]{:S(2)}) collective-permute-start(bf16[1024,512]{1,0:T(8,128)(2,1)} %param.13), channel_id=1, source_target_pairs={{0,1},{1,0},{2,3},{3,2},{4,5},{5,4},{6,7},{7,6},{8,9},{9,8},{10,11... | collective-permute-start | bytes 3145736 | tf_op jit(solution)/shard_map/ppermute | solution.py:67
  1.2 51.4 %collective-permute-start.4 = (bf16[512,1024]{1,0:T(8,128)(2,1)}, bf16[512,1024]{1,0:T(8,128)(2,1)}, u32[]{:S(2)}, u32[]{:S(2)}) collective-permute-start(bf16[512,1024]{1,0:T(8,128)(2,1)} %param.15), channel_id=1, source_target_pairs={{0,1},{1,0},{2,3},{3,2},{4,5},{5,4},{6,7},{7,6},{8,9},{9,8},{10,11... | collective-permute-start | bytes 3145736 | tf_op jit(solution)/shard_map/ppermute | solution.py:67
  1.6 3.5 %copy-start.8 = (bf16[1024,512]{1,0:T(8,128)(2,1)S(1)}, bf16[1024,512]{1,0:T(8,128)(2,1)}, u32[]{:S(2)}) copy-start(bf16[1024,512]{1,0:T(8,128)(2,1)} %param.13) | copy-start | bytes 3145732
  4.0 1.3 %copy-start.11 = (s32[4,8,16,4]{2,3,1,0:T(4,128)S(1)}, s32[4,8,16,4]{2,3,1,0:T(4,128)}, u32[]{:S(2)}) copy-start(s32[4,8,16,4]{2,3,1,0:T(4,128)} %param.12) | copy-start | bytes 24580
  4.0 1.5 %copy-start.13 = (s32[4,128]{1,0:T(4,128)S(1)}, s32[4,128]{1,0:T(4,128)}, u32[]{:S(2)}) copy-start(s32[4,128]{1,0:T(4,128)} %param.11) | copy-start | bytes 6148
  4.0 1.6 %copy-start.12 = (f32[1024]{0:T(1024)S(1)}, f32[1024]{0:T(1024)}, u32[]{:S(2)}) copy-start(f32[1024]{0:T(1024)} %param.14) | copy-start | bytes 12292
  18.3 11.0 %collective-permute-start.1 = (f32[1,2,1152]{2,1,0:T(2,128)S(1)}, f32[1,2,1152]{2,1,0:T(2,128)S(1)}, u32[]{:S(2)}, u32[]{:S(2)}) collective-permute-start(f32[1,2,1152]{2,1,0:T(2,128)S(1)} %maximum_bitcast_fusion), channel_id=1, source_target_pairs={{0,2},{2,4},{4,6},{6,8},{8,10},{10,12},{12,14},{14,0},{1,3},{3,5},... | collective-permute-start | bytes 27656 | tf_op jit(solution)/shard_map/ppermute | solution.py:43
  24.5 24.8 %all-to-all-start = ((bf16[2,8,16,1024]{3,2,0,1:T(8,128)(2,1)}), bf16[2,8,16,1024]{3,2,0,1:T(8,128)(2,1)}, u32[]{:S(2)}, u32[]{:S(2)}) async-start(bf16[2,8,16,1024]{3,2,0,1:T(8,128)(2,1)} %copy.25), calls=%async_computation | async-start | bytes 1048576 | tf_op jit(solution)/shard_map/all_to_all | solution.py:115
  29.4 13.3 %collective-permute-start.2 = (f32[2,2,1152]{2,1,0:T(2,128)S(1)}, f32[2,2,1152]{2,1,0:T(2,128)S(1)}, u32[]{:S(2)}, u32[]{:S(2)}) collective-permute-start(f32[2,2,1152]{2,1,0:T(2,128)S(1)} %pad_maximum_fusion.5), channel_id=1, source_target_pairs={{0,4},{2,6},{4,8},{6,10},{8,12},{10,14},{12,0},{14,2},{1,5},{3,7},... | collective-permute-start | bytes 55304 | tf_op jit(solution)/shard_map/ppermute | solution.py:43
  42.7 5.0 %collective-permute-start.3 = (f32[4,2,1152]{2,1,0:T(2,128)S(1)}, f32[4,2,1152]{2,1,0:T(2,128)S(1)}, u32[]{:S(2)}, u32[]{:S(2)}) collective-permute-start(f32[4,2,1152]{2,1,0:T(2,128)S(1)} %pad_maximum_fusion.4), channel_id=1, source_target_pairs={{0,8},{2,10},{4,12},{6,14},{8,0},{10,2},{12,4},{14,6},{1,9},{3,11}... | collective-permute-start | bytes 110600 | tf_op jit(solution)/shard_map/ppermute | solution.py:43
  50.7 1.4 %copy-start.1 = (bf16[512,1024]{1,0:T(8,128)(2,1)S(1)}, bf16[512,1024]{1,0:T(8,128)(2,1)}, u32[]{:S(2)}) copy-start(bf16[512,1024]{1,0:T(8,128)(2,1)} %param.15) | copy-start | bytes 3145732
  52.5 2.7 %copy-start.14 = (f32[1024]{0:T(1024)S(1)}, f32[1024]{0:T(1024)}, u32[]{:S(2)}) copy-start(f32[1024]{0:T(1024)} %param.16) | copy-start | bytes 12292
  62.1 3.1 %copy-start.2 = (bf16[512,1024]{1,0:T(8,128)(2,1)S(1)}, bf16[512,1024]{1,0:T(8,128)(2,1)}, u32[]{:S(2)}) copy-start(bf16[512,1024]{1,0:T(8,128)(2,1)} %param.15) | copy-start | bytes 3145732
  75.4 3.2 %copy-start.3 = (bf16[512,1024]{1,0:T(8,128)(2,1)S(1)}, bf16[512,1024]{1,0:T(8,128)(2,1)}, u32[]{:S(2)}) copy-start(bf16[512,1024]{1,0:T(8,128)(2,1)} %param.15) | copy-start | bytes 3145732
  88.7 2.2 %copy-start.4 = (bf16[512,1024]{1,0:T(8,128)(2,1)S(1)}, bf16[512,1024]{1,0:T(8,128)(2,1)}, u32[]{:S(2)}) copy-start(bf16[512,1024]{1,0:T(8,128)(2,1)} %param.15) | copy-start | bytes 3145732
  91.4 2.8 %copy-start.7 = (f32[256,1024]{1,0:T(8,128)S(1)}, f32[256,1024]{1,0:T(8,128)}, u32[]{:S(2)}) copy-start(f32[256,1024]{1,0:T(8,128)} %fusion.50) | copy-start | bytes 3145732
  94.2 7.6 %copy-start.5 = (bf16[256,512]{1,0:T(8,128)(2,1)S(1)}, bf16[256,512]{1,0:T(8,128)(2,1)}, u32[]{:S(2)}) copy-start(bf16[256,512]{1,0:T(8,128)(2,1)} %get-tuple-element.9) | copy-start | bytes 786436
  94.2 7.6 %copy-start.6 = (bf16[256,512]{1,0:T(8,128)(2,1)S(1)}, bf16[256,512]{1,0:T(8,128)(2,1)}, u32[]{:S(2)}) copy-start(bf16[256,512]{1,0:T(8,128)(2,1)} %get-tuple-element.11) | copy-start | bytes 786436
  99.0 1.7 %collective-permute-start.11 = (bf16[256,512]{1,0:T(8,128)(2,1)}, bf16[256,512]{1,0:T(8,128)(2,1)S(1)}, u32[]{:S(2)}, u32[]{:S(2)}) collective-permute-start(bf16[256,512]{1,0:T(8,128)(2,1)} %get-tuple-element.14), channel_id=1, source_target_pairs={{0,1},{1,0},{2,3},{3,2},{4,5},{5,4},{6,7},{7,6},{8,9},{9,8},{10,11... | collective-permute-start | bytes 786440 | tf_op jit(solution)/shard_map/ppermute | solution.py:67
  99.0 2.1 %collective-permute-start.10 = (bf16[256,512]{1,0:T(8,128)(2,1)}, bf16[256,512]{1,0:T(8,128)(2,1)S(1)}, u32[]{:S(2)}, u32[]{:S(2)}) collective-permute-start(bf16[256,512]{1,0:T(8,128)(2,1)} %get-tuple-element.12), channel_id=1, source_target_pairs={{0,1},{1,0},{2,3},{3,2},{4,5},{5,4},{6,7},{7,6},{8,9},{9,8},{10,11... | collective-permute-start | bytes 786440 | tf_op jit(solution)/shard_map/ppermute | solution.py:67
  99.5 2.0 %collective-permute-start.9 = (bf16[256,512]{1,0:T(8,128)(2,1)}, bf16[256,512]{1,0:T(8,128)(2,1)S(1)}, u32[]{:S(2)}, u32[]{:S(2)}) collective-permute-start(bf16[256,512]{1,0:T(8,128)(2,1)} %get-tuple-element.10), channel_id=1, source_target_pairs={{0,1},{1,0},{2,3},{3,2},{4,5},{5,4},{6,7},{7,6},{8,9},{9,8},{10,11... | collective-permute-start | bytes 786440 | tf_op jit(solution)/shard_map/ppermute | solution.py:67
  99.5 2.4 %collective-permute-start.8 = (bf16[256,512]{1,0:T(8,128)(2,1)}, bf16[256,512]{1,0:T(8,128)(2,1)S(1)}, u32[]{:S(2)}, u32[]{:S(2)}) collective-permute-start(bf16[256,512]{1,0:T(8,128)(2,1)} %get-tuple-element.8), channel_id=1, source_target_pairs={{0,1},{1,0},{2,3},{3,2},{4,5},{5,4},{6,7},{7,6},{8,9},{9,8},{10,11... | collective-permute-start | bytes 786440 | tf_op jit(solution)/shard_map/ppermute | solution.py:67

commit v3 on v2

--- a/solution.py
+++ b/solution.py
@@ -73,9 +73,6 @@
     wo_o = partner(w_out)
     emb_o = partner(action_embed)
     ip = jnp.concatenate([in_proj, ip_o], axis=1)
-    wh = jnp.concatenate([w_hidden, wh_o], axis=1)
-    wo = jnp.concatenate([w_out, wo_o], axis=0)
-    emb = jnp.concatenate([action_embed, emb_o], axis=1)
 
     rates = jnp.concatenate(
         [
@@ -137,34 +134,86 @@
     rows = bh * blocks * sub
     current = posterior.reshape(rows, width)
     my_actions = lax.dynamic_slice_in_dim(actions, m * bh, bh, 0).reshape(rows, horizon)
-    table_ids = jnp.arange(emb.shape[0], dtype=jnp.int32)
-    kept, given = [], []
-    for step in range(horizon):
-        rounded = current.astype(jnp.bfloat16)
-        features = jnp.dot(
-            rounded[:, :half], readout_w, preferred_element_type=jnp.float32
-        ).astype(jnp.bfloat16).astype(jnp.float32) + jnp.dot(
-            rounded[:, half:], r_o, preferred_element_type=jnp.float32
-        ).astype(jnp.bfloat16).astype(jnp.float32)
-        mean_sq = jnp.mean(features * features, axis=-1, keepdims=True)
-        normed = (features * lax.rsqrt(mean_sq + 1e-06) * norm_gain).astype(jnp.bfloat16)
-        one_hot = (my_actions[:, step][:, None] == table_ids[None, :]).astype(jnp.bfloat16)
-        pre_act = jnp.dot(normed, wh, preferred_element_type=jnp.float32) + jnp.dot(
-            one_hot, emb, preferred_element_type=jnp.float32
-        )
-        hidden = jax.nn.silu(pre_act).astype(jnp.bfloat16)
-        guessed = jnp.dot(hidden, wo, preferred_element_type=jnp.float32).astype(jnp.bfloat16)
-        kept.append(lax.dynamic_slice_in_dim(guessed, m * half, half, 1))
-        given.append(partner(lax.dynamic_slice_in_dim(guessed, (1 - m) * half, half, 1)))
-        if step < horizon - 1:
-            current = decays * current + scaling * jnp.dot(
-                guessed, ip, preferred_element_type=jnp.float32
-            )
-    mine = jnp.stack(kept, axis=1).reshape(bh, blocks, sub, horizon, half)
-    theirs = jnp.stack(given, axis=1).reshape(bh, blocks, sub, horizon, half)
+    table = jnp.concatenate([action_embed, emb_o], axis=1)
+    table = jnp.pad(table, ((0, 128 - table.shape[0]), (0, 0)))
+    one_hot = (
+        jnp.swapaxes(my_actions, 0, 1)[:, :, None] == jnp.arange(128, dtype=jnp.int32)
+    ).astype(jnp.bfloat16)
+    vecs = jnp.stack([decays, scaling, norm_gain], axis=0)
+    side = jnp.reshape(m, (1,)).astype(jnp.int32)
+    keep_part, give_part = imagine(
+        side, current, one_hot, vecs, readout_w, r_o, w_hidden, wh_o, table, w_out, wo_o,
+        in_proj, ip_o,
+    )
+    got = partner(give_part)
+
+    def arrange(part):
+        return jnp.transpose(part.reshape(horizon, bh, blocks, sub, half), (1, 2, 3, 0, 4))
+
+    mine, theirs = arrange(keep_part), arrange(got)
     first_half = jnp.where(m == 0, mine, theirs)
     second_half = jnp.where(m == 0, theirs, mine)
     return jnp.concatenate([first_half, second_half], axis=0)
+
+
+def _imagine_kernel(
+    side_ref, cur_ref, hot_ref, vec_ref, r_a, r_b, wh_a, wh_b, emb_ref, wo_a, wo_b, ip_a, ip_b,
+    keep_ref, give_ref,
+):
+    horizon, rows, _ = hot_ref.shape
+    half = r_a.shape[0]
+    width = 2 * half
+    tile = 128
+    lead = side_ref[0] == 0
+
+    def dot(a, b):
+        return jnp.dot(a, b, preferred_element_type=jnp.float32)
+
+    def chunk(c, carry):
+        rs = pl.ds(pl.multiple_of(c * tile, tile), tile)
+        cur_a = cur_ref[rs, :half]
+        cur_b = cur_ref[rs, half:]
+        for step in range(horizon):
+            f = dot(cur_a.astype(jnp.bfloat16), r_a[...]).astype(jnp.bfloat16).astype(
+                jnp.float32
+            ) + dot(cur_b.astype(jnp.bfloat16), r_b[...]).astype(jnp.bfloat16).astype(jnp.float32)
+            mean_sq = jnp.sum(f * f, axis=-1, keepdims=True) * (1.0 / width)
+            normed = (f * lax.rsqrt(mean_sq + 1e-06) * vec_ref[2:3, :]).astype(jnp.bfloat16)
+            hot = hot_ref[step, rs, :]
+            pre_a = dot(normed, wh_a[...]) + dot(hot, emb_ref[:, :half])
+            pre_b = dot(normed, wh_b[...]) + dot(hot, emb_ref[:, half:])
+            hid_a = (pre_a * jax.nn.sigmoid(pre_a)).astype(jnp.bfloat16)
+            hid_b = (pre_b * jax.nn.sigmoid(pre_b)).astype(jnp.bfloat16)
+            lo = (dot(hid_a, wo_a[:, :half]) + dot(hid_b, wo_b[:, :half])).astype(jnp.bfloat16)
+            hi = (dot(hid_a, wo_a[:, half:]) + dot(hid_b, wo_b[:, half:])).astype(jnp.bfloat16)
+            keep_ref[step, rs, :] = jnp.where(lead, lo, hi)
+            give_ref[step, rs, :] = jnp.where(lead, hi, lo)
+            if step < horizon - 1:
+                up_a = dot(lo, ip_a[:half, :]) + dot(hi, ip_a[half:, :])
+                up_b = dot(lo, ip_b[:half, :]) + dot(hi, ip_b[half:, :])
+                cur_a = vec_ref[0:1, :half] * cur_a + vec_ref[1:2, :half] * up_a
+                cur_b = vec_ref[0:1, half:] * cur_b + vec_ref[1:2, half:] * up_b
+        return carry
+
+    lax.fori_loop(0, rows // tile, chunk, 0)
+
+
+def imagine(side, current, one_hot, vecs, *weights):
+    horizon, rows, _ = one_hot.shape
+    half = weights[0].shape[0]
+    out = jax.ShapeDtypeStruct((horizon, rows, half), jnp.bfloat16)
+    vmem = pl.BlockSpec(memory_space=pltpu.VMEM)
+    flops = 2 * rows * horizon * 4 * (2 * half) * (2 * half)
+    return pl.pallas_call(
+        _imagine_kernel,
+        out_shape=(out, out),
+        in_specs=[pl.BlockSpec(memory_space=pltpu.SMEM)] + [vmem] * (3 + len(weights)),
+        out_specs=(vmem, vmem),
+        compiler_params=pltpu.CompilerParams(vmem_limit_bytes=48 * 1024 * 1024),
+        cost_estimate=pl.CostEstimate(
+            flops=flops, bytes_accessed=16 * 1024 * 1024, transcendentals=rows * horizon * 2 * half
+        ),
+    )(side, current, one_hot, vecs, *weights)
 
 
 def solution(mesh):

time: 106 us -> 74.8 us (0.71)
  matrix products: 47.5 us -> 2.91 us
  Pallas kernels: 3.13 us -> 19.5 us
  waiting for transfers between devices: 11 us -> 24.3 us
  local copies, waits for them, and re-layouts: 22.8 us -> 10.9 us
  starting transfers between devices: 14.6 us -> 8.4 us
  other arithmetic: 6.1 us -> 7.91 us
    dot_general x19 -> x0, matrix products: 45.8 us -> none  [the longest x4 19.2 us: per_device(): jnp.dot(hidden, wo, preferred_element_type=jnp.float32).astype(jnp.bfloat16)]
    pallas_call x0 -> x1, Pallas kernels: none -> 16.3 us  [imagine(): pl.pallas_call(_imagine_kernel, out_shape=(out, out), in_specs=[pl.BlockS...]
    all_to_all x1, waiting for transfers between devices: 0.01 us -> 11.1 us  [per_device(): recv = lax.all_to_all(send, 'tm', split_axis=1, concat_axis=1, tiled=True)]
    concatenate x5 -> x0, local copies, waits for them, and re-layouts: 9.28 us -> none  [the longest x1 3.27 us: per_device(): return jnp.concatenate([first_half, second_half], axis=0)]
    dynamic_slice x4 -> x0, local copies, waits for them, and re-layouts: 6.34 us -> none  [per_device(): kept.append(lax.dynamic_slice_in_dim(guessed, m * half, half, 1))]
    ppermute x3, starting transfers between devices: 7.09 us -> 2.71 us  [gather_blocks(): held = jnp.concatenate([held, lax.ppermute(held, axis, pairs)], axis=0)]
    concatenate x1, other arithmetic: 0.18 us -> 2.67 us  [per_device(): return jnp.concatenate([first_half, second_half], axis=0)]
    select_n x0 -> x2, local copies, waits for them, and re-layouts: none -> 1.78 us  [the longest x1 0.89 us: per_device(): second_half = jnp.where(m == 0, theirs, mine)]
  transfers between devices with their start and end apart: 13 -> 10, of which waited for: 6 -> 4; matrix products, arithmetic and copies ran while one was open for 25% -> 17% of each run, Pallas kernels for 3% -> 4%
where the time goes in v3:
time: 74.8 us; the launch traced here: 74.2 us
  waiting for transfers between devices  24.3 us (32%)
  Pallas kernels  19.5 us (26%)
  local copies, waits for them, and re-layouts  10.9 us (15%)
  starting transfers between devices  8.4 us (11%)
  other arithmetic  7.91 us (11%)
  matrix products  2.91 us (4%)
    pallas_call x1, Pallas kernels, imagine(): pl.pallas_call(_imagine_kernel, out_shape=(out, out), in_specs=[pl.BlockS...  16.3 us
    all_to_all x1, waiting for transfers between devices, per_device(): recv = lax.all_to_all(send, 'tm', split_axis=1, concat_axis=1, tiled=True)  11.1 us
    ppermute x3, waiting for transfers between devices, gather_blocks(): held = jnp.concatenate([held, lax.ppermute(held, axis, pairs)], axis=0)  10.3 us
    unnamed x13, local copies, waits for them, and re-layouts  4.42 us
    all_to_all x1, starting transfers between devices, per_device(): recv = lax.all_to_all(send, 'tm', split_axis=1, concat_axis=1, tiled=True)  4.17 us
    pallas_call x1, Pallas kernels, local_scan(): pl.pallas_call(_scan_kernel, out_shape=jax.ShapeDtypeStruct(driven.shape,...  3.17 us
    dot_general x1, matrix products, per_device(): jnp.dot(x.reshape(bh * steps, feat), ip, preferred_element_type=jnp.float32)  2.91 us
    ppermute x6, waiting for transfers between devices, partner(): return lax.ppermute(x, 'mp', swap)  2.88 us
  transfers between devices with their start and end apart: 10, of which 4 were waited for; matrix products, arithmetic and copies ran while one was open for 17% of the time, Pallas kernels for 4%

profile of v3, /device:TPU:0, one launch (start us, length us, event | category | flops | bytes accessed | tf_op | source)
XLA Modules:
  0.0 74.2 jit_solution(8927264675710101627)
XLA Ops:
  0.0 0.5 collective-permute-start
  0.5 0.1 collective-permute-start.4
  0.6 0.4 collective-permute-start.5
  1.0 0.1 collective-permute-start.7
  1.1 0.4 collective-permute-start.6
  1.5 0.8 %fusion.11 = (s32[2]{0:T(128)S(1)}, f32[2,128]{1,0:T(2,128)S(1)}) fusion(s32[4,128]{1,0:T(4,128)} %param.11, s32[]{:T(128)S(6)} %select_n.87), kind=kLoop, calls=%fused_computation.56 | loop fusion | flops 1278 | bytes 2060 | tf_op jit(solution)/shard_map/reduce_min | solution.py:102
  2.3 0.8 %constant_dynamic-slice_fusion = s32[2,8,16,4]{2,3,1,0:T(4,128)S(1)} fusion(s32[4,8,16,4]{2,3,1,0:T(4,128)} %param.12, s32[]{:T(128)S(6)} %select_n.87), kind=kLoop, calls=%fused_computation.58 | loop fusion | bytes 8196 | tf_op jit(solution)/shard_map/dynamic_slice | solution.py:136
  3.1 0.8 %fusion.20 = (f32[512]{0:T(512)S(1)}, f32[512]{0:T(512)S(1)}) fusion(f32[1024]{0:T(1024)} %param.14, s32[]{:T(128)S(6)} %select_n.88, s32[]{:T(128)S(6)} %select_n.89), kind=kLoop, calls=%fused_computation.69 | loop fusion | bytes 8200 | tf_op jit(solution)/shard_map/dynamic_slice | solution.py:79
  4.0 0.1 reshape.223
  4.1 0.7 pad_maximum_fusion.4.vec_ref
  4.8 0.1 broadcast_power_fusion
  5.0 0.2 fusion.7.hot_ref
  5.2 1.1 %broadcast_multiply_fusion.g_ref = f32[2,128,1024]{2,1,0:T(8,128)} fusion(f32[1024]{0:T(1024)S(1)} %get-tuple-element.21, f32[2,128]{1,0:T(2,128)S(1)} %get-tuple-element.25), kind=kLoop, calls=%fused_computation.16 | loop fusion | flops 262144 | bytes 1053696 | tf_op jit(solution)/shard_map/mul | solution.py:98
  6.3 1.0 %copy-done.5 = bf16[1024,512]{1,0:T(8,128)(2,1)} copy-done((bf16[1024,512]{1,0:T(8,128)(2,1)}, bf16[1024,512]{1,0:T(8,128)(2,1)S(1)}, u32[]{:S(2)}) %copy-start.5) | copy-done | bytes 1048600
  7.3 2.9 %fusion.3.x_ref = f32[2,128,1024]{2,1,0:T(8,128)} fusion(bf16[1024,512]{1,0:T(8,128)(2,1)S(1)} %collective-permute-done.ip_b, bf16[1024,512]{1,0:T(8,128)(2,1)} %ip_a.1, f32[1024]{0:T(1024)S(1)} %get-tuple-element.20, bf16[4,128,1024]{2,1,0:T(8,128)(2,1)S(1)} %copy-done, s32[]{:T(128)S(6)} %select_n.87), kind=kOutput, calls=%fused_computation.6 | convolution fusion | flops 541327360 | bytes 3674116 | tf_op jit(solution)/shard_map/dot_general | solution.py:91
  10.2 3.2 %shard_map.100 = f32[2,128,1024]{2,1,0:T(8,128)} custom-call(f32[2,128,1024]{2,1,0:T(8,128)} %fusion.3.x_ref, f32[2,128,1024]{2,1,0:T(8,128)} %broadcast_multiply_fusion.g_ref), custom_call_target="tpu_custom_call" | custom-call | flops 524288 | bytes 3145728 | tf_op jit(solution)/shard_map/pallas_call | solution.py:27
  13.4 0.8 %slice.39 = f32[2,1,1024]{2,1,0:T(1,128)S(1)} slice(f32[2,128,1024]{2,1,0:T(8,128)} %shard_map.100), slice={[0:2], [127:128], [0:1024]} | slice | bytes 16384 | tf_op jit(solution)/shard_map/slice | solution.py:104
  14.2 0.1 broadcast_in_dim.48
  14.3 2.6 %collective-permute-start.1 = (f32[1,2,1152]{2,1,0:T(2,128)S(1)}, f32[1,2,1152]{2,1,0:T(2,128)S(1)}, u32[]{:S(2)}, u32[]{:S(2)}) collective-permute-start(f32[1,2,1152]{2,1,0:T(2,128)S(1)} %maximum_bitcast_fusion.4), channel_id=1, source_target_pairs={{0,2},{2,4},{4,6},{6,8},{8,10},{10,12},{12,14},{14,0},{1,3},{3,5},... | collective-permute-start | bytes 27656 | tf_op jit(solution)/shard_map/ppermute | solution.py:43
  16.9 4.7 %collective-permute-done.1 = f32[1,2,1152]{2,1,0:T(2,128)S(1)} collective-permute-done((f32[1,2,1152]{2,1,0:T(2,128)S(1)}, f32[1,2,1152]{2,1,0:T(2,128)S(1)}, u32[]{:S(2)}, u32[]{:S(2)}) %collective-permute-start.1) | collective-permute-done | bytes 9248 | tf_op jit(solution)/shard_map/ppermute | solution.py:43
  21.6 0.1 collective-permute-start.2
  21.7 5.6 %collective-permute-done.2 = f32[2,2,1152]{2,1,0:T(2,128)S(1)} collective-permute-done((f32[2,2,1152]{2,1,0:T(2,128)S(1)}, f32[2,2,1152]{2,1,0:T(2,128)S(1)}, u32[]{:S(2)}, u32[]{:S(2)}) %collective-permute-start.2) | collective-permute-done | bytes 18464 | tf_op jit(solution)/shard_map/ppermute | solution.py:43
  27.3 0.1 collective-permute-start.3
  27.4 1.3 %convert_element_type.38 = bf16[2,128,1024]{2,1,0:T(8,128)(2,1)S(1)} convert(f32[2,128,1024]{2,1,0:T(8,128)} %shard_map.100) | non-fusion elementwise | flops 262144 | bytes 1572864 | tf_op jit(solution)/shard_map/convert_element_type | solution.py:111
  28.7 0.8 %copy.24 = bf16[2,8,16,1024]{3,2,0,1:T(8,128)(2,1)} copy(bf16[2,8,16,1024]{3,2,1,0:T(8,128)(2,1)S(1)} %bitcast.42) | data formatting | bytes 1048576 | tf_op jit(solution)/shard_map/reshape | solution.py:111
  29.5 4.2 %all-to-all-start = ((bf16[2,8,16,1024]{3,2,0,1:T(8,128)(2,1)}), bf16[2,8,16,1024]{3,2,0,1:T(8,128)(2,1)S(1)}, u32[]{:S(2)}, u32[]{:S(2)}) async-start(bf16[2,8,16,1024]{3,2,0,1:T(8,128)(2,1)} %copy.24), calls=%async_computation | async-start | bytes 1048576 | tf_op jit(solution)/shard_map/all_to_all | solution.py:112
  33.8 0.6 gather_fusion
  34.4 0.1 broadcast_select_fusion.2
  34.5 0.1 copy.27
  34.6 0.1 copy.28
  34.7 0.1 broadcast_multiply_fusion.1
  34.9 0.1 pad_multiply_fusion
  35.0 0.1 copy.25
  35.1 0.1 copy.26
  35.2 0.1 slice_add_fusion.1
  35.3 0.1 broadcast_compare_fusion
  35.3 11.1 %all-to-all-done = bf16[2,8,16,1024]{3,2,0,1:T(8,128)(2,1)S(1)} async-done(((bf16[2,8,16,1024]{3,2,0,1:T(8,128)(2,1)}), bf16[2,8,16,1024]{3,2,0,1:T(8,128)(2,1)S(1)}, u32[]{:S(2)}, u32[]{:S(2)}) %all-to-all-start) | async-done | bytes 524320 | tf_op jit(solution)/shard_map/all_to_all | solution.py:112
  46.5 0.2 multiply_add_fusion
  46.7 0.1 copy.29
  46.8 1.0 %copy-done.2 = bf16[512,1024]{1,0:T(8,128)(2,1)} copy-done((bf16[512,1024]{1,0:T(8,128)(2,1)}, bf16[512,1024]{1,0:T(8,128)(2,1)S(1)}, u32[]{:S(2)}) %copy-start.2) | copy-done | bytes 1048600
  47.8 1.2 %copy-done.1 = bf16[512,1024]{1,0:T(8,128)(2,1)S(1)} copy-done((bf16[512,1024]{1,0:T(8,128)(2,1)S(1)}, bf16[512,1024]{1,0:T(8,128)(2,1)}, u32[]{:S(2)}) %copy-start.1) | copy-done | bytes 1048600
  49.0 1.2 %copy-done.3 = bf16[512,1024]{1,0:T(8,128)(2,1)S(1)} copy-done((bf16[512,1024]{1,0:T(8,128)(2,1)S(1)}, bf16[512,1024]{1,0:T(8,128)(2,1)}, u32[]{:S(2)}) %copy-start.3) | copy-done | bytes 1048600
  50.3 16.3 %shard_map.101 = (bf16[4,256,512]{2,1,0:T(8,128)(2,1)S(1)}, bf16[4,256,512]{2,1,0:T(8,128)(2,1)}) custom-call(s32[1]{0:T(128)} %bitcast.side_ref, f32[256,1024]{1,0:T(8,128)S(1)} %bitcast.37, bf16[4,256,128]{2,1,0:T(8,128)(2,1)S(1)} %fusion.7.hot_ref, f32[3,1024]{1,0:T(4,128)S(1)} %pad_maximum_fusion.4.vec_ref, bf16[512,1024]{1,0:T(8,128)(2,1)S(1)} %copy-done.1, ...), custom_call_target="tpu_custom_call" | custom-call | flops 8589934592 | bytes 16777216 | tf_op jit(solution)/shard_map/pallas_call | solution.py:207
  66.6 2.9 %collective-permute-done.8 = bf16[4,256,512]{2,1,0:T(8,128)(2,1)S(1)} collective-permute-done((bf16[4,256,512]{2,1,0:T(8,128)(2,1)}, bf16[4,256,512]{2,1,0:T(8,128)(2,1)S(1)}, u32[]{:S(2)}, u32[]{:S(2)}) %collective-permute-start.8) | collective-permute-done | bytes 1048608 | tf_op jit(solution)/shard_map/ppermute | solution.py:67
  69.5 0.3 broadcast_select_fusion.1
  69.7 0.9 %copy.37 = bf16[4,2,8,16,512]{4,0,3,2,1:T(4,128)(2,1)S(1)} copy(bf16[4,2,8,16,512]{4,3,2,1,0:T(8,128)(2,1)S(1)} %bitcast.39) | data formatting | bytes 2097152 | tf_op jit(solution)/shard_map/jit(_where)/select_n | solution.py:155
  70.6 0.9 %copy.38 = bf16[4,2,8,16,512]{4,0,3,2,1:T(4,128)(2,1)S(1)} copy(bf16[4,2,8,16,512]{4,3,2,1,0:T(8,128)(2,1)S(1)} %bitcast.38) | data formatting | bytes 2097152 | tf_op jit(solution)/shard_map/jit(_where)/select_n | solution.py:154
  71.5 2.7 %pad_maximum_fusion = bf16[4,8,16,4,512]{4,3,2,1,0:T(4,128)(2,1)} fusion(bf16[2,8,16,4,512]{4,3,2,1,0:T(4,128)(2,1)S(1)} %bitcast.40, bf16[2,8,16,4,512]{4,3,2,1,0:T(4,128)(2,1)S(1)} %bitcast.41), kind=kLoop, calls=%fused_computation.5 | loop fusion | flops 1048576 | bytes 4194304 | tf_op jit(solution)/shard_map/concatenate | solution.py:156
  (36 shorter events, 0.3 us)
Async XLA Ops:
  0.0 7.3 %copy-start = (bf16[4,128,1024]{2,1,0:T(8,128)(2,1)S(1)}, bf16[4,128,1024]{2,1,0:T(8,128)(2,1)}, u32[]{:S(2)}) copy-start(bf16[4,128,1024]{2,1,0:T(8,128)(2,1)} %param.10) | copy-start | bytes 3145732
  0.0 6.3 %collective-permute-start = (bf16[1024,512]{1,0:T(8,128)(2,1)}, bf16[1024,512]{1,0:T(8,128)(2,1)S(1)}, u32[]{:S(2)}, u32[]{:S(2)}) collective-permute-start(bf16[1024,512]{1,0:T(8,128)(2,1)} %ip_a.1), channel_id=1, source_target_pairs={{0,1},{1,0},{2,3},{3,2},{4,5},{5,4},{6,7},{7,6},{8,9},{9,8},{10,11... | collective-permute-start | bytes 3145736 | tf_op jit(solution)/shard_map/ppermute | solution.py:67
  0.5 46.3 %collective-permute-start.4 = (bf16[512,1024]{1,0:T(8,128)(2,1)}, bf16[512,1024]{1,0:T(8,128)(2,1)S(1)}, u32[]{:S(2)}, u32[]{:S(2)}) collective-permute-start(bf16[512,1024]{1,0:T(8,128)(2,1)} %r_a.1), channel_id=1, source_target_pairs={{0,1},{1,0},{2,3},{3,2},{4,5},{5,4},{6,7},{7,6},{8,9},{9,8},{10,11... | collective-permute-start | bytes 3145736 | tf_op jit(solution)/shard_map/ppermute | solution.py:67
  0.6 47.2 %collective-permute-start.5 = (bf16[1024,512]{1,0:T(8,128)(2,1)}, bf16[1024,512]{1,0:T(8,128)(2,1)}, u32[]{:S(2)}, u32[]{:S(2)}) collective-permute-start(bf16[1024,512]{1,0:T(8,128)(2,1)} %wh_a.1), channel_id=1, source_target_pairs={{0,1},{1,0},{2,3},{3,2},{4,5},{5,4},{6,7},{7,6},{8,9},{9,8},{10,11... | collective-permute-start | bytes 3145736 | tf_op jit(solution)/shard_map/ppermute | solution.py:67
  1.0 46.8 %collective-permute-start.7 = (bf16[512,1024]{1,0:T(8,128)(2,1)}, bf16[512,1024]{1,0:T(8,128)(2,1)}, u32[]{:S(2)}, u32[]{:S(2)}) collective-permute-start(bf16[512,1024]{1,0:T(8,128)(2,1)} %wo_a.1), channel_id=1, source_target_pairs={{0,1},{1,0},{2,3},{3,2},{4,5},{5,4},{6,7},{7,6},{8,9},{9,8},{10,11... | collective-permute-start | bytes 3145736 | tf_op jit(solution)/shard_map/ppermute | solution.py:67
  1.1 26.3 %collective-permute-start.6 = (bf16[18,512]{1,0:T(8,128)(2,1)}, bf16[18,512]{1,0:T(8,128)(2,1)S(1)}, u32[]{:S(2)}, u32[]{:S(2)}) collective-permute-start(bf16[18,512]{1,0:T(8,128)(2,1)} %param.18), channel_id=1, source_target_pairs={{0,1},{1,0},{2,3},{3,2},{4,5},{5,4},{6,7},{7,6},{8,9},{9,8},{10,11... | collective-permute-start | bytes 55304 | tf_op jit(solution)/shard_map/ppermute | solution.py:67
  6.3 1.0 %copy-start.5 = (bf16[1024,512]{1,0:T(8,128)(2,1)}, bf16[1024,512]{1,0:T(8,128)(2,1)S(1)}, u32[]{:S(2)}) copy-start(bf16[1024,512]{1,0:T(8,128)(2,1)S(1)} %collective-permute-done.ip_b) | copy-start | bytes 3145732
  10.2 17.2 %copy-start.4 = (bf16[18,512]{1,0:T(8,128)(2,1)S(1)}, bf16[18,512]{1,0:T(8,128)(2,1)}, u32[]{:S(2)}) copy-start(bf16[18,512]{1,0:T(8,128)(2,1)} %param.18) | copy-start | bytes 55300
  14.3 7.3 %collective-permute-start.1 = (f32[1,2,1152]{2,1,0:T(2,128)S(1)}, f32[1,2,1152]{2,1,0:T(2,128)S(1)}, u32[]{:S(2)}, u32[]{:S(2)}) collective-permute-start(f32[1,2,1152]{2,1,0:T(2,128)S(1)} %maximum_bitcast_fusion.4), channel_id=1, source_target_pairs={{0,2},{2,4},{4,6},{6,8},{8,10},{10,12},{12,14},{14,0},{1,3},{3,5},... | collective-permute-start | bytes 27656 | tf_op jit(solution)/shard_map/ppermute | solution.py:43
  21.6 5.7 %collective-permute-start.2 = (f32[2,2,1152]{2,1,0:T(2,128)S(1)}, f32[2,2,1152]{2,1,0:T(2,128)S(1)}, u32[]{:S(2)}, u32[]{:S(2)}) collective-permute-start(f32[2,2,1152]{2,1,0:T(2,128)S(1)} %pad_maximum_fusion.3), channel_id=1, source_target_pairs={{0,4},{2,6},{4,8},{6,10},{8,12},{10,14},{12,0},{14,2},{1,5},{3,7},... | collective-permute-start | bytes 55304 | tf_op jit(solution)/shard_map/ppermute | solution.py:43
  27.3 6.4 %collective-permute-start.3 = (f32[4,2,1152]{2,1,0:T(2,128)S(1)}, f32[4,2,1152]{2,1,0:T(2,128)S(1)}, u32[]{:S(2)}, u32[]{:S(2)}) collective-permute-start(f32[4,2,1152]{2,1,0:T(2,128)S(1)} %pad_maximum_fusion.2), channel_id=1, source_target_pairs={{0,8},{2,10},{4,12},{6,14},{8,0},{10,2},{12,4},{14,6},{1,9},{3,11}... | collective-permute-start | bytes 110600 | tf_op jit(solution)/shard_map/ppermute | solution.py:43
  29.5 16.9 %all-to-all-start = ((bf16[2,8,16,1024]{3,2,0,1:T(8,128)(2,1)}), bf16[2,8,16,1024]{3,2,0,1:T(8,128)(2,1)S(1)}, u32[]{:S(2)}, u32[]{:S(2)}) async-start(bf16[2,8,16,1024]{3,2,0,1:T(8,128)(2,1)} %copy.24), calls=%async_computation | async-start | bytes 1048576 | tf_op jit(solution)/shard_map/all_to_all | solution.py:112
  46.8 1.0 %copy-start.2 = (bf16[512,1024]{1,0:T(8,128)(2,1)}, bf16[512,1024]{1,0:T(8,128)(2,1)S(1)}, u32[]{:S(2)}) copy-start(bf16[512,1024]{1,0:T(8,128)(2,1)S(1)} %collective-permute-done.4.r_b) | copy-start | bytes 3145732
  47.8 1.2 %copy-start.1 = (bf16[512,1024]{1,0:T(8,128)(2,1)S(1)}, bf16[512,1024]{1,0:T(8,128)(2,1)}, u32[]{:S(2)}) copy-start(bf16[512,1024]{1,0:T(8,128)(2,1)} %r_a.1) | copy-start | bytes 3145732
  49.0 1.2 %copy-start.3 = (bf16[512,1024]{1,0:T(8,128)(2,1)S(1)}, bf16[512,1024]{1,0:T(8,128)(2,1)}, u32[]{:S(2)}) copy-start(bf16[512,1024]{1,0:T(8,128)(2,1)} %copy-done.2) | copy-start | bytes 3145732
  66.6 2.9 %collective-permute-start.8 = (bf16[4,256,512]{2,1,0:T(8,128)(2,1)}, bf16[4,256,512]{2,1,0:T(8,128)(2,1)S(1)}, u32[]{:S(2)}, u32[]{:S(2)}) collective-permute-start(bf16[4,256,512]{2,1,0:T(8,128)(2,1)} %get-tuple-element.8), channel_id=1, source_target_pairs={{0,1},{1,0},{2,3},{3,2},{4,5},{5,4},{6,7},{7,6},{8,9},{9,8},{10,11... | collective-permute-start | bytes 3145736 | tf_op jit(solution)/shard_map/ppermute | solution.py:67

commit v4 on v3

--- a/solution.py
+++ b/solution.py
@@ -33,20 +33,7 @@
     )(driven, gates)
 
 
-def gather_blocks(value, axis, mine, count):
-    if count & (count - 1):
-        return lax.all_gather(value, axis)
-    held = value[None]
-    shift = 1
-    while shift < count:
-        pairs = [(i, (i + shift) % count) for i in range(count)]
-        held = jnp.concatenate([held, lax.ppermute(held, axis, pairs)], axis=0)
-        shift *= 2
-    order = (mine - jnp.arange(count, dtype=jnp.int32)) % count
-    return jnp.take(held, order, axis=0)
-
-
-def per_device(
+def body(
     inputs,
     resets,
     actions,
@@ -96,20 +83,30 @@
     my_resets = lax.dynamic_slice_in_dim(resets, m * bh, bh, 0)
     keep = (1 - my_resets).astype(jnp.float32)
     gates = keep[:, :, None] * decays
-    local = local_scan(driven, gates)
-
+    sub = steps // ntm
+    locals_ = [local_scan(driven[b : b + 1], gates[b : b + 1])[0] for b in range(bh)]
     positions = lax.broadcasted_iota(jnp.int32, my_resets.shape, 1)
     first = jnp.min(jnp.where(my_resets != 0, positions, steps), axis=1).astype(jnp.float32)
-    payload = jnp.concatenate(
-        [local[:, -1, :], jnp.broadcast_to(first[:, None], (bh, 128))], axis=1
-    )
-    gathered = gather_blocks(payload, "tm", d, ntm)
-    ends = gathered[:, :, :width]
-    firsts = gathered[:, :, width]
-
-    sub = steps // ntm
-    send = local.astype(jnp.bfloat16).reshape(bh, ntm, sub, width)
-    recv = lax.all_to_all(send, "tm", split_axis=1, concat_axis=1, tiled=True)
+    ends_local = jnp.stack([loc[-1, :] for loc in locals_], axis=0)
+    ends_hi = ends_local.astype(jnp.bfloat16)
+    ends_lo = (ends_local - ends_hi.astype(jnp.float32)).astype(jnp.bfloat16)
+    first_rows = jnp.broadcast_to(first[:, None], (bh, width)).astype(jnp.bfloat16)
+    extra = jnp.concatenate([ends_hi, ends_lo, first_rows], axis=0)
+    pad_rows = -(-extra.shape[0] // 16) * 16
+    extra = jnp.pad(extra, ((0, pad_rows - extra.shape[0]), (0, 0)))
+    recvs = []
+    for b in range(bh):
+        send = locals_[b].astype(jnp.bfloat16).reshape(ntm, sub, width)
+        if b == 0:
+            send = jnp.concatenate(
+                [send, jnp.broadcast_to(extra[None], (ntm,) + extra.shape)], axis=1
+            )
+        recvs.append(lax.all_to_all(send, "tm", split_axis=0, concat_axis=0, tiled=True))
+    got_extra = recvs[0][:, sub:]
+    recvs[0] = recvs[0][:, :sub]
+    ends = got_extra[:, :bh].astype(jnp.float32) + got_extra[:, bh : 2 * bh].astype(jnp.float32)
+    firsts = got_extra[:, 2 * bh : 3 * bh, 0].astype(jnp.float32)
+    gathered = ends
 
     nblocks = gathered.shape[0]
     whole_block = decays ** steps
@@ -126,31 +123,36 @@
 
     t_glob = d * sub + lax.broadcasted_iota(jnp.int32, (sub,), 0)
     powers = decays[None, :] ** (t_glob[:, None] + 1).astype(jnp.float32)
-    alive = t_glob[None, None, :].astype(jnp.float32) < jnp.swapaxes(firsts, 0, 1)[:, :, None]
-    cum = jnp.where(alive[..., None], powers[None, None], 0.0)
-    posterior = recv.astype(jnp.float32) + cum * jnp.swapaxes(carry, 0, 1)[:, :, None, :]
 
     _, blocks, _, horizon = actions.shape
-    rows = bh * blocks * sub
-    current = posterior.reshape(rows, width)
-    my_actions = lax.dynamic_slice_in_dim(actions, m * bh, bh, 0).reshape(rows, horizon)
+    rows = blocks * sub
+    my_actions = lax.dynamic_slice_in_dim(actions, m * bh, bh, 0)
     table = jnp.concatenate([action_embed, emb_o], axis=1)
     table = jnp.pad(table, ((0, 128 - table.shape[0]), (0, 0)))
-    one_hot = (
-        jnp.swapaxes(my_actions, 0, 1)[:, :, None] == jnp.arange(128, dtype=jnp.int32)
-    ).astype(jnp.bfloat16)
     vecs = jnp.stack([decays, scaling, norm_gain], axis=0)
     side = jnp.reshape(m, (1,)).astype(jnp.int32)
-    keep_part, give_part = imagine(
-        side, current, one_hot, vecs, readout_w, r_o, w_hidden, wh_o, table, w_out, wo_o,
-        in_proj, ip_o,
-    )
-    got = partner(give_part)
 
     def arrange(part):
-        return jnp.transpose(part.reshape(horizon, bh, blocks, sub, half), (1, 2, 3, 0, 4))
-
-    mine, theirs = arrange(keep_part), arrange(got)
+        return jnp.transpose(part.reshape(horizon, blocks, sub, half), (1, 2, 0, 3))
+
+    mine, theirs = [], []
+    for b in range(bh):
+        alive = t_glob[None, :].astype(jnp.float32) < firsts[:, b][:, None]
+        cum = jnp.where(alive[..., None], powers[None], 0.0)
+        posterior = recvs[b].astype(jnp.float32) + cum * carry[:, b][:, None, :]
+        current = posterior.reshape(rows, width)
+        one_hot = (
+            jnp.swapaxes(my_actions[b].reshape(rows, horizon), 0, 1)[:, :, None]
+            == jnp.arange(128, dtype=jnp.int32)
+        ).astype(jnp.bfloat16)
+        keep_part, give_part = imagine(
+            side, current, one_hot, vecs, readout_w, r_o, w_hidden, wh_o, table, w_out, wo_o,
+            in_proj, ip_o,
+        )
+        mine.append(arrange(keep_part))
+        theirs.append(arrange(partner(give_part)))
+    mine = jnp.stack(mine, axis=0)
+    theirs = jnp.stack(theirs, axis=0)
     first_half = jnp.where(m == 0, mine, theirs)
     second_half = jnp.where(m == 0, theirs, mine)
     return jnp.concatenate([first_half, second_half], axis=0)
@@ -230,6 +232,4 @@
         P("mp", None),
     )
     out_specs = P("rep", None, "tm", None, "mp")
-    return jax.shard_map(
-        per_device, mesh=mesh, in_specs=in_specs, out_specs=out_specs, check_vma=False
-    )
+    return jax.shard_map(body, mesh=mesh, in_specs=in_specs, out_specs=out_specs, check_vma=False)

time: 74.8 us -> 84.3 us (1.13)
  other arithmetic: 7.91 us -> 15.9 us
  waiting for transfers between devices: 24.3 us -> 16.8 us
  Pallas kernels: 19.5 us -> 24.9 us
  starting transfers between devices: 8.4 us -> 12.7 us
  matrix products: 2.91 us -> 1.96 us
    ppermute x3 -> x0, waiting for transfers between devices: 10.3 us -> none  [gather_blocks(): held = jnp.concatenate([held, lax.ppermute(held, axis, pairs)], axis=0)]
    all_to_all x1 -> x2, starting transfers between devices: 4.17 us -> 10.7 us  [body(): lax.all_to_all(send, 'tm', split_axis=0, concat_axis=0, tiled=True)]
    all_to_all x1 -> x2, waiting for transfers between devices: 11.1 us -> 16.8 us  [body(): lax.all_to_all(send, 'tm', split_axis=0, concat_axis=0, tiled=True)]
    pallas_call x1 -> x2, Pallas kernels: 16.3 us -> 20 us  [imagine(): pl.pallas_call(_imagine_kernel, out_shape=(out, out), in_specs=[pl.BlockS...]
    slice x7 -> x14, local copies, waits for them, and re-layouts: 0.97 us -> 4.56 us  [the longest x2 1.6 us: body(): ends_local = jnp.stack([loc[-1, :] for loc in locals_], axis=0)]
    unnamed x13 -> x21, local copies, waits for them, and re-layouts: 4.42 us -> 1.27 us
    ppermute x6 -> x7, waiting for transfers between devices: 2.88 us -> 0.02 us  [partner(): return lax.ppermute(x, 'mp', swap)]
    ppermute x3 -> x0, starting transfers between devices: 2.71 us -> none  [gather_blocks(): held = jnp.concatenate([held, lax.ppermute(held, axis, pairs)], axis=0)]
  transfers between devices with their start and end apart: 10 -> 9, of which waited for: 4 -> 2; matrix products, arithmetic and copies ran while one was open for 17% -> 27% of each run, Pallas kernels for 4% -> 18%
where the time goes in v4:
time: 84.3 us; the launch traced here: 83.4 us
  Pallas kernels  24.9 us (30%)
  waiting for transfers between devices  16.8 us (20%)
  other arithmetic  15.9 us (19%)
  starting transfers between devices  12.7 us (15%)
  local copies, waits for them, and re-layouts  10.9 us (13%)
  matrix products  1.96 us (2%)
    pallas_call x2, Pallas kernels, imagine(): pl.pallas_call(_imagine_kernel, out_shape=(out, out), in_specs=[pl.BlockS...  20 us
    all_to_all x2, waiting for transfers between devices, body(): lax.all_to_all(send, 'tm', split_axis=0, concat_axis=0, tiled=True)  16.8 us
    all_to_all x2, starting transfers between devices, body(): lax.all_to_all(send, 'tm', split_axis=0, concat_axis=0, tiled=True)  10.7 us
    pallas_call x2, Pallas kernels, local_scan(): pl.pallas_call(_scan_kernel, out_shape=jax.ShapeDtypeStruct(driven.shape,...  4.85 us
    reshape x4, local copies, waits for them, and re-layouts, arrange(): return jnp.transpose(part.reshape(horizon, blocks, sub, half), (1, 2, 0, 3))  2.91 us
    concatenate x1, other arithmetic, body(): return jnp.concatenate([first_half, second_half], axis=0)  2.67 us
    ppermute x7, starting transfers between devices, partner(): return lax.ppermute(x, 'mp', swap)  2.03 us
    dot_general x1, matrix products, body(): jnp.dot(x.reshape(bh * steps, feat), ip, preferred_element_type=jnp.float32)  1.96 us
  transfers between devices with their start and end apart: 9, of which 2 were waited for; matrix products, arithmetic and copies ran while one was open for 27% of the time, Pallas kernels for 18%

profile of v4, /device:TPU:0, one launch (start us, length us, event | category | flops | bytes accessed | tf_op | source)
XLA Modules:
  0.0 83.4 jit_solution(2185218313822989640)
XLA Ops:
  0.0 0.5 collective-permute-start
  0.6 0.4 collective-permute-start.2
  1.1 0.4 collective-permute-start.3
  1.5 0.8 fusion.13
  2.4 0.9 %fusion.20 = (f32[512]{0:T(512)S(1)}, f32[512]{0:T(512)S(1)}) fusion(f32[1024]{0:T(1024)} %param.14, s32[]{:T(128)S(6)} %select_n.41, s32[]{:T(128)S(6)} %select_n.42), kind=kLoop, calls=%fused_computation.74 | loop fusion | bytes 8200 | tf_op jit(solution)/shard_map/dynamic_slice | solution.py:66
  3.3 0.6 multiply_multiply_fusion
  3.9 0.7 pad_maximum_fusion.4.vec_ref
  4.6 0.7 constant_dynamic-slice_fusion
  5.4 0.1 broadcast_multiply_fusion
  5.5 1.1 %fusion.18 = (f32[1,128,1024]{2,1,0:T(8,128)}, f32[1,128,1024]{2,1,0:T(8,128)}) fusion(f32[2,128,1024]{2,1,0:T(8,128)S(1)} %broadcast_multiply_fusion), kind=kLoop, calls=%fused_computation.72 | loop fusion | bytes 2097152 | tf_op jit(solution)/shard_map/slice | solution.py:87
  6.6 2.0 %fusion.3 = f32[2,128,1024]{2,1,0:T(8,128)S(1)} fusion(bf16[1024,512]{1,0:T(8,128)(2,1)} %collective-permute-done.ip_b, bf16[1024,512]{1,0:T(8,128)(2,1)S(1)} %copy-done.9, f32[1024]{0:T(1024)S(1)} %get-tuple-element.32, bf16[4,128,1024]{2,1,0:T(8,128)(2,1)S(1)} %copy-done, s32[]{:T(128)S(6)} %select_n.40), kind=kOutput, calls=%fused_computation.5 | convolution fusion | flops 541327360 | bytes 3674116 | tf_op jit(solution)/shard_map/dot_general | solution.py:78
  8.6 1.1 %fusion.19 = (f32[1,128,1024]{2,1,0:T(8,128)}, f32[1,128,1024]{2,1,0:T(8,128)}) fusion(f32[2,128,1024]{2,1,0:T(8,128)S(1)} %fusion.3), kind=kLoop, calls=%fused_computation.73 | loop fusion | bytes 2097152 | tf_op jit(solution)/shard_map/slice | solution.py:87
  9.6 2.4 %shard_map.100 = f32[1,128,1024]{2,1,0:T(8,128)} custom-call(f32[1,128,1024]{2,1,0:T(8,128)} %get-tuple-element.19.x_ref, f32[1,128,1024]{2,1,0:T(8,128)} %get-tuple-element.17.g_ref), custom_call_target="tpu_custom_call" | custom-call | flops 262144 | bytes 1572864 | tf_op jit(solution)/shard_map/pallas_call | solution.py:27
  12.1 0.8 slice_bitcast_fusion.1
  12.8 2.4 %shard_map.101 = f32[1,128,1024]{2,1,0:T(8,128)} custom-call(f32[1,128,1024]{2,1,0:T(8,128)} %get-tuple-element.20.x_ref, f32[1,128,1024]{2,1,0:T(8,128)} %get-tuple-element.18.g_ref), custom_call_target="tpu_custom_call" | custom-call | flops 262144 | bytes 1572864 | tf_op jit(solution)/shard_map/pallas_call | solution.py:27
  15.2 0.8 %slice_bitcast_fusion = f32[1,1024]{1,0:T(1,128)S(1)} fusion(f32[1,128,1024]{2,1,0:T(8,128)} %shard_map.101), kind=kLoop, calls=%fused_computation.46 | loop fusion | bytes 8192 | tf_op jit(solution)/shard_map/slice | solution.py:90
  16.1 1.1 %convert_element_type.86 = bf16[1,128,1024]{2,1,0:T(8,128)(2,1)S(1)} convert(f32[1,128,1024]{2,1,0:T(8,128)} %shard_map.100) | non-fusion elementwise | flops 131072 | bytes 786432 | tf_op jit(solution)/shard_map/convert_element_type | solution.py:99
  17.3 0.9 %pad_maximum_fusion.3 = bf16[8,32,1024]{2,1,0:T(8,128)(2,1)} fusion(bf16[8,16,1024]{2,1,0:T(8,128)(2,1)S(1)} %broadcast_in_dim.47, bf16[8,16,1024]{2,1,0:T(8,128)(2,1)S(1)} %bitcast.69), kind=kLoop, calls=%fused_computation.13 | loop fusion | flops 1048576 | bytes 1048576 | tf_op jit(solution)/shard_map/concatenate | solution.py:101
  18.2 7.0 %all-to-all-start = ((bf16[8,32,1024]{2,1,0:T(8,128)(2,1)}), bf16[8,32,1024]{2,1,0:T(8,128)(2,1)}, u32[]{:S(2)}, u32[]{:S(2)}) async-start(bf16[8,32,1024]{2,1,0:T(8,128)(2,1)} %pad_maximum_fusion.3), calls=%async_computation | async-start | bytes 1048576 | tf_op jit(solution)/shard_map/all_to_all | solution.py:104
  25.2 0.1 reshape_squeeze.6
  25.3 0.1 reshape_squeeze.7
  25.4 0.8 broadcast_power_fusion
  26.1 0.1 fusion.8.hot_ref
  26.3 0.1 fusion.9.hot_ref
  26.4 0.6 fusion.15
  27.1 0.7 convert_element_type.102
  27.8 12.6 %all-to-all-done = bf16[8,32,1024]{2,1,0:T(8,128)(2,1)} async-done(((bf16[8,32,1024]{2,1,0:T(8,128)(2,1)}), bf16[8,32,1024]{2,1,0:T(8,128)(2,1)}, u32[]{:S(2)}, u32[]{:S(2)}) %all-to-all-start) | async-done | bytes 524320 | tf_op jit(solution)/shard_map/all_to_all | solution.py:104
  40.4 3.6 %all-to-all-start.1 = ((bf16[8,16,1024]{2,1,0:T(8,128)(2,1)}), bf16[8,16,1024]{2,1,0:T(8,128)(2,1)S(1)}, u32[]{:S(2)}, u32[]{:S(2)}) async-start(bf16[8,16,1024]{2,1,0:T(8,128)(2,1)} %bitcast.16), calls=%async_computation.1 | async-start | bytes 524288 | tf_op jit(solution)/shard_map/all_to_all | solution.py:104
  44.0 0.7 slice_convert_fusion
  44.8 0.1 copy.30
  44.8 1.0 %convert_add_fusion = f32[8,2,1024]{2,1,0:T(2,128)S(1)} fusion(bf16[8,32,1024]{2,1,0:T(8,128)(2,1)} %all-to-all-done), kind=kLoop, calls=%fused_computation.29 | loop fusion | flops 49152 | bytes 131072 | tf_op jit(solution)/shard_map/add | solution.py:107
  45.9 0.7 compare_select_fusion
  46.6 0.1 copy.31
  46.7 0.1 copy.32
  46.8 1.1 %broadcast_multiply_fusion.1 = (f32[8,2,1024]{2,1,0:T(2,128)S(1)}, f32[8,2,1024]{2,1,0:T(2,128)S(1)}) fusion(f32[1024]{0:T(1024)S(1)} %copy-done.6, f32[8,2]{1,0:T(8,128)S(1)} %copy.32, bf16[8,32,1024]{2,1,0:T(8,128)(2,1)} %all-to-all-done, f32[7,2,1024]{2,1,0:T(2,128)S(1)} %slice.118), kind=kLoop, calls=%fused_computation.38 | loop fusion | flops 98304 | bytes 258112 | tf_op jit(solution)/shard_map/mul | solution.py:113
  47.9 0.8 pad_multiply_fusion
  49.0 4.2 %all-to-all-done.1 = bf16[8,16,1024]{2,1,0:T(8,128)(2,1)S(1)} async-done(((bf16[8,16,1024]{2,1,0:T(8,128)(2,1)}), bf16[8,16,1024]{2,1,0:T(8,128)(2,1)S(1)}, u32[]{:S(2)}, u32[]{:S(2)}) %all-to-all-start.1) | async-done | bytes 262176 | tf_op jit(solution)/shard_map/all_to_all | solution.py:104
  53.2 1.2 %multiply_add_fusion.1 = (f32[8,16,1024]{2,1,0:T(8,128)S(1)}, f32[8,16,1024]{2,1,0:T(8,128)S(1)}) fusion(bf16[8,32,1024]{2,1,0:T(8,128)(2,1)} %all-to-all-done, f32[8,1024]{1,0:T(8,128)S(1)} %get-tuple-element.43, f32[16,1024]{1,0:T(8,128)S(1)} %copy-done.5, pred[8,16]{1,0:T(8,128)(4,1)S(1)} %get-tuple-element.40, f32[8,1024]{1,0:T(8,128)S(1)} %get-tuple-element.42, ...), kind=kLoop, calls=%fused_computation.19 | loop fusion | flops 1048576 | bytes 1704192 | tf_op jit(solution)/shard_map/add | solution.py:142
  54.4 1.2 %copy-done.2 = bf16[1024,512]{1,0:T(8,128)(2,1)S(1)} copy-done((bf16[1024,512]{1,0:T(8,128)(2,1)S(1)}, bf16[1024,512]{1,0:T(8,128)(2,1)}, u32[]{:S(2)}) %copy-start.2) | copy-done | bytes 1048600
  55.6 10.0 %shard_map.102 = (bf16[4,128,512]{2,1,0:T(8,128)(2,1)S(1)}, bf16[4,128,512]{2,1,0:T(8,128)(2,1)}) custom-call(s32[1]{0:T(128)} %bitcast.side_ref, f32[128,1024]{1,0:T(8,128)S(1)} %bitcast.64, bf16[4,128,128]{2,1,0:T(8,128)(2,1)S(1)} %fusion.8.hot_ref, f32[3,1024]{1,0:T(4,128)S(1)} %pad_maximum_fusion.4.vec_ref, bf16[512,1024]{1,0:T(8,128)(2,1)S(1)} %copy-done.1, ...), custom_call_target="tpu_custom_call" | custom-call | flops 4294967296 | bytes 16777216 | tf_op jit(solution)/shard_map/pallas_call | solution.py:209
  65.6 10.0 %shard_map.103 = (bf16[4,128,512]{2,1,0:T(8,128)(2,1)S(1)}, bf16[4,128,512]{2,1,0:T(8,128)(2,1)}) custom-call(s32[1]{0:T(128)} %bitcast.side_ref, f32[128,1024]{1,0:T(8,128)S(1)} %bitcast.63, bf16[4,128,128]{2,1,0:T(8,128)(2,1)S(1)} %fusion.9.hot_ref, f32[3,1024]{1,0:T(4,128)S(1)} %pad_maximum_fusion.4.vec_ref, bf16[512,1024]{1,0:T(8,128)(2,1)S(1)} %copy-done.1, ...), custom_call_target="tpu_custom_call" | custom-call | flops 4294967296 | bytes 16777216 | tf_op jit(solution)/shard_map/pallas_call | solution.py:209
  75.6 0.5 collective-permute-start.6
  76.1 0.4 copy.50
  76.5 0.4 copy.49
  77.0 1.7 %copy.48 = bf16[4,8,16,512]{3,0,2,1:T(4,128)(2,1)S(1)} copy(bf16[4,8,16,512]{3,2,1,0:T(8,128)(2,1)} %bitcast.23) | data formatting | bytes 1048576 | tf_op jit(solution)/shard_map/reshape | solution.py:136
  78.7 0.4 copy.47
  79.1 1.6 %broadcast_select_fusion.1 = (bf16[2,8,16,4,512]{4,3,2,1,0:T(4,128)(2,1)S(1)}, bf16[2,8,16,4,512]{4,3,2,1,0:T(4,128)(2,1)S(1)}) fusion(pred[]{:T(512)S(6)} %eq.14, bf16[1,8,16,4,512]{4,3,2,1,0:T(4,128)(2,1)S(1)} %bitcast.68, bf16[1,8,16,4,512]{4,3,2,1,0:T(4,128)(2,1)S(1)} %bitcast.67, bf16[1,8,16,4,512]{4,3,2,1,0:T(4,128)(2,1)S(1)} %bitcast.66, ...), kind=kLoop, calls=%fused_computation.9 | loop fusion | flops 2097152 | bytes 4194305 | tf_op jit(solution)/shard_map/jit(_where)/select_n | solution.py:156
  80.7 2.7 %pad_maximum_fusion = bf16[4,8,16,4,512]{4,3,2,1,0:T(4,128)(2,1)} fusion(bf16[2,8,16,4,512]{4,3,2,1,0:T(4,128)(2,1)S(1)} %get-tuple-element.16, bf16[2,8,16,4,512]{4,3,2,1,0:T(4,128)(2,1)S(1)} %get-tuple-element.15), kind=kLoop, calls=%fused_computation.4 | loop fusion | flops 1048576 | bytes 4194304 | tf_op jit(solution)/shard_map/concatenate | solution.py:158
  (51 shorter events, 0.7 us)
Async XLA Ops:
  0.0 6.6 %copy-start = (bf16[4,128,1024]{2,1,0:T(8,128)(2,1)S(1)}, bf16[4,128,1024]{2,1,0:T(8,128)(2,1)}, u32[]{:S(2)}) copy-start(bf16[4,128,1024]{2,1,0:T(8,128)(2,1)} %param.10) | copy-start | bytes 3145732
  0.0 6.6 %collective-permute-start = (bf16[1024,512]{1,0:T(8,128)(2,1)}, bf16[1024,512]{1,0:T(8,128)(2,1)}, u32[]{:S(2)}, u32[]{:S(2)}) collective-permute-start(bf16[1024,512]{1,0:T(8,128)(2,1)} %ip_a.3), channel_id=1, source_target_pairs={{0,1},{1,0},{2,3},{3,2},{4,5},{5,4},{6,7},{7,6},{8,9},{9,8},{10,11... | collective-permute-start | bytes 3145736 | tf_op jit(solution)/shard_map/ppermute | solution.py:54
  0.5 53.8 %collective-permute-start.1 = (bf16[512,1024]{1,0:T(8,128)(2,1)}, bf16[512,1024]{1,0:T(8,128)(2,1)}, u32[]{:S(2)}, u32[]{:S(2)}) collective-permute-start(bf16[512,1024]{1,0:T(8,128)(2,1)} %r_a.3), channel_id=1, source_target_pairs={{0,1},{1,0},{2,3},{3,2},{4,5},{5,4},{6,7},{7,6},{8,9},{9,8},{10,11... | collective-permute-start | bytes 3145736 | tf_op jit(solution)/shard_map/ppermute | solution.py:54
  0.6 53.8 %collective-permute-start.2 = (bf16[1024,512]{1,0:T(8,128)(2,1)}, bf16[1024,512]{1,0:T(8,128)(2,1)}, u32[]{:S(2)}, u32[]{:S(2)}) collective-permute-start(bf16[1024,512]{1,0:T(8,128)(2,1)} %wh_a.3), channel_id=1, source_target_pairs={{0,1},{1,0},{2,3},{3,2},{4,5},{5,4},{6,7},{7,6},{8,9},{9,8},{10,11... | collective-permute-start | bytes 3145736 | tf_op jit(solution)/shard_map/ppermute | solution.py:54
  1.0 53.3 %collective-permute-start.4 = (bf16[512,1024]{1,0:T(8,128)(2,1)}, bf16[512,1024]{1,0:T(8,128)(2,1)}, u32[]{:S(2)}, u32[]{:S(2)}) collective-permute-start(bf16[512,1024]{1,0:T(8,128)(2,1)} %wo_a.3), channel_id=1, source_target_pairs={{0,1},{1,0},{2,3},{3,2},{4,5},{5,4},{6,7},{7,6},{8,9},{9,8},{10,11... | collective-permute-start | bytes 3145736 | tf_op jit(solution)/shard_map/ppermute | solution.py:54
  1.1 25.9 %collective-permute-start.3 = (bf16[18,512]{1,0:T(8,128)(2,1)}, bf16[18,512]{1,0:T(8,128)(2,1)S(1)}, u32[]{:S(2)}, u32[]{:S(2)}) collective-permute-start(bf16[18,512]{1,0:T(8,128)(2,1)} %param.18), channel_id=1, source_target_pairs={{0,1},{1,0},{2,3},{3,2},{4,5},{5,4},{6,7},{7,6},{8,9},{9,8},{10,11... | collective-permute-start | bytes 55304 | tf_op jit(solution)/shard_map/ppermute | solution.py:54
  2.4 4.2 %copy-start.9 = (bf16[1024,512]{1,0:T(8,128)(2,1)S(1)}, bf16[1024,512]{1,0:T(8,128)(2,1)}, u32[]{:S(2)}) copy-start(bf16[1024,512]{1,0:T(8,128)(2,1)} %ip_a.3) | copy-start | bytes 3145732
  15.2 11.8 %copy-start.7 = (bf16[18,512]{1,0:T(8,128)(2,1)S(1)}, bf16[18,512]{1,0:T(8,128)(2,1)}, u32[]{:S(2)}) copy-start(bf16[18,512]{1,0:T(8,128)(2,1)} %param.18) | copy-start | bytes 55300
  15.2 11.8 %copy-start.4 = (f32[1,128,1024]{2,1,0:T(8,128)S(1)}, f32[1,128,1024]{2,1,0:T(8,128)}, u32[]{:S(2)}) copy-start(f32[1,128,1024]{2,1,0:T(8,128)} %shard_map.101) | copy-start | bytes 1572868
  18.2 28.6 %copy-start.6 = (f32[1024]{0:T(1024)S(1)}, f32[1024]{0:T(1024)}, u32[]{:S(2)}) copy-start(f32[1024]{0:T(1024)} %get-tuple-element.31) | copy-start | bytes 12292
  18.2 22.2 %all-to-all-start = ((bf16[8,32,1024]{2,1,0:T(8,128)(2,1)}), bf16[8,32,1024]{2,1,0:T(8,128)(2,1)}, u32[]{:S(2)}, u32[]{:S(2)}) async-start(bf16[8,32,1024]{2,1,0:T(8,128)(2,1)} %pad_maximum_fusion.3), calls=%async_computation | async-start | bytes 1048576 | tf_op jit(solution)/shard_map/all_to_all | solution.py:104
  27.8 21.1 %copy-start.8 = (f32[16]{0:T(128)S(1)}, f32[16]{0:T(128)}, u32[]{:S(2)}) copy-start(f32[16]{0:T(128)} %fusion.15) | copy-start | bytes 196
  27.8 25.3 %copy-start.5 = (f32[16,1024]{1,0:T(8,128)S(1)}, f32[16,1024]{1,0:T(8,128)}, u32[]{:S(2)}) copy-start(f32[16,1024]{1,0:T(8,128)} %broadcast_power_fusion) | copy-start | bytes 196612
  27.8 26.5 %copy-start.1 = (bf16[512,1024]{1,0:T(8,128)(2,1)S(1)}, bf16[512,1024]{1,0:T(8,128)(2,1)}, u32[]{:S(2)}) copy-start(bf16[512,1024]{1,0:T(8,128)(2,1)} %r_a.3) | copy-start | bytes 3145732
  40.4 12.8 %all-to-all-start.1 = ((bf16[8,16,1024]{2,1,0:T(8,128)(2,1)}), bf16[8,16,1024]{2,1,0:T(8,128)(2,1)S(1)}, u32[]{:S(2)}, u32[]{:S(2)}) async-start(bf16[8,16,1024]{2,1,0:T(8,128)(2,1)} %bitcast.16), calls=%async_computation.1 | async-start | bytes 524288 | tf_op jit(solution)/shard_map/all_to_all | solution.py:104
  54.4 1.2 %copy-start.2 = (bf16[1024,512]{1,0:T(8,128)(2,1)S(1)}, bf16[1024,512]{1,0:T(8,128)(2,1)}, u32[]{:S(2)}) copy-start(bf16[1024,512]{1,0:T(8,128)(2,1)} %wh_a.3) | copy-start | bytes 3145732
  55.6 10.1 %copy-start.3 = (bf16[1024,512]{1,0:T(8,128)(2,1)S(1)}, bf16[1024,512]{1,0:T(8,128)(2,1)}, u32[]{:S(2)}) copy-start(bf16[1024,512]{1,0:T(8,128)(2,1)} %wh_a.3) | copy-start | bytes 3145732
  65.6 11.3 %collective-permute-start.5 = (bf16[4,128,512]{2,1,0:T(8,128)(2,1)}, bf16[4,128,512]{2,1,0:T(8,128)(2,1)}, u32[]{:S(2)}, u32[]{:S(2)}) collective-permute-start(bf16[4,128,512]{2,1,0:T(8,128)(2,1)} %get-tuple-element.11), channel_id=1, source_target_pairs={{0,1},{1,0},{2,3},{3,2},{4,5},{5,4},{6,7},{7,6},{8,9},{9,8},{10,11... | collective-permute-start | bytes 1572872 | tf_op jit(solution)/shard_map/ppermute | solution.py:54
  75.6 3.0 %collective-permute-start.6 = (bf16[4,128,512]{2,1,0:T(8,128)(2,1)}, bf16[4,128,512]{2,1,0:T(8,128)(2,1)S(1)}, u32[]{:S(2)}, u32[]{:S(2)}) collective-permute-start(bf16[4,128,512]{2,1,0:T(8,128)(2,1)} %get-tuple-element.12), channel_id=1, source_target_pairs={{0,1},{1,0},{2,3},{3,2},{4,5},{5,4},{6,7},{7,6},{8,9},{9,8},{10,11... | collective-permute-start | bytes 1572872 | tf_op jit(solution)/shard_map/ppermute | solution.py:54

commit v5 on v3

--- a/solution.py
+++ b/solution.py
@@ -97,19 +97,30 @@
     keep = (1 - my_resets).astype(jnp.float32)
     gates = keep[:, :, None] * decays
     local = local_scan(driven, gates)
+    sub = steps // ntm
 
     positions = lax.broadcasted_iota(jnp.int32, my_resets.shape, 1)
     first = jnp.min(jnp.where(my_resets != 0, positions, steps), axis=1).astype(jnp.float32)
-    payload = jnp.concatenate(
-        [local[:, -1, :], jnp.broadcast_to(first[:, None], (bh, 128))], axis=1
-    )
-    gathered = gather_blocks(payload, "tm", d, ntm)
-    ends = gathered[:, :, :width]
-    firsts = gathered[:, :, width]
-
-    sub = steps // ntm
-    send = local.astype(jnp.bfloat16).reshape(bh, ntm, sub, width)
-    recv = lax.all_to_all(send, "tm", split_axis=1, concat_axis=1, tiled=True)
+    ends_local = local[:, -1, :]
+    ends_hi = ends_local.astype(jnp.bfloat16)
+    ends_lo = (ends_local - ends_hi.astype(jnp.float32)).astype(jnp.bfloat16)
+    first_rows = jnp.broadcast_to(first[:, None], (bh, width)).astype(jnp.bfloat16)
+    extra = jnp.concatenate([ends_hi, ends_lo, first_rows], axis=0)
+    pad_rows = -(-(extra.shape[0] + bh * sub) // 16) * 16 - bh * sub
+    extra = jnp.pad(extra, ((0, pad_rows - extra.shape[0]), (0, 0)))
+    states = jnp.swapaxes(local.astype(jnp.bfloat16).reshape(bh, ntm, sub, width), 0, 1)
+    send = jnp.concatenate(
+        [states.reshape(ntm, bh * sub, width), jnp.broadcast_to(extra[None], (ntm,) + extra.shape)],
+        axis=1,
+    )
+    got = lax.all_to_all(send, "tm", split_axis=0, concat_axis=0, tiled=True)
+    recv = jnp.swapaxes(got[:, : bh * sub].reshape(ntm, bh, sub, width), 0, 1)
+    got_extra = got[:, bh * sub :]
+    gathered = got_extra[:, :bh].astype(jnp.float32) + got_extra[:, bh : 2 * bh].astype(
+        jnp.float32
+    )
+    ends = gathered
+    firsts = got_extra[:, 2 * bh : 3 * bh, 0].astype(jnp.float32)
 
     nblocks = gathered.shape[0]
     whole_block = decays ** steps

time: 74.8 us -> 72.7 us (0.972)
  waiting for transfers between devices: 24.3 us -> 21.5 us
  other arithmetic: 7.91 us -> 10.4 us
  local copies, waits for them, and re-layouts: 10.9 us -> 8.63 us
    ppermute x3 -> x0, waiting for transfers between devices: 10.3 us -> none  [gather_blocks(): held = jnp.concatenate([held, lax.ppermute(held, axis, pairs)], axis=0)]
    ppermute x6, waiting for transfers between devices: 2.88 us -> 6.62 us  [partner(): return lax.ppermute(x, 'mp', swap)]
    all_to_all x1, waiting for transfers between devices: 11.1 us -> 14.8 us  [per_device(): got = lax.all_to_all(send, 'tm', split_axis=0, concat_axis=0, tiled=True)]
    unnamed x13 -> x15, local copies, waits for them, and re-layouts: 4.42 us -> 1.26 us
    all_to_all x1, starting transfers between devices: 4.17 us -> 6.92 us  [per_device(): got = lax.all_to_all(send, 'tm', split_axis=0, concat_axis=0, tiled=True)]
    ppermute x3 -> x0, starting transfers between devices: 2.71 us -> none  [gather_blocks(): held = jnp.concatenate([held, lax.ppermute(held, axis, pairs)], axis=0)]
    transpose x1, local copies, waits for them, and re-layouts: 0.08 us -> 1.35 us  [per_device(): jnp.swapaxes(firsts, 0, 1)[:, :, None]]
    select_n x1, local copies, waits for them, and re-layouts: 0.09 us -> 1.35 us  [per_device(): gain = jnp.where(firsts >= steps, 1.0, 0.0)[:, :, None] * whole_block]
  transfers between devices with their start and end apart: 10 -> 7, of which waited for: 4 -> 3; matrix products, arithmetic and copies ran while one was open for 17% -> 14% of each run, Pallas kernels for 4% -> 0%
where the time goes in v5:
time: 72.7 us; the launch traced here: 72.2 us
  waiting for transfers between devices  21.5 us (30%)
  Pallas kernels  19.7 us (27%)
  other arithmetic  10.4 us (14%)
  local copies, waits for them, and re-layouts  8.63 us (12%)
  starting transfers between devices  8.5 us (12%)
  matrix products  3.28 us (5%)
    pallas_call x1, Pallas kernels, imagine(): pl.pallas_call(_imagine_kernel, out_shape=(out, out), in_specs=[pl.BlockS...  16.6 us
    all_to_all x1, waiting for transfers between devices, per_device(): got = lax.all_to_all(send, 'tm', split_axis=0, concat_axis=0, tiled=True)  14.8 us
    all_to_all x1, starting transfers between devices, per_device(): got = lax.all_to_all(send, 'tm', split_axis=0, concat_axis=0, tiled=True)  6.92 us
    ppermute x6, waiting for transfers between devices, partner(): return lax.ppermute(x, 'mp', swap)  6.62 us
    dot_general x1, matrix products, per_device(): jnp.dot(x.reshape(bh * steps, feat), ip, preferred_element_type=jnp.float32)  3.28 us
    pallas_call x1, Pallas kernels, local_scan(): pl.pallas_call(_scan_kernel, out_shape=jax.ShapeDtypeStruct(driven.shape,...  3.12 us
    concatenate x1, other arithmetic, per_device(): return jnp.concatenate([first_half, second_half], axis=0)  2.67 us
    ppermute x6, starting transfers between devices, partner(): return lax.ppermute(x, 'mp', swap)  1.58 us
  transfers between devices with their start and end apart: 7, of which 3 were waited for; matrix products, arithmetic and copies ran while one was open for 14% of the time, Pallas kernels for 0%

profile of v5, /device:TPU:0, one launch (start us, length us, event | category | flops | bytes accessed | tf_op | source)
XLA Modules:
  0.0 72.2 jit_solution(13346511622529549197)
XLA Ops:
  0.0 0.5 collective-permute-start
  0.5 0.8 %fusion.12 = (s32[2]{0:T(128)S(1)}, f32[2,128]{1,0:T(2,128)S(1)}) fusion(s32[4,128]{1,0:T(4,128)} %param.11, s32[]{:T(128)S(6)} %select_n.49), kind=kLoop, calls=%fused_computation.46 | loop fusion | flops 1278 | bytes 2060 | tf_op jit(solution)/shard_map/reduce_min | solution.py:103
  1.3 0.1 pad.29.clone
  1.4 0.8 %fusion.17 = (f32[512]{0:T(512)S(1)}, f32[512]{0:T(512)S(1)}) fusion(f32[1024]{0:T(1024)} %param.14, s32[]{:T(128)S(6)} %select_n.50, s32[]{:T(128)S(6)} %select_n.51), kind=kLoop, calls=%fused_computation.56 | loop fusion | bytes 8200 | tf_op jit(solution)/shard_map/dynamic_slice | solution.py:79
  2.2 1.1 %broadcast_multiply_fusion.g_ref = f32[2,128,1024]{2,1,0:T(8,128)} fusion(f32[1024]{0:T(1024)S(1)} %get-tuple-element.19, f32[2,128]{1,0:T(2,128)S(1)} %get-tuple-element.23), kind=kLoop, calls=%fused_computation.16 | loop fusion | flops 262144 | bytes 1053696 | tf_op jit(solution)/shard_map/mul | solution.py:98
  3.4 0.0 collective-permute-done.ip_b
  3.4 3.3 %fusion.3.x_ref = f32[2,128,1024]{2,1,0:T(8,128)} fusion(bf16[1024,512]{1,0:T(8,128)(2,1)S(1)} %collective-permute-done.ip_b, bf16[1024,512]{1,0:T(8,128)(2,1)} %ip_a.1, f32[1024]{0:T(1024)S(1)} %get-tuple-element.18, bf16[4,128,1024]{2,1,0:T(8,128)(2,1)S(1)} %copy-done, s32[]{:T(128)S(6)} %select_n.49), kind=kOutput, calls=%fused_computation.5 | convolution fusion | flops 541327360 | bytes 3674116 | tf_op jit(solution)/shard_map/dot_general | solution.py:91
  6.7 3.1 %shard_map.100 = f32[2,128,1024]{2,1,0:T(8,128)} custom-call(f32[2,128,1024]{2,1,0:T(8,128)} %fusion.3.x_ref, f32[2,128,1024]{2,1,0:T(8,128)} %broadcast_multiply_fusion.g_ref), custom_call_target="tpu_custom_call" | custom-call | flops 524288 | bytes 3145728 | tf_op jit(solution)/shard_map/pallas_call | solution.py:27
  9.8 1.3 %convert_element_type.72 = bf16[2,128,1024]{2,1,0:T(8,128)(2,1)S(1)} convert(f32[2,128,1024]{2,1,0:T(8,128)} %shard_map.100) | non-fusion elementwise | flops 262144 | bytes 1572864 | tf_op jit(solution)/shard_map/convert_element_type | solution.py:111
  11.1 0.8 %slice.48 = f32[2,1,1024]{2,1,0:T(1,128)S(1)} slice(f32[2,128,1024]{2,1,0:T(8,128)} %shard_map.100), slice={[0:2], [127:128], [0:1024]} | slice | bytes 16384 | tf_op jit(solution)/shard_map/slice | solution.py:104
  12.0 0.0 copy-start.1
  12.0 0.0 copy-start.3
  12.0 0.0 copy-start.4
  12.0 0.0 copy-start.5
  12.0 0.1 maximum_maximum_fusion
  12.2 1.0 %pad_maximum_fusion.1 = bf16[8,48,1024]{2,1,0:T(8,128)(2,1)} fusion(bf16[8,16,1024]{2,1,0:T(8,128)(2,1)S(1)} %broadcast_in_dim.31, bf16[8,32,1024]{2,1,0:T(8,128)(2,1)S(1)} %bitcast.50), kind=kLoop, calls=%fused_computation.11 | loop fusion | flops 1572864 | bytes 1572864 | tf_op jit(solution)/shard_map/concatenate | solution.py:112
  13.1 6.9 %all-to-all-start = ((bf16[8,48,1024]{2,1,0:T(8,128)(2,1)}), bf16[8,48,1024]{2,1,0:T(8,128)(2,1)S(1)}, u32[]{:S(2)}, u32[]{:S(2)}) async-start(bf16[8,48,1024]{2,1,0:T(8,128)(2,1)} %pad_maximum_fusion.1), calls=%async_computation | async-start | bytes 1572864 | tf_op jit(solution)/shard_map/all_to_all | solution.py:116
  20.0 0.2 collective-permute-start.1
  20.2 0.4 collective-permute-start.2
  20.6 0.1 collective-permute-start.4
  20.8 0.4 collective-permute-start.3
  21.1 0.1 reshape.179
  21.2 0.5 add_convert_fusion
  21.8 0.1 broadcast_power_fusion
  21.9 0.2 fusion.7.hot_ref
  22.2 3.7 %collective-permute-done.3 = bf16[18,512]{1,0:T(8,128)(2,1)S(1)} collective-permute-done((bf16[18,512]{1,0:T(8,128)(2,1)S(1)}, bf16[18,512]{1,0:T(8,128)(2,1)S(1)}, u32[]{:S(2)}, u32[]{:S(2)}) %collective-permute-start.3) | collective-permute-done | bytes 18464 | tf_op jit(solution)/shard_map/ppermute | solution.py:67
  25.9 14.8 %all-to-all-done = bf16[8,48,1024]{2,1,0:T(8,128)(2,1)S(1)} async-done(((bf16[8,48,1024]{2,1,0:T(8,128)(2,1)}), bf16[8,48,1024]{2,1,0:T(8,128)(2,1)S(1)}, u32[]{:S(2)}, u32[]{:S(2)}) %all-to-all-start) | async-done | bytes 786464 | tf_op jit(solution)/shard_map/all_to_all | solution.py:116
  40.8 0.6 compare_select_fusion
  41.4 1.4 %copy.27 = f32[8,2,1]{0,1,2:T(2,128)} copy(f32[8,2,1]{2,1,0:T(2,128)} %compare_select_fusion) | data formatting | bytes 128 | tf_op jit(solution)/shard_map/jit(_where)/select_n | solution.py:127
  42.8 0.7 %copy.28 = f32[8,2]{1,0:T(8,128)S(1)} copy(f32[8,2]{0,1:T(2,128)} %bitcast.59) | data formatting | bytes 128 | tf_op jit(solution)/shard_map/mul | solution.py:127
  43.5 0.1 broadcast_multiply_fusion.1
  43.7 0.1 pad_multiply_fusion
  43.8 0.1 slice_add_fusion
  43.9 0.6 slice_convert_fusion
  44.5 1.4 %copy.26 = f32[8,2,1]{0,1,2:T(2,128)} copy(f32[8,2,1]{2,1,0:T(2,128)} %slice_convert_fusion) | data formatting | bytes 128 | tf_op jit(solution)/shard_map/transpose | solution.py:140
  45.9 0.7 %broadcast_compare_fusion = pred[2,8,16]{2,1,0:T(8,128)(4,1)S(1)} fusion(f32[2,8]{1,0:T(2,128)} %bitcast.58, f32[16]{0:T(128)} %get-tuple-element.25), kind=kLoop, calls=%fused_computation.43 | loop fusion | flops 256 | bytes 384 | tf_op jit(solution)/shard_map/lt | solution.py:140
  46.7 0.2 bitcast_add_fusion
  46.9 0.0 collective-permute-done.1.r_b
  46.9 0.0 collective-permute-done.4.wo_b
  46.9 0.0 copy-start.2
  46.9 1.2 %copy-done.2 = bf16[512,1024]{1,0:T(8,128)(2,1)S(1)} copy-done((bf16[512,1024]{1,0:T(8,128)(2,1)S(1)}, bf16[512,1024]{1,0:T(8,128)(2,1)}, u32[]{:S(2)}) %copy-start.2) | copy-done | bytes 1048600
  48.1 16.6 %shard_map.101 = (bf16[4,256,512]{2,1,0:T(8,128)(2,1)S(1)}, bf16[4,256,512]{2,1,0:T(8,128)(2,1)}) custom-call(s32[1]{0:T(128)} %bitcast.side_ref, f32[256,1024]{1,0:T(8,128)S(1)} %bitcast.45, bf16[4,256,128]{2,1,0:T(8,128)(2,1)S(1)} %fusion.7.hot_ref, f32[3,1024]{1,0:T(4,128)S(1)} %pad_maximum_fusion.2.vec_ref, bf16[512,1024]{1,0:T(8,128)(2,1)S(1)} %copy-done.2, ...), custom_call_target="tpu_custom_call" | custom-call | flops 8589934592 | bytes 16777216 | tf_op jit(solution)/shard_map/pallas_call | solution.py:218
  64.7 0.0 collective-permute-start.5
  64.7 2.9 %collective-permute-done.5 = bf16[4,256,512]{2,1,0:T(8,128)(2,1)S(1)} collective-permute-done((bf16[4,256,512]{2,1,0:T(8,128)(2,1)}, bf16[4,256,512]{2,1,0:T(8,128)(2,1)S(1)}, u32[]{:S(2)}, u32[]{:S(2)}) %collective-permute-start.5) | collective-permute-done | bytes 1048608 | tf_op jit(solution)/shard_map/ppermute | solution.py:67
  67.6 0.1 broadcast_select_fusion.1
  67.7 0.9 %copy.41 = bf16[4,2,8,16,512]{4,0,3,2,1:T(4,128)(2,1)S(1)} copy(bf16[4,2,8,16,512]{4,3,2,1,0:T(8,128)(2,1)S(1)} %bitcast.47) | data formatting | bytes 2097152 | tf_op jit(solution)/shard_map/jit(_where)/select_n | solution.py:166
  68.6 0.9 %copy.42 = bf16[4,2,8,16,512]{4,0,3,2,1:T(4,128)(2,1)S(1)} copy(bf16[4,2,8,16,512]{4,3,2,1,0:T(8,128)(2,1)S(1)} %bitcast.46) | data formatting | bytes 2097152 | tf_op jit(solution)/shard_map/jit(_where)/select_n | solution.py:165
  69.5 2.7 %pad_maximum_fusion = bf16[4,8,16,4,512]{4,3,2,1,0:T(4,128)(2,1)} fusion(bf16[2,8,16,4,512]{4,3,2,1,0:T(4,128)(2,1)S(1)} %bitcast.48, bf16[2,8,16,4,512]{4,3,2,1,0:T(4,128)(2,1)S(1)} %bitcast.49), kind=kLoop, calls=%fused_computation.4 | loop fusion | flops 1048576 | bytes 4194304 | tf_op jit(solution)/shard_map/concatenate | solution.py:167
  (30 shorter events, 0.3 us)
Async XLA Ops:
  0.0 3.4 %copy-start = (bf16[4,128,1024]{2,1,0:T(8,128)(2,1)S(1)}, bf16[4,128,1024]{2,1,0:T(8,128)(2,1)}, u32[]{:S(2)}) copy-start(bf16[4,128,1024]{2,1,0:T(8,128)(2,1)} %param.10) | copy-start | bytes 3145732
  0.0 3.4 %collective-permute-start = (bf16[1024,512]{1,0:T(8,128)(2,1)}, bf16[1024,512]{1,0:T(8,128)(2,1)S(1)}, u32[]{:S(2)}, u32[]{:S(2)}) collective-permute-start(bf16[1024,512]{1,0:T(8,128)(2,1)} %ip_a.1), channel_id=1, source_target_pairs={{0,1},{1,0},{2,3},{3,2},{4,5},{5,4},{6,7},{7,6},{8,9},{9,8},{10,11... | collective-permute-start | bytes 3145736 | tf_op jit(solution)/shard_map/ppermute | solution.py:67
  3.4 3.3 %copy-start.6 = (bf16[1024,512]{1,0:T(8,128)(2,1)}, bf16[1024,512]{1,0:T(8,128)(2,1)S(1)}, u32[]{:S(2)}) copy-start(bf16[1024,512]{1,0:T(8,128)(2,1)S(1)} %collective-permute-done.ip_b) | copy-start | bytes 3145732
  12.0 8.1 %copy-start.1 = (bf16[512,1024]{1,0:T(8,128)(2,1)S(1)}, bf16[512,1024]{1,0:T(8,128)(2,1)}, u32[]{:S(2)}) copy-start(bf16[512,1024]{1,0:T(8,128)(2,1)} %r_a.1) | copy-start | bytes 3145732
  12.0 8.8 %copy-start.3 = (bf16[18,512]{1,0:T(8,128)(2,1)S(1)}, bf16[18,512]{1,0:T(8,128)(2,1)}, u32[]{:S(2)}) copy-start(bf16[18,512]{1,0:T(8,128)(2,1)} %param.18) | copy-start | bytes 55300
  12.0 9.2 %copy-start.4 = (s32[4,8,16,4]{2,3,1,0:T(4,128)S(1)}, s32[4,8,16,4]{2,3,1,0:T(4,128)}, u32[]{:S(2)}) copy-start(s32[4,8,16,4]{2,3,1,0:T(4,128)} %param.12) | copy-start | bytes 24580
  12.0 10.1 %copy-start.5 = (f32[1024]{0:T(1024)S(1)}, f32[1024]{0:T(1024)}, u32[]{:S(2)}) copy-start(f32[1024]{0:T(1024)} %param.16) | copy-start | bytes 12292
  13.1 27.6 %all-to-all-start = ((bf16[8,48,1024]{2,1,0:T(8,128)(2,1)}), bf16[8,48,1024]{2,1,0:T(8,128)(2,1)S(1)}, u32[]{:S(2)}, u32[]{:S(2)}) async-start(bf16[8,48,1024]{2,1,0:T(8,128)(2,1)} %pad_maximum_fusion.1), calls=%async_computation | async-start | bytes 1572864 | tf_op jit(solution)/shard_map/all_to_all | solution.py:116
  20.0 26.8 %collective-permute-start.1 = (bf16[512,1024]{1,0:T(8,128)(2,1)S(1)}, bf16[512,1024]{1,0:T(8,128)(2,1)}, u32[]{:S(2)}, u32[]{:S(2)}) collective-permute-start(bf16[512,1024]{1,0:T(8,128)(2,1)S(1)} %copy-done.1), channel_id=1, source_target_pairs={{0,1},{1,0},{2,3},{3,2},{4,5},{5,4},{6,7},{7,6},{8,9},{9,8},{10,11... | collective-permute-start | bytes 3145736 | tf_op jit(solution)/shard_map/ppermute | solution.py:67
  20.2 26.6 %collective-permute-start.2 = (bf16[1024,512]{1,0:T(8,128)(2,1)}, bf16[1024,512]{1,0:T(8,128)(2,1)}, u32[]{:S(2)}, u32[]{:S(2)}) collective-permute-start(bf16[1024,512]{1,0:T(8,128)(2,1)} %wh_a.1), channel_id=1, source_target_pairs={{0,1},{1,0},{2,3},{3,2},{4,5},{5,4},{6,7},{7,6},{8,9},{9,8},{10,11... | collective-permute-start | bytes 3145736 | tf_op jit(solution)/shard_map/ppermute | solution.py:67
  20.6 26.3 %collective-permute-start.4 = (bf16[512,1024]{1,0:T(8,128)(2,1)}, bf16[512,1024]{1,0:T(8,128)(2,1)}, u32[]{:S(2)}, u32[]{:S(2)}) collective-permute-start(bf16[512,1024]{1,0:T(8,128)(2,1)} %wo_a.1), channel_id=1, source_target_pairs={{0,1},{1,0},{2,3},{3,2},{4,5},{5,4},{6,7},{7,6},{8,9},{9,8},{10,11... | collective-permute-start | bytes 3145736 | tf_op jit(solution)/shard_map/ppermute | solution.py:67
  20.8 5.1 %collective-permute-start.3 = (bf16[18,512]{1,0:T(8,128)(2,1)S(1)}, bf16[18,512]{1,0:T(8,128)(2,1)S(1)}, u32[]{:S(2)}, u32[]{:S(2)}) collective-permute-start(bf16[18,512]{1,0:T(8,128)(2,1)S(1)} %copy-done.3), channel_id=1, source_target_pairs={{0,1},{1,0},{2,3},{3,2},{4,5},{5,4},{6,7},{7,6},{8,9},{9,8},{10,11... | collective-permute-start | bytes 55304 | tf_op jit(solution)/shard_map/ppermute | solution.py:67
  46.9 1.2 %copy-start.2 = (bf16[512,1024]{1,0:T(8,128)(2,1)S(1)}, bf16[512,1024]{1,0:T(8,128)(2,1)}, u32[]{:S(2)}) copy-start(bf16[512,1024]{1,0:T(8,128)(2,1)} %r_a.1) | copy-start | bytes 3145732
  64.7 2.9 %collective-permute-start.5 = (bf16[4,256,512]{2,1,0:T(8,128)(2,1)}, bf16[4,256,512]{2,1,0:T(8,128)(2,1)S(1)}, u32[]{:S(2)}, u32[]{:S(2)}) collective-permute-start(bf16[4,256,512]{2,1,0:T(8,128)(2,1)} %get-tuple-element.8), channel_id=1, source_target_pairs={{0,1},{1,0},{2,3},{3,2},{4,5},{5,4},{6,7},{7,6},{8,9},{9,8},{10,11... | collective-permute-start | bytes 3145736 | tf_op jit(solution)/shard_map/ppermute | solution.py:67

commit v6 on v5

--- a/solution.py
+++ b/solution.py
@@ -106,7 +106,7 @@
     ends_lo = (ends_local - ends_hi.astype(jnp.float32)).astype(jnp.bfloat16)
     first_rows = jnp.broadcast_to(first[:, None], (bh, width)).astype(jnp.bfloat16)
     extra = jnp.concatenate([ends_hi, ends_lo, first_rows], axis=0)
-    pad_rows = -(-(extra.shape[0] + bh * sub) // 16) * 16 - bh * sub
+    pad_rows = -(-(extra.shape[0] + bh * sub) // 8) * 8 - bh * sub
     extra = jnp.pad(extra, ((0, pad_rows - extra.shape[0]), (0, 0)))
     states = jnp.swapaxes(local.astype(jnp.bfloat16).reshape(bh, ntm, sub, width), 0, 1)
     send = jnp.concatenate(

time: 72.7 us -> 64.7 us (0.89)
  local copies, waits for them, and re-layouts: 8.63 us -> 5.54 us
  other arithmetic: 10.4 us -> 7.93 us
  waiting for transfers between devices: 21.5 us -> 19.1 us
    all_to_all x1, waiting for transfers between devices: 14.8 us -> 12 us  [per_device(): got = lax.all_to_all(send, 'tm', split_axis=0, concat_axis=0, tiled=True)]
    select_n x1, local copies, waits for them, and re-layouts: 1.35 us -> 0.09 us  [per_device(): gain = jnp.where(firsts >= steps, 1.0, 0.0)[:, :, None] * whole_block]
    transpose x1, local copies, waits for them, and re-layouts: 1.35 us -> 0.09 us  [per_device(): jnp.swapaxes(firsts, 0, 1)[:, :, None]]
  transfers between devices with their start and end apart: 7 -> 7, of which waited for: 3 -> 3; matrix products, arithmetic and copies ran while one was open for 14% -> 7% of each run, Pallas kernels for 0% -> 0%
where the time goes in v6:
time: 64.7 us; the launch traced here: 64.3 us
  Pallas kernels  19.7 us (30%)
  waiting for transfers between devices  19.1 us (30%)
  starting transfers between devices  8.5 us (13%)
  other arithmetic  7.93 us (12%)
  local copies, waits for them, and re-layouts  5.54 us (9%)
  matrix products  3.28 us (5%)
    pallas_call x1, Pallas kernels, imagine(): pl.pallas_call(_imagine_kernel, out_shape=(out, out), in_specs=[pl.BlockS...  16.6 us
    all_to_all x1, waiting for transfers between devices, per_device(): got = lax.all_to_all(send, 'tm', split_axis=0, concat_axis=0, tiled=True)  12 us
    ppermute x6, waiting for transfers between devices, partner(): return lax.ppermute(x, 'mp', swap)  7.12 us
    all_to_all x1, starting transfers between devices, per_device(): got = lax.all_to_all(send, 'tm', split_axis=0, concat_axis=0, tiled=True)  6.92 us
    dot_general x1, matrix products, per_device(): jnp.dot(x.reshape(bh * steps, feat), ip, preferred_element_type=jnp.float32)  3.28 us
    pallas_call x1, Pallas kernels, local_scan(): pl.pallas_call(_scan_kernel, out_shape=jax.ShapeDtypeStruct(driven.shape,...  3.12 us
    concatenate x1, other arithmetic, per_device(): return jnp.concatenate([first_half, second_half], axis=0)  2.67 us
    ppermute x6, starting transfers between devices, partner(): return lax.ppermute(x, 'mp', swap)  1.58 us
  transfers between devices with their start and end apart: 7, of which 3 were waited for; matrix products, arithmetic and copies ran while one was open for 7% of the time, Pallas kernels for 0%

profile of v6, /device:TPU:0, one launch (start us, length us, event | category | flops | bytes accessed | tf_op | source)
XLA Modules:
  0.0 64.3 jit_solution(7647144871538312708)
XLA Ops:
  0.0 0.0 copy-start
  0.0 0.5 collective-permute-start
  0.5 0.8 %fusion.12 = (s32[2]{0:T(128)S(1)}, f32[2,128]{1,0:T(2,128)S(1)}) fusion(s32[4,128]{1,0:T(4,128)} %param.11, s32[]{:T(128)S(6)} %select_n.49), kind=kLoop, calls=%fused_computation.46 | loop fusion | flops 1278 | bytes 2060 | tf_op jit(solution)/shard_map/reduce_min | solution.py:103
  1.3 0.1 pad.29.clone
  1.4 0.8 %fusion.17 = (f32[512]{0:T(512)S(1)}, f32[512]{0:T(512)S(1)}) fusion(f32[1024]{0:T(1024)} %param.14, s32[]{:T(128)S(6)} %select_n.50, s32[]{:T(128)S(6)} %select_n.51), kind=kLoop, calls=%fused_computation.56 | loop fusion | bytes 8200 | tf_op jit(solution)/shard_map/dynamic_slice | solution.py:79
  2.2 1.1 %broadcast_multiply_fusion.g_ref = f32[2,128,1024]{2,1,0:T(8,128)} fusion(f32[1024]{0:T(1024)S(1)} %get-tuple-element.19, f32[2,128]{1,0:T(2,128)S(1)} %get-tuple-element.23), kind=kLoop, calls=%fused_computation.16 | loop fusion | flops 262144 | bytes 1053696 | tf_op jit(solution)/shard_map/mul | solution.py:98
  3.4 0.0 collective-permute-done.ip_b
  3.4 3.3 %fusion.3.x_ref = f32[2,128,1024]{2,1,0:T(8,128)} fusion(bf16[1024,512]{1,0:T(8,128)(2,1)S(1)} %collective-permute-done.ip_b, bf16[1024,512]{1,0:T(8,128)(2,1)} %ip_a.1, f32[1024]{0:T(1024)S(1)} %get-tuple-element.18, bf16[4,128,1024]{2,1,0:T(8,128)(2,1)S(1)} %copy-done, s32[]{:T(128)S(6)} %select_n.49), kind=kOutput, calls=%fused_computation.5 | convolution fusion | flops 541327360 | bytes 3674116 | tf_op jit(solution)/shard_map/dot_general | solution.py:91
  6.7 3.1 %shard_map.100 = f32[2,128,1024]{2,1,0:T(8,128)} custom-call(f32[2,128,1024]{2,1,0:T(8,128)} %fusion.3.x_ref, f32[2,128,1024]{2,1,0:T(8,128)} %broadcast_multiply_fusion.g_ref), custom_call_target="tpu_custom_call" | custom-call | flops 524288 | bytes 3145728 | tf_op jit(solution)/shard_map/pallas_call | solution.py:27
  9.8 1.3 %convert_element_type.72 = bf16[2,128,1024]{2,1,0:T(8,128)(2,1)S(1)} convert(f32[2,128,1024]{2,1,0:T(8,128)} %shard_map.100) | non-fusion elementwise | flops 262144 | bytes 1572864 | tf_op jit(solution)/shard_map/convert_element_type | solution.py:111
  11.1 0.0 copy-start.1
  11.1 0.0 copy-start.3
  11.1 0.0 copy-start.4
  11.1 0.9 %slice.48 = f32[2,1,1024]{2,1,0:T(1,128)S(1)} slice(f32[2,128,1024]{2,1,0:T(8,128)} %shard_map.100), slice={[0:2], [127:128], [0:1024]} | slice | bytes 16384 | tf_op jit(solution)/shard_map/slice | solution.py:104
  12.1 0.0 copy-start.5
  12.1 0.1 maximum_maximum_fusion
  12.2 0.9 %pad_maximum_fusion.1 = bf16[8,40,1024]{2,1,0:T(8,128)(2,1)} fusion(bf16[8,8,1024]{2,1,0:T(8,128)(2,1)S(1)} %broadcast_in_dim.31, bf16[8,32,1024]{2,1,0:T(8,128)(2,1)S(1)} %bitcast.51), kind=kLoop, calls=%fused_computation.11 | loop fusion | flops 1310720 | bytes 1310720 | tf_op jit(solution)/shard_map/concatenate | solution.py:112
  13.1 6.9 %all-to-all-start = ((bf16[8,40,1024]{2,1,0:T(8,128)(2,1)}), bf16[8,40,1024]{2,1,0:T(8,128)(2,1)S(1)}, u32[]{:S(2)}, u32[]{:S(2)}) async-start(bf16[8,40,1024]{2,1,0:T(8,128)(2,1)} %pad_maximum_fusion.1), calls=%async_computation | async-start | bytes 1310720 | tf_op jit(solution)/shard_map/all_to_all | solution.py:116
  20.1 0.2 collective-permute-start.1
  20.2 0.4 collective-permute-start.2
  20.6 0.1 collective-permute-start.4
  20.8 0.4 collective-permute-start.3
  21.2 0.1 reshape.179
  21.3 0.1 broadcast_power_fusion
  21.4 0.2 fusion.7.hot_ref
  21.6 0.0 copy-done.5
  21.7 4.2 %collective-permute-done.3 = bf16[18,512]{1,0:T(8,128)(2,1)S(1)} collective-permute-done((bf16[18,512]{1,0:T(8,128)(2,1)S(1)}, bf16[18,512]{1,0:T(8,128)(2,1)S(1)}, u32[]{:S(2)}, u32[]{:S(2)}) %collective-permute-start.3) | collective-permute-done | bytes 18464 | tf_op jit(solution)/shard_map/ppermute | solution.py:67
  25.9 12.0 %all-to-all-done = bf16[8,40,1024]{2,1,0:T(8,128)(2,1)S(1)} async-done(((bf16[8,40,1024]{2,1,0:T(8,128)(2,1)}), bf16[8,40,1024]{2,1,0:T(8,128)(2,1)S(1)}, u32[]{:S(2)}, u32[]{:S(2)}) %all-to-all-start) | async-done | bytes 655392 | tf_op jit(solution)/shard_map/all_to_all | solution.py:116
  38.0 0.1 copy.27
  38.1 0.1 copy.28
  38.2 0.1 broadcast_multiply_fusion.1
  38.3 0.1 pad_multiply_fusion
  38.5 0.1 slice_add_fusion
  38.6 0.1 copy.26
  38.7 0.1 broadcast_compare_fusion
  38.8 0.2 bitcast_add_fusion
  39.0 0.0 collective-permute-done.1.r_b
  39.0 0.0 collective-permute-done.2.wh_b
  39.0 0.0 collective-permute-done.4.wo_b
  39.0 0.0 copy-start.2
  39.1 1.2 %copy-done.2 = bf16[512,1024]{1,0:T(8,128)(2,1)S(1)} copy-done((bf16[512,1024]{1,0:T(8,128)(2,1)S(1)}, bf16[512,1024]{1,0:T(8,128)(2,1)}, u32[]{:S(2)}) %copy-start.2) | copy-done | bytes 1048600
  40.3 16.6 %shard_map.101 = (bf16[4,256,512]{2,1,0:T(8,128)(2,1)S(1)}, bf16[4,256,512]{2,1,0:T(8,128)(2,1)}) custom-call(s32[1]{0:T(128)} %bitcast.side_ref, f32[256,1024]{1,0:T(8,128)S(1)} %bitcast.45, bf16[4,256,128]{2,1,0:T(8,128)(2,1)S(1)} %fusion.7.hot_ref, f32[3,1024]{1,0:T(4,128)S(1)} %pad_maximum_fusion.2.vec_ref, bf16[512,1024]{1,0:T(8,128)(2,1)S(1)} %copy-done.2, ...), custom_call_target="tpu_custom_call" | custom-call | flops 8589934592 | bytes 16777216 | tf_op jit(solution)/shard_map/pallas_call | solution.py:218
  56.8 0.0 collective-permute-start.5
  56.8 2.9 %collective-permute-done.5 = bf16[4,256,512]{2,1,0:T(8,128)(2,1)S(1)} collective-permute-done((bf16[4,256,512]{2,1,0:T(8,128)(2,1)}, bf16[4,256,512]{2,1,0:T(8,128)(2,1)S(1)}, u32[]{:S(2)}, u32[]{:S(2)}) %collective-permute-start.5) | collective-permute-done | bytes 1048608 | tf_op jit(solution)/shard_map/ppermute | solution.py:67
  59.7 0.1 broadcast_select_fusion.1
  59.9 0.9 %copy.41 = bf16[4,2,8,16,512]{4,0,3,2,1:T(4,128)(2,1)S(1)} copy(bf16[4,2,8,16,512]{4,3,2,1,0:T(8,128)(2,1)S(1)} %bitcast.47) | data formatting | bytes 2097152 | tf_op jit(solution)/shard_map/jit(_where)/select_n | solution.py:166
  60.8 0.9 %copy.42 = bf16[4,2,8,16,512]{4,0,3,2,1:T(4,128)(2,1)S(1)} copy(bf16[4,2,8,16,512]{4,3,2,1,0:T(8,128)(2,1)S(1)} %bitcast.46) | data formatting | bytes 2097152 | tf_op jit(solution)/shard_map/jit(_where)/select_n | solution.py:165
  61.6 2.7 %pad_maximum_fusion = bf16[4,8,16,4,512]{4,3,2,1,0:T(4,128)(2,1)} fusion(bf16[2,8,16,4,512]{4,3,2,1,0:T(4,128)(2,1)S(1)} %bitcast.48, bf16[2,8,16,4,512]{4,3,2,1,0:T(4,128)(2,1)S(1)} %bitcast.49), kind=kLoop, calls=%fused_computation.4 | loop fusion | flops 1048576 | bytes 4194304 | tf_op jit(solution)/shard_map/concatenate | solution.py:167
  (30 shorter events, 0.3 us)
Async XLA Ops:
  0.0 3.4 %copy-start = (bf16[4,128,1024]{2,1,0:T(8,128)(2,1)S(1)}, bf16[4,128,1024]{2,1,0:T(8,128)(2,1)}, u32[]{:S(2)}) copy-start(bf16[4,128,1024]{2,1,0:T(8,128)(2,1)} %param.10) | copy-start | bytes 3145732
  0.0 3.4 %collective-permute-start = (bf16[1024,512]{1,0:T(8,128)(2,1)}, bf16[1024,512]{1,0:T(8,128)(2,1)S(1)}, u32[]{:S(2)}, u32[]{:S(2)}) collective-permute-start(bf16[1024,512]{1,0:T(8,128)(2,1)} %ip_a.1), channel_id=1, source_target_pairs={{0,1},{1,0},{2,3},{3,2},{4,5},{5,4},{6,7},{7,6},{8,9},{9,8},{10,11... | collective-permute-start | bytes 3145736 | tf_op jit(solution)/shard_map/ppermute | solution.py:67
  3.4 3.3 %copy-start.6 = (bf16[1024,512]{1,0:T(8,128)(2,1)}, bf16[1024,512]{1,0:T(8,128)(2,1)S(1)}, u32[]{:S(2)}) copy-start(bf16[1024,512]{1,0:T(8,128)(2,1)S(1)} %collective-permute-done.ip_b) | copy-start | bytes 3145732
  11.1 9.0 %copy-start.1 = (bf16[512,1024]{1,0:T(8,128)(2,1)S(1)}, bf16[512,1024]{1,0:T(8,128)(2,1)}, u32[]{:S(2)}) copy-start(bf16[512,1024]{1,0:T(8,128)(2,1)} %r_a.1) | copy-start | bytes 3145732
  11.1 9.7 %copy-start.3 = (bf16[18,512]{1,0:T(8,128)(2,1)S(1)}, bf16[18,512]{1,0:T(8,128)(2,1)}, u32[]{:S(2)}) copy-start(bf16[18,512]{1,0:T(8,128)(2,1)} %param.18) | copy-start | bytes 55300
  11.1 10.0 %copy-start.4 = (s32[4,8,16,4]{2,3,1,0:T(4,128)S(1)}, s32[4,8,16,4]{2,3,1,0:T(4,128)}, u32[]{:S(2)}) copy-start(s32[4,8,16,4]{2,3,1,0:T(4,128)} %param.12) | copy-start | bytes 24580
  12.1 9.6 %copy-start.5 = (f32[1024]{0:T(1024)S(1)}, f32[1024]{0:T(1024)}, u32[]{:S(2)}) copy-start(f32[1024]{0:T(1024)} %param.16) | copy-start | bytes 12292
  13.1 24.8 %all-to-all-start = ((bf16[8,40,1024]{2,1,0:T(8,128)(2,1)}), bf16[8,40,1024]{2,1,0:T(8,128)(2,1)S(1)}, u32[]{:S(2)}, u32[]{:S(2)}) async-start(bf16[8,40,1024]{2,1,0:T(8,128)(2,1)} %pad_maximum_fusion.1), calls=%async_computation | async-start | bytes 1310720 | tf_op jit(solution)/shard_map/all_to_all | solution.py:116
  20.1 19.0 %collective-permute-start.1 = (bf16[512,1024]{1,0:T(8,128)(2,1)S(1)}, bf16[512,1024]{1,0:T(8,128)(2,1)}, u32[]{:S(2)}, u32[]{:S(2)}) collective-permute-start(bf16[512,1024]{1,0:T(8,128)(2,1)S(1)} %copy-done.1), channel_id=1, source_target_pairs={{0,1},{1,0},{2,3},{3,2},{4,5},{5,4},{6,7},{7,6},{8,9},{9,8},{10,11... | collective-permute-start | bytes 3145736 | tf_op jit(solution)/shard_map/ppermute | solution.py:67
  20.2 18.8 %collective-permute-start.2 = (bf16[1024,512]{1,0:T(8,128)(2,1)}, bf16[1024,512]{1,0:T(8,128)(2,1)}, u32[]{:S(2)}, u32[]{:S(2)}) collective-permute-start(bf16[1024,512]{1,0:T(8,128)(2,1)} %wh_a.1), channel_id=1, source_target_pairs={{0,1},{1,0},{2,3},{3,2},{4,5},{5,4},{6,7},{7,6},{8,9},{9,8},{10,11... | collective-permute-start | bytes 3145736 | tf_op jit(solution)/shard_map/ppermute | solution.py:67
  20.6 18.4 %collective-permute-start.4 = (bf16[512,1024]{1,0:T(8,128)(2,1)}, bf16[512,1024]{1,0:T(8,128)(2,1)}, u32[]{:S(2)}, u32[]{:S(2)}) collective-permute-start(bf16[512,1024]{1,0:T(8,128)(2,1)} %wo_a.1), channel_id=1, source_target_pairs={{0,1},{1,0},{2,3},{3,2},{4,5},{5,4},{6,7},{7,6},{8,9},{9,8},{10,11... | collective-permute-start | bytes 3145736 | tf_op jit(solution)/shard_map/ppermute | solution.py:67
  20.8 5.1 %collective-permute-start.3 = (bf16[18,512]{1,0:T(8,128)(2,1)S(1)}, bf16[18,512]{1,0:T(8,128)(2,1)S(1)}, u32[]{:S(2)}, u32[]{:S(2)}) collective-permute-start(bf16[18,512]{1,0:T(8,128)(2,1)S(1)} %copy-done.3), channel_id=1, source_target_pairs={{0,1},{1,0},{2,3},{3,2},{4,5},{5,4},{6,7},{7,6},{8,9},{9,8},{10,11... | collective-permute-start | bytes 55304 | tf_op jit(solution)/shard_map/ppermute | solution.py:67
  39.0 1.2 %copy-start.2 = (bf16[512,1024]{1,0:T(8,128)(2,1)S(1)}, bf16[512,1024]{1,0:T(8,128)(2,1)}, u32[]{:S(2)}) copy-start(bf16[512,1024]{1,0:T(8,128)(2,1)} %r_a.1) | copy-start | bytes 3145732
  56.8 2.9 %collective-permute-start.5 = (bf16[4,256,512]{2,1,0:T(8,128)(2,1)}, bf16[4,256,512]{2,1,0:T(8,128)(2,1)S(1)}, u32[]{:S(2)}, u32[]{:S(2)}) collective-permute-start(bf16[4,256,512]{2,1,0:T(8,128)(2,1)} %get-tuple-element.8), channel_id=1, source_target_pairs={{0,1},{1,0},{2,3},{3,2},{4,5},{5,4},{6,7},{7,6},{8,9},{9,8},{10,11... | collective-permute-start | bytes 3145736 | tf_op jit(solution)/shard_map/ppermute | solution.py:67

commit v7 on v6

--- a/solution.py
+++ b/solution.py
@@ -93,34 +93,37 @@
         )
         * scaling
     )
-    my_resets = lax.dynamic_slice_in_dim(resets, m * bh, bh, 0)
+    all_resets = lax.dynamic_slice_in_dim(resets, m * bh, bh, 0)
+    nblocks = all_resets.shape[1] // steps
+    block_resets = all_resets.reshape(bh, nblocks, steps)
+    my_resets = lax.dynamic_index_in_dim(block_resets, d, axis=1, keepdims=False)
     keep = (1 - my_resets).astype(jnp.float32)
     gates = keep[:, :, None] * decays
     local = local_scan(driven, gates)
     sub = steps // ntm
 
-    positions = lax.broadcasted_iota(jnp.int32, my_resets.shape, 1)
-    first = jnp.min(jnp.where(my_resets != 0, positions, steps), axis=1).astype(jnp.float32)
+    positions = lax.broadcasted_iota(jnp.int32, block_resets.shape, 2)
+    firsts = jnp.swapaxes(
+        jnp.min(jnp.where(block_resets != 0, positions, steps), axis=2), 0, 1
+    ).astype(jnp.float32)
+
     ends_local = local[:, -1, :]
     ends_hi = ends_local.astype(jnp.bfloat16)
     ends_lo = (ends_local - ends_hi.astype(jnp.float32)).astype(jnp.bfloat16)
-    first_rows = jnp.broadcast_to(first[:, None], (bh, width)).astype(jnp.bfloat16)
-    extra = jnp.concatenate([ends_hi, ends_lo, first_rows], axis=0)
-    pad_rows = -(-(extra.shape[0] + bh * sub) // 8) * 8 - bh * sub
-    extra = jnp.pad(extra, ((0, pad_rows - extra.shape[0]), (0, 0)))
+    extra = jnp.concatenate([ends_hi, ends_lo], axis=0).reshape(-1)
+    rows_sent = bh * sub
+    lanes = -(-extra.shape[0] // (rows_sent * 128)) * 128
+    extra = jnp.pad(extra, (0, rows_sent * lanes - extra.shape[0])).reshape(rows_sent, lanes)
     states = jnp.swapaxes(local.astype(jnp.bfloat16).reshape(bh, ntm, sub, width), 0, 1)
     send = jnp.concatenate(
-        [states.reshape(ntm, bh * sub, width), jnp.broadcast_to(extra[None], (ntm,) + extra.shape)],
-        axis=1,
+        [states.reshape(ntm, rows_sent, width), jnp.broadcast_to(extra[None], (ntm,) + extra.shape)],
+        axis=2,
     )
     got = lax.all_to_all(send, "tm", split_axis=0, concat_axis=0, tiled=True)
-    recv = jnp.swapaxes(got[:, : bh * sub].reshape(ntm, bh, sub, width), 0, 1)
-    got_extra = got[:, bh * sub :]
-    gathered = got_extra[:, :bh].astype(jnp.float32) + got_extra[:, bh : 2 * bh].astype(
-        jnp.float32
-    )
+    recv = jnp.swapaxes(got[:, :, :width].reshape(ntm, bh, sub, width), 0, 1)
+    got_extra = got[:, :, width:].reshape(ntm, -1)[:, : 2 * bh * width].reshape(ntm, 2, bh, width)
+    gathered = got_extra[:, 0].astype(jnp.float32) + got_extra[:, 1].astype(jnp.float32)
     ends = gathered
-    firsts = got_extra[:, 2 * bh : 3 * bh, 0].astype(jnp.float32)
 
     nblocks = gathered.shape[0]
     whole_block = decays ** steps
@@ -230,7 +233,7 @@
 def solution(mesh):
     in_specs = (
         P("rep", "tm", None),
-        P("rep", "tm"),
+        P("rep", None),
         P("rep", None, "tm", None),
         P(None, "mp"),
         P(),

time: 64.7 us -> 85.4 us (1.32)
  blocking collectives: 0 us -> 27.6 us
  waiting for transfers between devices: 19.1 us -> 14.7 us
  starting transfers between devices: 8.5 us -> 5.38 us
  local copies, waits for them, and re-layouts: 5.54 us -> 6.97 us
    unnamed x0 -> x1, blocking collectives: none -> 27.6 us
    ppermute x6, waiting for transfers between devices: 7.12 us -> 2.88 us  [partner(): return lax.ppermute(x, 'mp', swap)]
    all_to_all x1, starting transfers between devices: 6.92 us -> 3.86 us  [per_device(): got = lax.all_to_all(send, 'tm', split_axis=0, concat_axis=0, tiled=True)]
    unnamed x15 -> x13, local copies, waits for them, and re-layouts: 1.26 us -> 2.21 us
  transfers between devices with their start and end apart: 7 -> 7, of which waited for: 3 -> 2; matrix products, arithmetic and copies ran while one was open for 7% -> 13% of each run, Pallas kernels for 0% -> 4%
where the time goes in v7:
time: 85.4 us; the launch traced here: 84.9 us
  blocking collectives  27.6 us (32%)
  Pallas kernels  19.4 us (23%)
  waiting for transfers between devices  14.7 us (17%)
  other arithmetic  7.24 us (8%)
  local copies, waits for them, and re-layouts  6.97 us (8%)
  starting transfers between devices  5.38 us (6%)
  matrix products  3.22 us (4%)
    unnamed x1, blocking collectives  27.6 us
    pallas_call x1, Pallas kernels, imagine(): pl.pallas_call(_imagine_kernel, out_shape=(out, out), in_specs=[pl.BlockS...  16.3 us
    all_to_all x1, waiting for transfers between devices, per_device(): got = lax.all_to_all(send, 'tm', split_axis=0, concat_axis=0, tiled=True)  11.8 us
    all_to_all x1, starting transfers between devices, per_device(): got = lax.all_to_all(send, 'tm', split_axis=0, concat_axis=0, tiled=True)  3.86 us
    dot_general x1, matrix products, per_device(): jnp.dot(x.reshape(bh * steps, feat), ip, preferred_element_type=jnp.float32)  3.22 us
    pallas_call x1, Pallas kernels, local_scan(): pl.pallas_call(_scan_kernel, out_shape=jax.ShapeDtypeStruct(driven.shape,...  3.13 us
    ppermute x6, waiting for transfers between devices, partner(): return lax.ppermute(x, 'mp', swap)  2.88 us
    concatenate x1, other arithmetic, per_device(): return jnp.concatenate([first_half, second_half], axis=0)  2.67 us
  transfers between devices with their start and end apart: 7, of which 2 were waited for; matrix products, arithmetic and copies ran while one was open for 13% of the time, Pallas kernels for 4%

profile of v7, /device:TPU:0, one launch (start us, length us, event | category | flops | bytes accessed | tf_op | source)
XLA Modules:
  0.0 84.9 jit_solution(16211111119147699037)
XLA Ops:
  0.0 0.0 copy-start
  0.0 0.5 collective-permute-start
  0.5 0.1 collective-permute-start.1
  0.6 0.4 collective-permute-start.2
  1.0 0.1 collective-permute-start.4
  1.1 0.4 collective-permute-start.3
  1.5 27.6 %all-gather = s32[4,1024]{1,0:T(4,128)S(1)} all-gather(s32[4,128]{1,0:T(4,128)} %param.11), channel_id=9, replica_groups=mesh['axis_0'=2,'axis_1'=8,'axis_2'=2] {'axis_1'}, dimensions={1}, use_global_device_ids=true | all-gather | bytes 18432 | tf_op args[1]
  29.2 0.2 fusion.11
  29.4 0.8 fusion.19
  30.3 0.8 constant_dynamic-slice_fusion
  31.0 1.1 %broadcast_multiply_fusion.g_ref = f32[2,128,1024]{2,1,0:T(8,128)} fusion(f32[1024]{0:T(1024)S(1)} %get-tuple-element.21, f32[2,128]{1,0:T(2,128)S(1)} %convert_bitcast_fusion.1), kind=kLoop, calls=%fused_computation.17 | loop fusion | flops 262144 | bytes 1053696 | tf_op jit(solution)/shard_map/mul | solution.py:101
  32.2 0.0 collective-permute-done.ip_b
  32.2 3.2 %fusion.3.x_ref = f32[2,128,1024]{2,1,0:T(8,128)} fusion(bf16[1024,512]{1,0:T(8,128)(2,1)} %collective-permute-done.ip_b, bf16[1024,512]{1,0:T(8,128)(2,1)} %ip_a.1, f32[1024]{0:T(1024)S(1)} %get-tuple-element.20, bf16[4,128,1024]{2,1,0:T(8,128)(2,1)S(1)} %copy-done, s32[]{:T(128)S(6)} %select_n.55), kind=kOutput, calls=%fused_computation.5 | convolution fusion | flops 541327360 | bytes 3674116 | tf_op jit(solution)/shard_map/dot_general | solution.py:91
  35.4 3.1 %shard_map.100 = f32[2,128,1024]{2,1,0:T(8,128)} custom-call(f32[2,128,1024]{2,1,0:T(8,128)} %fusion.3.x_ref, f32[2,128,1024]{2,1,0:T(8,128)} %broadcast_multiply_fusion.g_ref), custom_call_target="tpu_custom_call" | custom-call | flops 524288 | bytes 3145728 | tf_op jit(solution)/shard_map/pallas_call | solution.py:27
  38.5 1.3 %convert_element_type.67 = bf16[2,128,1024]{2,1,0:T(8,128)(2,1)S(1)} convert(f32[2,128,1024]{2,1,0:T(8,128)} %shard_map.100) | non-fusion elementwise | flops 262144 | bytes 1572864 | tf_op jit(solution)/shard_map/convert_element_type | solution.py:117
  39.8 0.0 copy-start.5
  39.8 0.0 copy-start.4
  39.8 0.9 %slice.48 = f32[2,1,1024]{2,1,0:T(1,128)S(1)} slice(f32[2,128,1024]{2,1,0:T(8,128)} %shard_map.100), slice={[0:2], [127:128], [0:1024]} | slice | bytes 16384 | tf_op jit(solution)/shard_map/slice | solution.py:110
  40.8 0.9 %pad_maximum_fusion.1 = bf16[8,32,1152]{2,1,0:T(8,128)(2,1)} fusion(bf16[8,32,128]{2,1,0:T(8,128)(2,1)S(1)} %broadcast_in_dim.30, bf16[8,32,1024]{2,1,0:T(8,128)(2,1)S(1)} %bitcast.63), kind=kLoop, calls=%fused_computation.12 | loop fusion | flops 1179648 | bytes 1179648 | tf_op jit(solution)/shard_map/concatenate | solution.py:118
  41.7 3.9 %all-to-all-start = ((bf16[8,32,1152]{2,1,0:T(8,128)(2,1)}), bf16[8,32,1152]{2,1,0:T(8,128)(2,1)S(1)}, u32[]{:S(2)}, u32[]{:S(2)}) async-start(bf16[8,32,1152]{2,1,0:T(8,128)(2,1)} %pad_maximum_fusion.1), calls=%async_computation | async-start | bytes 1179648 | tf_op jit(solution)/shard_map/all_to_all | solution.py:122
  45.6 0.1 reshape.195
  45.7 0.1 broadcast_compare_fusion
  45.8 0.1 broadcast_power_fusion
  45.9 0.2 fusion.8.hot_ref
  46.1 0.0 copy-done.5
  46.2 0.0 collective-permute-done.3
  46.2 11.8 %all-to-all-done = bf16[8,32,1152]{2,1,0:T(8,128)(2,1)S(1)} async-done(((bf16[8,32,1152]{2,1,0:T(8,128)(2,1)}), bf16[8,32,1152]{2,1,0:T(8,128)(2,1)S(1)}, u32[]{:S(2)}, u32[]{:S(2)}) %all-to-all-start) | async-done | bytes 589856 | tf_op jit(solution)/shard_map/all_to_all | solution.py:122
  58.1 0.1 broadcast_multiply_fusion.1
  58.3 0.1 pad_multiply_fusion
  58.4 0.1 slice.49
  58.5 0.0 copy-start.1
  58.5 0.1 slice_add_fusion
  58.6 0.2 fusion.4
  58.8 0.1 copy.15
  58.9 0.0 collective-permute-done.1.r_b
  58.9 0.0 copy-start.2
  58.9 1.0 %copy-done.2 = bf16[512,1024]{1,0:T(8,128)(2,1)} copy-done((bf16[512,1024]{1,0:T(8,128)(2,1)}, bf16[512,1024]{1,0:T(8,128)(2,1)S(1)}, u32[]{:S(2)}) %copy-start.2) | copy-done | bytes 1048600
  59.9 0.0 collective-permute-done.2.wh_b
  59.9 0.0 collective-permute-done.4.wo_b
  59.9 0.0 copy-start.3
  59.9 1.2 %copy-done.3 = bf16[512,1024]{1,0:T(8,128)(2,1)S(1)} copy-done((bf16[512,1024]{1,0:T(8,128)(2,1)S(1)}, bf16[512,1024]{1,0:T(8,128)(2,1)}, u32[]{:S(2)}) %copy-start.3) | copy-done | bytes 1048600
  61.1 16.3 %shard_map.101 = (bf16[4,256,512]{2,1,0:T(8,128)(2,1)S(1)}, bf16[4,256,512]{2,1,0:T(8,128)(2,1)}) custom-call(s32[1]{0:T(128)} %bitcast.side_ref, f32[256,1024]{1,0:T(8,128)S(1)} %bitcast.56, bf16[4,256,128]{2,1,0:T(8,128)(2,1)S(1)} %fusion.8.hot_ref, f32[3,1024]{1,0:T(4,128)S(1)} %pad_maximum_fusion.2.vec_ref, bf16[512,1024]{1,0:T(8,128)(2,1)S(1)} %copy-done.1, ...), custom_call_target="tpu_custom_call" | custom-call | flops 8589934592 | bytes 16777216 | tf_op jit(solution)/shard_map/pallas_call | solution.py:221
  77.4 0.0 collective-permute-start.5
  77.4 2.9 %collective-permute-done.5 = bf16[4,256,512]{2,1,0:T(8,128)(2,1)S(1)} collective-permute-done((bf16[4,256,512]{2,1,0:T(8,128)(2,1)}, bf16[4,256,512]{2,1,0:T(8,128)(2,1)S(1)}, u32[]{:S(2)}, u32[]{:S(2)}) %collective-permute-start.5) | collective-permute-done | bytes 1048608 | tf_op jit(solution)/shard_map/ppermute | solution.py:67
  80.3 0.1 broadcast_select_fusion.1
  80.4 0.9 %copy.26 = bf16[4,2,8,16,512]{4,0,3,2,1:T(4,128)(2,1)S(1)} copy(bf16[4,2,8,16,512]{4,3,2,1,0:T(8,128)(2,1)S(1)} %bitcast.58) | data formatting | bytes 2097152 | tf_op jit(solution)/shard_map/jit(_where)/select_n | solution.py:169
  81.3 0.9 %copy.27 = bf16[4,2,8,16,512]{4,0,3,2,1:T(4,128)(2,1)S(1)} copy(bf16[4,2,8,16,512]{4,3,2,1,0:T(8,128)(2,1)S(1)} %bitcast.57) | data formatting | bytes 2097152 | tf_op jit(solution)/shard_map/jit(_where)/select_n | solution.py:168
  82.2 2.7 %pad_maximum_fusion = bf16[4,8,16,4,512]{4,3,2,1,0:T(4,128)(2,1)} fusion(bf16[2,8,16,4,512]{4,3,2,1,0:T(4,128)(2,1)S(1)} %bitcast.59, bf16[2,8,16,4,512]{4,3,2,1,0:T(4,128)(2,1)S(1)} %bitcast.60), kind=kLoop, calls=%fused_computation.4 | loop fusion | flops 1048576 | bytes 4194304 | tf_op jit(solution)/shard_map/concatenate | solution.py:170
  (27 shorter events, 0.3 us)
Async XLA Ops:
  0.0 32.2 %copy-start = (bf16[4,128,1024]{2,1,0:T(8,128)(2,1)S(1)}, bf16[4,128,1024]{2,1,0:T(8,128)(2,1)}, u32[]{:S(2)}) copy-start(bf16[4,128,1024]{2,1,0:T(8,128)(2,1)} %param.10) | copy-start | bytes 3145732
  0.0 32.2 %collective-permute-start = (bf16[1024,512]{1,0:T(8,128)(2,1)}, bf16[1024,512]{1,0:T(8,128)(2,1)}, u32[]{:S(2)}, u32[]{:S(2)}) collective-permute-start(bf16[1024,512]{1,0:T(8,128)(2,1)} %ip_a.1), channel_id=1, source_target_pairs={{0,1},{1,0},{2,3},{3,2},{4,5},{5,4},{6,7},{7,6},{8,9},{9,8},{10,11... | collective-permute-start | bytes 3145736 | tf_op jit(solution)/shard_map/ppermute | solution.py:67
  0.5 58.4 %collective-permute-start.1 = (bf16[512,1024]{1,0:T(8,128)(2,1)}, bf16[512,1024]{1,0:T(8,128)(2,1)S(1)}, u32[]{:S(2)}, u32[]{:S(2)}) collective-permute-start(bf16[512,1024]{1,0:T(8,128)(2,1)} %r_a.1), channel_id=1, source_target_pairs={{0,1},{1,0},{2,3},{3,2},{4,5},{5,4},{6,7},{7,6},{8,9},{9,8},{10,11... | collective-permute-start | bytes 3145736 | tf_op jit(solution)/shard_map/ppermute | solution.py:67
  0.6 59.3 %collective-permute-start.2 = (bf16[1024,512]{1,0:T(8,128)(2,1)}, bf16[1024,512]{1,0:T(8,128)(2,1)}, u32[]{:S(2)}, u32[]{:S(2)}) collective-permute-start(bf16[1024,512]{1,0:T(8,128)(2,1)} %wh_a.1), channel_id=1, source_target_pairs={{0,1},{1,0},{2,3},{3,2},{4,5},{5,4},{6,7},{7,6},{8,9},{9,8},{10,11... | collective-permute-start | bytes 3145736 | tf_op jit(solution)/shard_map/ppermute | solution.py:67
  1.0 58.9 %collective-permute-start.4 = (bf16[512,1024]{1,0:T(8,128)(2,1)}, bf16[512,1024]{1,0:T(8,128)(2,1)}, u32[]{:S(2)}, u32[]{:S(2)}) collective-permute-start(bf16[512,1024]{1,0:T(8,128)(2,1)} %wo_a.1), channel_id=1, source_target_pairs={{0,1},{1,0},{2,3},{3,2},{4,5},{5,4},{6,7},{7,6},{8,9},{9,8},{10,11... | collective-permute-start | bytes 3145736 | tf_op jit(solution)/shard_map/ppermute | solution.py:67
  1.1 45.1 %collective-permute-start.3 = (bf16[18,512]{1,0:T(8,128)(2,1)}, bf16[18,512]{1,0:T(8,128)(2,1)S(1)}, u32[]{:S(2)}, u32[]{:S(2)}) collective-permute-start(bf16[18,512]{1,0:T(8,128)(2,1)} %param.18), channel_id=1, source_target_pairs={{0,1},{1,0},{2,3},{3,2},{4,5},{5,4},{6,7},{7,6},{8,9},{9,8},{10,11... | collective-permute-start | bytes 55304 | tf_op jit(solution)/shard_map/ppermute | solution.py:67
  39.8 6.3 %copy-start.5 = (f32[1024]{0:T(1024)S(1)}, f32[1024]{0:T(1024)}, u32[]{:S(2)}) copy-start(f32[1024]{0:T(1024)} %param.16) | copy-start | bytes 12292
  39.8 6.3 %copy-start.4 = (bf16[18,512]{1,0:T(8,128)(2,1)S(1)}, bf16[18,512]{1,0:T(8,128)(2,1)}, u32[]{:S(2)}) copy-start(bf16[18,512]{1,0:T(8,128)(2,1)} %param.18) | copy-start | bytes 55300
  41.7 16.3 %all-to-all-start = ((bf16[8,32,1152]{2,1,0:T(8,128)(2,1)}), bf16[8,32,1152]{2,1,0:T(8,128)(2,1)S(1)}, u32[]{:S(2)}, u32[]{:S(2)}) async-start(bf16[8,32,1152]{2,1,0:T(8,128)(2,1)} %pad_maximum_fusion.1), calls=%async_computation | async-start | bytes 1179648 | tf_op jit(solution)/shard_map/all_to_all | solution.py:122
  58.5 1.4 %copy-start.1 = (bf16[512,1024]{1,0:T(8,128)(2,1)S(1)}, bf16[512,1024]{1,0:T(8,128)(2,1)}, u32[]{:S(2)}) copy-start(bf16[512,1024]{1,0:T(8,128)(2,1)} %r_a.1) | copy-start | bytes 3145732
  58.9 1.0 %copy-start.2 = (bf16[512,1024]{1,0:T(8,128)(2,1)}, bf16[512,1024]{1,0:T(8,128)(2,1)S(1)}, u32[]{:S(2)}) copy-start(bf16[512,1024]{1,0:T(8,128)(2,1)S(1)} %collective-permute-done.1.r_b) | copy-start | bytes 3145732
  59.9 1.2 %copy-start.3 = (bf16[512,1024]{1,0:T(8,128)(2,1)S(1)}, bf16[512,1024]{1,0:T(8,128)(2,1)}, u32[]{:S(2)}) copy-start(bf16[512,1024]{1,0:T(8,128)(2,1)} %copy-done.2) | copy-start | bytes 3145732
  77.4 2.9 %collective-permute-start.5 = (bf16[4,256,512]{2,1,0:T(8,128)(2,1)}, bf16[4,256,512]{2,1,0:T(8,128)(2,1)S(1)}, u32[]{:S(2)}, u32[]{:S(2)}) collective-permute-start(bf16[4,256,512]{2,1,0:T(8,128)(2,1)} %get-tuple-element.8), channel_id=1, source_target_pairs={{0,1},{1,0},{2,3},{3,2},{4,5},{5,4},{6,7},{7,6},{8,9},{9,8},{10,11... | collective-permute-start | bytes 3145736 | tf_op jit(solution)/shard_map/ppermute | solution.py:67

commit v8 on v7

--- a/solution.py
+++ b/solution.py
@@ -93,26 +93,24 @@
         )
         * scaling
     )
-    all_resets = lax.dynamic_slice_in_dim(resets, m * bh, bh, 0)
-    nblocks = all_resets.shape[1] // steps
-    block_resets = all_resets.reshape(bh, nblocks, steps)
-    my_resets = lax.dynamic_index_in_dim(block_resets, d, axis=1, keepdims=False)
+    my_resets = lax.dynamic_slice_in_dim(resets, m * bh, bh, 0)
     keep = (1 - my_resets).astype(jnp.float32)
     gates = keep[:, :, None] * decays
     local = local_scan(driven, gates)
     sub = steps // ntm
-
-    positions = lax.broadcasted_iota(jnp.int32, block_resets.shape, 2)
-    firsts = jnp.swapaxes(
-        jnp.min(jnp.where(block_resets != 0, positions, steps), axis=2), 0, 1
-    ).astype(jnp.float32)
+    positions = lax.broadcasted_iota(jnp.int32, my_resets.shape, 1)
+    first = jnp.min(jnp.where(my_resets != 0, positions, steps), axis=1).astype(jnp.float32)
 
     ends_local = local[:, -1, :]
     ends_hi = ends_local.astype(jnp.bfloat16)
     ends_lo = (ends_local - ends_hi.astype(jnp.float32)).astype(jnp.bfloat16)
-    extra = jnp.concatenate([ends_hi, ends_lo], axis=0).reshape(-1)
     rows_sent = bh * sub
-    lanes = -(-extra.shape[0] // (rows_sent * 128)) * 128
+    lanes = -(-(2 * bh * width) // (rows_sent * 128)) * 128
+    room = rows_sent * lanes - bh * width - bh
+    lo_flat = ends_lo.reshape(-1)[:room]
+    extra = jnp.concatenate(
+        [ends_hi.reshape(-1), first.astype(jnp.bfloat16), lo_flat]
+    )
     extra = jnp.pad(extra, (0, rows_sent * lanes - extra.shape[0])).reshape(rows_sent, lanes)
     states = jnp.swapaxes(local.astype(jnp.bfloat16).reshape(bh, ntm, sub, width), 0, 1)
     send = jnp.concatenate(
@@ -121,8 +119,12 @@
     )
     got = lax.all_to_all(send, "tm", split_axis=0, concat_axis=0, tiled=True)
     recv = jnp.swapaxes(got[:, :, :width].reshape(ntm, bh, sub, width), 0, 1)
-    got_extra = got[:, :, width:].reshape(ntm, -1)[:, : 2 * bh * width].reshape(ntm, 2, bh, width)
-    gathered = got_extra[:, 0].astype(jnp.float32) + got_extra[:, 1].astype(jnp.float32)
+    flat = got[:, :, width:].reshape(ntm, -1)
+    got_hi = flat[:, : bh * width].astype(jnp.float32)
+    firsts = flat[:, bh * width : bh * width + bh].astype(jnp.float32)
+    got_lo = flat[:, bh * width + bh : bh * width + bh + lo_flat.shape[0]].astype(jnp.float32)
+    got_lo = jnp.pad(got_lo, ((0, 0), (0, bh * width - lo_flat.shape[0])))
+    gathered = (got_hi + got_lo).reshape(ntm, bh, width)
     ends = gathered
 
     nblocks = gathered.shape[0]
@@ -233,7 +235,7 @@
 def solution(mesh):
     in_specs = (
         P("rep", "tm", None),
-        P("rep", None),
+        P("rep", "tm"),
         P("rep", None, "tm", None),
         P(None, "mp"),
         P(),

time: 85.4 us -> 62.7 us (0.73)
  blocking collectives: 27.6 us -> 0 us
  starting transfers between devices: 5.38 us -> 8.5 us
  waiting for transfers between devices: 14.7 us -> 17.2 us
  local copies, waits for them, and re-layouts: 6.97 us -> 5.07 us
  other arithmetic: 7.24 us -> 8.28 us
    unnamed x1 -> x0, blocking collectives: 27.6 us -> none
    ppermute x6, waiting for transfers between devices: 2.88 us -> 6.62 us  [partner(): return lax.ppermute(x, 'mp', swap)]
    all_to_all x1, starting transfers between devices: 3.86 us -> 6.92 us  [per_device(): got = lax.all_to_all(send, 'tm', split_axis=0, concat_axis=0, tiled=True)]
    unnamed x13 -> x18, local copies, waits for them, and re-layouts: 2.21 us -> 0.77 us
    all_to_all x1, waiting for transfers between devices: 11.8 us -> 10.6 us  [per_device(): got = lax.all_to_all(send, 'tm', split_axis=0, concat_axis=0, tiled=True)]
  transfers between devices with their start and end apart: 7 -> 7, of which waited for: 2 -> 3; matrix products, arithmetic and copies ran while one was open for 13% -> 8% of each run, Pallas kernels for 4% -> 0%
where the time goes in v8:
time: 62.7 us; the launch traced here: 62.3 us
  Pallas kernels  19.7 us (31%)
  waiting for transfers between devices  17.2 us (27%)
  starting transfers between devices  8.5 us (14%)
  other arithmetic  8.28 us (13%)
  local copies, waits for them, and re-layouts  5.07 us (8%)
  matrix products  3.28 us (5%)
    pallas_call x1, Pallas kernels, imagine(): pl.pallas_call(_imagine_kernel, out_shape=(out, out), in_specs=[pl.BlockS...  16.5 us
    all_to_all x1, waiting for transfers between devices, per_device(): got = lax.all_to_all(send, 'tm', split_axis=0, concat_axis=0, tiled=True)  10.6 us
    all_to_all x1, starting transfers between devices, per_device(): got = lax.all_to_all(send, 'tm', split_axis=0, concat_axis=0, tiled=True)  6.92 us
    ppermute x6, waiting for transfers between devices, partner(): return lax.ppermute(x, 'mp', swap)  6.62 us
    dot_general x1, matrix products, per_device(): jnp.dot(x.reshape(bh * steps, feat), ip, preferred_element_type=jnp.float32)  3.28 us
    pallas_call x1, Pallas kernels, local_scan(): pl.pallas_call(_scan_kernel, out_shape=jax.ShapeDtypeStruct(driven.shape,...  3.13 us
    concatenate x1, other arithmetic, per_device(): return jnp.concatenate([first_half, second_half], axis=0)  2.67 us
    ppermute x6, starting transfers between devices, partner(): return lax.ppermute(x, 'mp', swap)  1.58 us
  transfers between devices with their start and end apart: 7, of which 3 were waited for; matrix products, arithmetic and copies ran while one was open for 8% of the time, Pallas kernels for 0%

profile of v8, /device:TPU:0, one launch (start us, length us, event | category | flops | bytes accessed | tf_op | source)
XLA Modules:
  0.0 62.3 jit_solution(9424594123703314089)
XLA Ops:
  0.0 0.5 collective-permute-start
  0.5 0.8 %fusion.14 = (s32[2]{0:T(128)S(1)}, f32[2,128]{1,0:T(2,128)S(1)}) fusion(s32[4,128]{1,0:T(4,128)} %param.11, s32[]{:T(128)S(6)} %select_n.48), kind=kLoop, calls=%fused_computation.48 | loop fusion | flops 1278 | bytes 2060 | tf_op jit(solution)/shard_map/reduce_min | solution.py:102
  1.3 0.8 %fusion.19 = (f32[512]{0:T(512)S(1)}, f32[512]{0:T(512)S(1)}) fusion(f32[1024]{0:T(1024)} %param.14, s32[]{:T(128)S(6)} %select_n.49, s32[]{:T(128)S(6)} %select_n.50), kind=kLoop, calls=%fused_computation.58 | loop fusion | bytes 8200 | tf_op jit(solution)/shard_map/dynamic_slice | solution.py:79
  2.2 1.1 %broadcast_multiply_fusion.g_ref = f32[2,128,1024]{2,1,0:T(8,128)} fusion(f32[1024]{0:T(1024)S(1)} %get-tuple-element.19, f32[2,128]{1,0:T(2,128)S(1)} %get-tuple-element.23), kind=kLoop, calls=%fused_computation.17 | loop fusion | flops 262144 | bytes 1053696 | tf_op jit(solution)/shard_map/mul | solution.py:98
  3.3 0.0 collective-permute-done.ip_b
  3.3 3.3 %fusion.3.x_ref = f32[2,128,1024]{2,1,0:T(8,128)} fusion(bf16[1024,512]{1,0:T(8,128)(2,1)S(1)} %collective-permute-done.ip_b, bf16[1024,512]{1,0:T(8,128)(2,1)} %ip_a.1, f32[1024]{0:T(1024)S(1)} %get-tuple-element.18, bf16[4,128,1024]{2,1,0:T(8,128)(2,1)S(1)} %copy-done, s32[]{:T(128)S(6)} %select_n.48), kind=kOutput, calls=%fused_computation.5 | convolution fusion | flops 541327360 | bytes 3674116 | tf_op jit(solution)/shard_map/dot_general | solution.py:91
  6.6 3.1 %shard_map.100 = f32[2,128,1024]{2,1,0:T(8,128)} custom-call(f32[2,128,1024]{2,1,0:T(8,128)} %fusion.3.x_ref, f32[2,128,1024]{2,1,0:T(8,128)} %broadcast_multiply_fusion.g_ref), custom_call_target="tpu_custom_call" | custom-call | flops 524288 | bytes 3145728 | tf_op jit(solution)/shard_map/pallas_call | solution.py:27
  9.7 1.3 %convert_element_type.65 = bf16[2,128,1024]{2,1,0:T(8,128)(2,1)S(1)} convert(f32[2,128,1024]{2,1,0:T(8,128)} %shard_map.100) | non-fusion elementwise | flops 262144 | bytes 1572864 | tf_op jit(solution)/shard_map/convert_element_type | solution.py:115
  11.0 0.0 copy-start.1
  11.0 0.0 copy-start.3
  11.0 0.0 copy-start.4
  11.0 0.0 copy-start.5
  11.1 0.9 %slice.56 = f32[2,1,1024]{2,1,0:T(1,128)S(1)} slice(f32[2,128,1024]{2,1,0:T(8,128)} %shard_map.100), slice={[0:2], [127:128], [0:1024]} | slice | bytes 16384 | tf_op jit(solution)/shard_map/slice | solution.py:104
  12.1 0.1 concatenate.66
  12.2 0.9 %pad_maximum_fusion.1 = bf16[8,32,1152]{2,1,0:T(8,128)(2,1)} fusion(bf16[8,32,128]{2,1,0:T(8,128)(2,1)S(1)} %broadcast_in_dim.38, bf16[8,32,1024]{2,1,0:T(8,128)(2,1)S(1)} %bitcast.52), kind=kLoop, calls=%fused_computation.12 | loop fusion | flops 1179648 | bytes 1179648 | tf_op jit(solution)/shard_map/concatenate | solution.py:116
  13.0 6.9 %all-to-all-start = ((bf16[8,32,1152]{2,1,0:T(8,128)(2,1)}), bf16[8,32,1152]{2,1,0:T(8,128)(2,1)S(1)}, u32[]{:S(2)}, u32[]{:S(2)}) async-start(bf16[8,32,1152]{2,1,0:T(8,128)(2,1)} %pad_maximum_fusion.1), calls=%async_computation | async-start | bytes 1179648 | tf_op jit(solution)/shard_map/all_to_all | solution.py:120
  19.9 0.2 collective-permute-start.1
  20.1 0.4 collective-permute-start.2
  20.5 0.1 collective-permute-start.4
  20.7 0.4 collective-permute-start.3
  21.0 0.1 reshape.188
  21.1 0.5 add_convert_fusion
  21.7 0.1 broadcast_power_fusion
  21.8 0.2 fusion.8.hot_ref
  22.1 3.7 %collective-permute-done.3 = bf16[18,512]{1,0:T(8,128)(2,1)S(1)} collective-permute-done((bf16[18,512]{1,0:T(8,128)(2,1)S(1)}, bf16[18,512]{1,0:T(8,128)(2,1)S(1)}, u32[]{:S(2)}, u32[]{:S(2)}) %collective-permute-start.3) | collective-permute-done | bytes 18464 | tf_op jit(solution)/shard_map/ppermute | solution.py:67
  25.8 10.6 %all-to-all-done = bf16[8,32,1152]{2,1,0:T(8,128)(2,1)S(1)} async-done(((bf16[8,32,1152]{2,1,0:T(8,128)(2,1)}), bf16[8,32,1152]{2,1,0:T(8,128)(2,1)S(1)}, u32[]{:S(2)}, u32[]{:S(2)}) %all-to-all-start) | async-done | bytes 589856 | tf_op jit(solution)/shard_map/all_to_all | solution.py:120
  36.5 0.1 slice.65
  36.6 0.1 reshape.186
  36.6 0.1 slice.52
  36.7 0.1 broadcast_multiply_fusion.1
  36.8 0.1 pad_multiply_fusion
  37.0 0.1 slice.59
  37.1 0.0 copy-start.2
  37.1 0.1 slice_add_fusion
  37.2 0.1 copy-done.6
  37.3 0.1 broadcast_compare_fusion
  37.4 0.2 fusion.4
  37.6 0.1 copy.14
  37.7 0.0 collective-permute-done.1.r_b
  37.7 0.0 collective-permute-done.2.wh_b
  37.7 0.6 copy-done.2
  38.3 16.5 %shard_map.101 = (bf16[4,256,512]{2,1,0:T(8,128)(2,1)S(1)}, bf16[4,256,512]{2,1,0:T(8,128)(2,1)}) custom-call(s32[1]{0:T(128)} %bitcast.side_ref, f32[256,1024]{1,0:T(8,128)S(1)} %bitcast.45, bf16[4,256,128]{2,1,0:T(8,128)(2,1)S(1)} %fusion.8.hot_ref, f32[3,1024]{1,0:T(4,128)S(1)} %pad_maximum_fusion.2.vec_ref, bf16[512,1024]{1,0:T(8,128)(2,1)S(1)} %copy-done.2, ...), custom_call_target="tpu_custom_call" | custom-call | flops 8589934592 | bytes 16777216 | tf_op jit(solution)/shard_map/pallas_call | solution.py:223
  54.8 0.0 collective-permute-start.5
  54.8 2.9 %collective-permute-done.5 = bf16[4,256,512]{2,1,0:T(8,128)(2,1)S(1)} collective-permute-done((bf16[4,256,512]{2,1,0:T(8,128)(2,1)}, bf16[4,256,512]{2,1,0:T(8,128)(2,1)S(1)}, u32[]{:S(2)}, u32[]{:S(2)}) %collective-permute-start.5) | collective-permute-done | bytes 1048608 | tf_op jit(solution)/shard_map/ppermute | solution.py:67
  57.7 0.1 broadcast_select_fusion.1
  57.8 0.9 %copy.22 = bf16[4,2,8,16,512]{4,0,3,2,1:T(4,128)(2,1)S(1)} copy(bf16[4,2,8,16,512]{4,3,2,1,0:T(8,128)(2,1)S(1)} %bitcast.47) | data formatting | bytes 2097152 | tf_op jit(solution)/shard_map/jit(_where)/select_n | solution.py:171
  58.7 0.9 %copy.23 = bf16[4,2,8,16,512]{4,0,3,2,1:T(4,128)(2,1)S(1)} copy(bf16[4,2,8,16,512]{4,3,2,1,0:T(8,128)(2,1)S(1)} %bitcast.46) | data formatting | bytes 2097152 | tf_op jit(solution)/shard_map/jit(_where)/select_n | solution.py:170
  59.6 2.7 %pad_maximum_fusion = bf16[4,8,16,4,512]{4,3,2,1,0:T(4,128)(2,1)} fusion(bf16[2,8,16,4,512]{4,3,2,1,0:T(4,128)(2,1)S(1)} %bitcast.48, bf16[2,8,16,4,512]{4,3,2,1,0:T(4,128)(2,1)S(1)} %bitcast.49), kind=kLoop, calls=%fused_computation.4 | loop fusion | flops 1048576 | bytes 4194304 | tf_op jit(solution)/shard_map/concatenate | solution.py:172
  (31 shorter events, 0.3 us)
Async XLA Ops:
  0.0 3.3 %copy-start = (bf16[4,128,1024]{2,1,0:T(8,128)(2,1)S(1)}, bf16[4,128,1024]{2,1,0:T(8,128)(2,1)}, u32[]{:S(2)}) copy-start(bf16[4,128,1024]{2,1,0:T(8,128)(2,1)} %param.10) | copy-start | bytes 3145732
  0.0 3.3 %collective-permute-start = (bf16[1024,512]{1,0:T(8,128)(2,1)}, bf16[1024,512]{1,0:T(8,128)(2,1)S(1)}, u32[]{:S(2)}, u32[]{:S(2)}) collective-permute-start(bf16[1024,512]{1,0:T(8,128)(2,1)} %ip_a.1), channel_id=1, source_target_pairs={{0,1},{1,0},{2,3},{3,2},{4,5},{5,4},{6,7},{7,6},{8,9},{9,8},{10,11... | collective-permute-start | bytes 3145736 | tf_op jit(solution)/shard_map/ppermute | solution.py:67
  3.3 3.3 %copy-start.7 = (bf16[1024,512]{1,0:T(8,128)(2,1)}, bf16[1024,512]{1,0:T(8,128)(2,1)S(1)}, u32[]{:S(2)}) copy-start(bf16[1024,512]{1,0:T(8,128)(2,1)S(1)} %collective-permute-done.ip_b) | copy-start | bytes 3145732
  11.0 8.9 %copy-start.1 = (bf16[512,1024]{1,0:T(8,128)(2,1)S(1)}, bf16[512,1024]{1,0:T(8,128)(2,1)}, u32[]{:S(2)}) copy-start(bf16[512,1024]{1,0:T(8,128)(2,1)} %r_a.1) | copy-start | bytes 3145732
  11.0 9.6 %copy-start.3 = (bf16[18,512]{1,0:T(8,128)(2,1)S(1)}, bf16[18,512]{1,0:T(8,128)(2,1)}, u32[]{:S(2)}) copy-start(bf16[18,512]{1,0:T(8,128)(2,1)} %param.18) | copy-start | bytes 55300
  11.0 10.0 %copy-start.4 = (s32[4,8,16,4]{2,3,1,0:T(4,128)S(1)}, s32[4,8,16,4]{2,3,1,0:T(4,128)}, u32[]{:S(2)}) copy-start(s32[4,8,16,4]{2,3,1,0:T(4,128)} %param.12) | copy-start | bytes 24580
  11.0 11.0 %copy-start.5 = (f32[1024]{0:T(1024)S(1)}, f32[1024]{0:T(1024)}, u32[]{:S(2)}) copy-start(f32[1024]{0:T(1024)} %param.16) | copy-start | bytes 12292
  13.0 23.4 %all-to-all-start = ((bf16[8,32,1152]{2,1,0:T(8,128)(2,1)}), bf16[8,32,1152]{2,1,0:T(8,128)(2,1)S(1)}, u32[]{:S(2)}, u32[]{:S(2)}) async-start(bf16[8,32,1152]{2,1,0:T(8,128)(2,1)} %pad_maximum_fusion.1), calls=%async_computation | async-start | bytes 1179648 | tf_op jit(solution)/shard_map/all_to_all | solution.py:120
  19.9 17.8 %collective-permute-start.1 = (bf16[512,1024]{1,0:T(8,128)(2,1)S(1)}, bf16[512,1024]{1,0:T(8,128)(2,1)}, u32[]{:S(2)}, u32[]{:S(2)}) collective-permute-start(bf16[512,1024]{1,0:T(8,128)(2,1)S(1)} %copy-done.1), channel_id=1, source_target_pairs={{0,1},{1,0},{2,3},{3,2},{4,5},{5,4},{6,7},{7,6},{8,9},{9,8},{10,11... | collective-permute-start | bytes 3145736 | tf_op jit(solution)/shard_map/ppermute | solution.py:67
  20.1 17.6 %collective-permute-start.2 = (bf16[1024,512]{1,0:T(8,128)(2,1)}, bf16[1024,512]{1,0:T(8,128)(2,1)}, u32[]{:S(2)}, u32[]{:S(2)}) collective-permute-start(bf16[1024,512]{1,0:T(8,128)(2,1)} %wh_a.1), channel_id=1, source_target_pairs={{0,1},{1,0},{2,3},{3,2},{4,5},{5,4},{6,7},{7,6},{8,9},{9,8},{10,11... | collective-permute-start | bytes 3145736 | tf_op jit(solution)/shard_map/ppermute | solution.py:67
  20.5 17.2 %collective-permute-start.4 = (bf16[512,1024]{1,0:T(8,128)(2,1)}, bf16[512,1024]{1,0:T(8,128)(2,1)}, u32[]{:S(2)}, u32[]{:S(2)}) collective-permute-start(bf16[512,1024]{1,0:T(8,128)(2,1)} %wo_a.1), channel_id=1, source_target_pairs={{0,1},{1,0},{2,3},{3,2},{4,5},{5,4},{6,7},{7,6},{8,9},{9,8},{10,11... | collective-permute-start | bytes 3145736 | tf_op jit(solution)/shard_map/ppermute | solution.py:67
  20.7 5.1 %collective-permute-start.3 = (bf16[18,512]{1,0:T(8,128)(2,1)S(1)}, bf16[18,512]{1,0:T(8,128)(2,1)S(1)}, u32[]{:S(2)}, u32[]{:S(2)}) collective-permute-start(bf16[18,512]{1,0:T(8,128)(2,1)S(1)} %copy-done.3), channel_id=1, source_target_pairs={{0,1},{1,0},{2,3},{3,2},{4,5},{5,4},{6,7},{7,6},{8,9},{9,8},{10,11... | collective-permute-start | bytes 55304 | tf_op jit(solution)/shard_map/ppermute | solution.py:67
  36.7 0.6 copy-start.6
  37.1 1.2 %copy-start.2 = (bf16[512,1024]{1,0:T(8,128)(2,1)S(1)}, bf16[512,1024]{1,0:T(8,128)(2,1)}, u32[]{:S(2)}) copy-start(bf16[512,1024]{1,0:T(8,128)(2,1)} %r_a.1) | copy-start | bytes 3145732
  54.8 2.9 %collective-permute-start.5 = (bf16[4,256,512]{2,1,0:T(8,128)(2,1)}, bf16[4,256,512]{2,1,0:T(8,128)(2,1)S(1)}, u32[]{:S(2)}, u32[]{:S(2)}) collective-permute-start(bf16[4,256,512]{2,1,0:T(8,128)(2,1)} %get-tuple-element.8), channel_id=1, source_target_pairs={{0,1},{1,0},{2,3},{3,2},{4,5},{5,4},{6,7},{7,6},{8,9},{9,8},{10,11... | collective-permute-start | bytes 3145736 | tf_op jit(solution)/shard_map/ppermute | solution.py:67

commit v9 on v8

--- a/solution.py
+++ b/solution.py
@@ -164,7 +164,7 @@
     got = partner(give_part)
 
     def arrange(part):
-        return jnp.transpose(part.reshape(horizon, bh, blocks, sub, half), (1, 2, 3, 0, 4))
+        return part.reshape(bh, blocks, sub, horizon, half)
 
     mine, theirs = arrange(keep_part), arrange(got)
     first_half = jnp.where(m == 0, mine, theirs)
@@ -202,8 +202,9 @@
             hid_b = (pre_b * jax.nn.sigmoid(pre_b)).astype(jnp.bfloat16)
             lo = (dot(hid_a, wo_a[:, :half]) + dot(hid_b, wo_b[:, :half])).astype(jnp.bfloat16)
             hi = (dot(hid_a, wo_a[:, half:]) + dot(hid_b, wo_b[:, half:])).astype(jnp.bfloat16)
-            keep_ref[step, rs, :] = jnp.where(lead, lo, hi)
-            give_ref[step, rs, :] = jnp.where(lead, hi, lo)
+            cols = pl.ds(step * half, half)
+            keep_ref[rs, cols] = jnp.where(lead, lo, hi)
+            give_ref[rs, cols] = jnp.where(lead, hi, lo)
             if step < horizon - 1:
                 up_a = dot(lo, ip_a[:half, :]) + dot(hi, ip_a[half:, :])
                 up_b = dot(lo, ip_b[:half, :]) + dot(hi, ip_b[half:, :])
@@ -217,7 +218,7 @@
 def imagine(side, current, one_hot, vecs, *weights):
     horizon, rows, _ = one_hot.shape
     half = weights[0].shape[0]
-    out = jax.ShapeDtypeStruct((horizon, rows, half), jnp.bfloat16)
+    out = jax.ShapeDtypeStruct((rows, horizon * half), jnp.bfloat16)
     vmem = pl.BlockSpec(memory_space=pltpu.VMEM)
     flops = 2 * rows * horizon * 4 * (2 * half) * (2 * half)
     return pl.pallas_call(

time: 62.7 us -> 68.8 us (1.097)
  other arithmetic: 8.28 us -> 11.8 us
  local copies, waits for them, and re-layouts: 5.07 us -> 7.69 us
    select_n x1, other arithmetic: 0.14 us -> 2.33 us  [per_device(): first_half = jnp.where(m == 0, mine, theirs)]
    concatenate x1, other arithmetic: 2.67 us -> 3.9 us  [per_device(): return jnp.concatenate([first_half, second_half], axis=0)]
    unnamed x18 -> x20, local copies, waits for them, and re-layouts: 0.77 us -> 1.74 us
    select_n x1, local copies, waits for them, and re-layouts: 0.89 us -> 1.84 us  [per_device(): first_half = jnp.where(m == 0, mine, theirs)]
    select_n x1, local copies, waits for them, and re-layouts: 0.89 us -> 1.58 us  [per_device(): second_half = jnp.where(m == 0, theirs, mine)]
  transfers between devices with their start and end apart: 7 -> 7, of which waited for: 3 -> 3; matrix products, arithmetic and copies ran while one was open for 8% -> 7% of each run, Pallas kernels for 0% -> 0%
where the time goes in v9:
time: 68.8 us; the launch traced here: 68.3 us
  Pallas kernels  19.7 us (29%)
  waiting for transfers between devices  17.1 us (25%)
  other arithmetic  11.8 us (17%)
  starting transfers between devices  8.5 us (12%)
  local copies, waits for them, and re-layouts  7.69 us (11%)
  matrix products  3.28 us (5%)
    pallas_call x1, Pallas kernels, imagine(): pl.pallas_call(_imagine_kernel, out_shape=(out, out), in_specs=[pl.BlockS...  16.5 us
    all_to_all x1, waiting for transfers between devices, per_device(): got = lax.all_to_all(send, 'tm', split_axis=0, concat_axis=0, tiled=True)  10.6 us
    all_to_all x1, starting transfers between devices, per_device(): got = lax.all_to_all(send, 'tm', split_axis=0, concat_axis=0, tiled=True)  6.92 us
    ppermute x6, waiting for transfers between devices, partner(): return lax.ppermute(x, 'mp', swap)  6.55 us
    concatenate x1, other arithmetic, per_device(): return jnp.concatenate([first_half, second_half], axis=0)  3.9 us
    dot_general x1, matrix products, per_device(): jnp.dot(x.reshape(bh * steps, feat), ip, preferred_element_type=jnp.float32)  3.28 us
    pallas_call x1, Pallas kernels, local_scan(): pl.pallas_call(_scan_kernel, out_shape=jax.ShapeDtypeStruct(driven.shape,...  3.13 us
    select_n x1, other arithmetic, per_device(): first_half = jnp.where(m == 0, mine, theirs)  2.33 us
  transfers between devices with their start and end apart: 7, of which 3 were waited for; matrix products, arithmetic and copies ran while one was open for 7% of the time, Pallas kernels for 0%

profile of v9, /device:TPU:0, one launch (start us, length us, event | category | flops | bytes accessed | tf_op | source)
XLA Modules:
  0.0 68.3 jit_solution(13259991397903778688)
XLA Ops:
  0.0 0.5 collective-permute-start
  0.5 0.8 %fusion.14 = (s32[2]{0:T(128)S(1)}, f32[2,128]{1,0:T(2,128)S(1)}) fusion(s32[4,128]{1,0:T(4,128)} %param.11, s32[]{:T(128)S(6)} %select_n.42), kind=kLoop, calls=%fused_computation.46 | loop fusion | flops 1278 | bytes 2060 | tf_op jit(solution)/shard_map/reduce_min | solution.py:102
  1.3 0.8 %fusion.19 = (f32[512]{0:T(512)S(1)}, f32[512]{0:T(512)S(1)}) fusion(f32[1024]{0:T(1024)} %param.14, s32[]{:T(128)S(6)} %select_n.43, s32[]{:T(128)S(6)} %select_n.44), kind=kLoop, calls=%fused_computation.56 | loop fusion | bytes 8200 | tf_op jit(solution)/shard_map/dynamic_slice | solution.py:79
  2.2 1.1 %broadcast_multiply_fusion.g_ref = f32[2,128,1024]{2,1,0:T(8,128)} fusion(f32[1024]{0:T(1024)S(1)} %get-tuple-element.19, f32[2,128]{1,0:T(2,128)S(1)} %get-tuple-element.23), kind=kLoop, calls=%fused_computation.15 | loop fusion | flops 262144 | bytes 1053696 | tf_op jit(solution)/shard_map/mul | solution.py:98
  3.3 3.3 %fusion.3.x_ref = f32[2,128,1024]{2,1,0:T(8,128)} fusion(bf16[1024,512]{1,0:T(8,128)(2,1)S(1)} %collective-permute-done.ip_b, bf16[1024,512]{1,0:T(8,128)(2,1)} %ip_a.1, f32[1024]{0:T(1024)S(1)} %get-tuple-element.18, bf16[4,128,1024]{2,1,0:T(8,128)(2,1)S(1)} %copy-done, s32[]{:T(128)S(6)} %select_n.42), kind=kOutput, calls=%fused_computation.5 | convolution fusion | flops 541327360 | bytes 3674116 | tf_op jit(solution)/shard_map/dot_general | solution.py:91
  6.6 3.1 %shard_map.100 = f32[2,128,1024]{2,1,0:T(8,128)} custom-call(f32[2,128,1024]{2,1,0:T(8,128)} %fusion.3.x_ref, f32[2,128,1024]{2,1,0:T(8,128)} %broadcast_multiply_fusion.g_ref), custom_call_target="tpu_custom_call" | custom-call | flops 524288 | bytes 3145728 | tf_op jit(solution)/shard_map/pallas_call | solution.py:27
  9.7 1.3 %convert_element_type.65 = bf16[2,128,1024]{2,1,0:T(8,128)(2,1)S(1)} convert(f32[2,128,1024]{2,1,0:T(8,128)} %shard_map.100) | non-fusion elementwise | flops 262144 | bytes 1572864 | tf_op jit(solution)/shard_map/convert_element_type | solution.py:115
  11.0 0.0 copy-start.1
  11.0 0.0 copy-start.4
  11.0 0.0 copy-start.5
  11.0 0.0 copy-start.6
  11.0 0.9 %slice.56 = f32[2,1,1024]{2,1,0:T(1,128)S(1)} slice(f32[2,128,1024]{2,1,0:T(8,128)} %shard_map.100), slice={[0:2], [127:128], [0:1024]} | slice | bytes 16384 | tf_op jit(solution)/shard_map/slice | solution.py:104
  12.0 0.1 concatenate.66
  12.1 0.9 %pad_maximum_fusion.1 = bf16[8,32,1152]{2,1,0:T(8,128)(2,1)} fusion(bf16[8,32,128]{2,1,0:T(8,128)(2,1)S(1)} %broadcast_in_dim.38, bf16[8,32,1024]{2,1,0:T(8,128)(2,1)S(1)} %bitcast.40), kind=kLoop, calls=%fused_computation.10 | loop fusion | flops 1179648 | bytes 1179648 | tf_op jit(solution)/shard_map/concatenate | solution.py:116
  13.0 6.9 %all-to-all-start = ((bf16[8,32,1152]{2,1,0:T(8,128)(2,1)}), bf16[8,32,1152]{2,1,0:T(8,128)(2,1)S(1)}, u32[]{:S(2)}, u32[]{:S(2)}) async-start(bf16[8,32,1152]{2,1,0:T(8,128)(2,1)} %pad_maximum_fusion.1), calls=%async_computation | async-start | bytes 1179648 | tf_op jit(solution)/shard_map/all_to_all | solution.py:120
  19.9 0.2 collective-permute-start.1
  20.1 0.4 collective-permute-start.2
  20.5 0.1 collective-permute-start.4
  20.6 0.4 collective-permute-start.3
  21.0 0.1 reshape.188
  21.1 0.6 add_convert_fusion
  21.7 0.1 broadcast_power_fusion
  21.9 0.2 fusion.8.hot_ref
  22.1 3.7 %collective-permute-done.3 = bf16[18,512]{1,0:T(8,128)(2,1)S(1)} collective-permute-done((bf16[18,512]{1,0:T(8,128)(2,1)S(1)}, bf16[18,512]{1,0:T(8,128)(2,1)S(1)}, u32[]{:S(2)}, u32[]{:S(2)}) %collective-permute-start.3) | collective-permute-done | bytes 18464 | tf_op jit(solution)/shard_map/ppermute | solution.py:67
  25.8 10.6 %all-to-all-done = bf16[8,32,1152]{2,1,0:T(8,128)(2,1)S(1)} async-done(((bf16[8,32,1152]{2,1,0:T(8,128)(2,1)}), bf16[8,32,1152]{2,1,0:T(8,128)(2,1)S(1)}, u32[]{:S(2)}, u32[]{:S(2)}) %all-to-all-start) | async-done | bytes 589856 | tf_op jit(solution)/shard_map/all_to_all | solution.py:120
  36.4 0.1 slice.65
  36.6 0.1 reshape.186
  36.6 0.1 slice.52
  36.7 0.1 broadcast_multiply_fusion.1
  36.8 0.1 pad_multiply_fusion
  37.0 0.1 slice.59
  37.0 0.0 copy-start.2
  37.1 0.1 slice_add_fusion
  37.1 0.2 copy-done.7
  37.3 0.1 broadcast_compare_fusion
  37.4 0.2 fusion.4
  37.6 0.1 copy.12
  37.8 0.0 collective-permute-done.1.r_b
  37.8 0.0 collective-permute-done.4.wo_b
  37.8 0.5 copy-done.2
  38.3 16.5 %shard_map.101 = (bf16[256,2048]{1,0:T(8,128)(2,1)S(1)}, bf16[256,2048]{1,0:T(8,128)(2,1)}) custom-call(s32[1]{0:T(128)} %bitcast.side_ref, f32[256,1024]{1,0:T(8,128)S(1)} %bitcast.37, bf16[4,256,128]{2,1,0:T(8,128)(2,1)S(1)} %fusion.8.hot_ref, f32[3,1024]{1,0:T(4,128)S(1)} %pad_maximum_fusion.2.vec_ref, bf16[512,1024]{1,0:T(8,128)(2,1)S(1)} %copy-done.2, ...), custom_call_target="tpu_custom_call" | custom-call | flops 8589934592 | bytes 16777216 | tf_op jit(solution)/shard_map/pallas_call | solution.py:224
  54.8 0.0 collective-permute-start.5
  54.8 2.9 %collective-permute-done.5 = bf16[256,2048]{1,0:T(8,128)(2,1)S(1)} collective-permute-done((bf16[256,2048]{1,0:T(8,128)(2,1)}, bf16[256,2048]{1,0:T(8,128)(2,1)S(1)}, u32[]{:S(2)}, u32[]{:S(2)}) %collective-permute-start.5) | collective-permute-done | bytes 1048608 | tf_op jit(solution)/shard_map/ppermute | solution.py:67
  57.7 1.0 %copy-done.3 = bf16[256,2048]{1,0:T(8,128)(2,1)} copy-done((bf16[256,2048]{1,0:T(8,128)(2,1)}, bf16[256,2048]{1,0:T(8,128)(2,1)S(1)}, u32[]{:S(2)}) %copy-start.3) | copy-done | bytes 1048600
  58.7 2.3 %broadcast_select_fusion.1 = (bf16[256,2048]{1,0:T(8,128)(2,1)}, bf16[256,2048]{1,0:T(8,128)(2,1)S(1)}) fusion(bf16[256,2048]{1,0:T(8,128)(2,1)S(1)} %get-tuple-element.7, bf16[256,2048]{1,0:T(8,128)(2,1)} %copy-done.3, pred[]{:T(512)S(6)} %eq.8), kind=kLoop, calls=%fused_computation.9 | loop fusion | flops 1048576 | bytes 4194305 | tf_op jit(solution)/shard_map/jit(_where)/select_n | solution.py:170
  61.0 1.8 %select_n.49 = bf16[2,8,16,4,512]{4,3,2,1,0:T(4,128)(2,1)S(1)} reshape(bf16[256,2048]{1,0:T(8,128)(2,1)} %get-tuple-element.11) | data formatting | bytes 2097152 | tf_op jit(solution)/shard_map/jit(_where)/select_n | solution.py:170
  62.8 1.6 %select_n.51 = bf16[2,8,16,4,512]{4,3,2,1,0:T(4,128)(2,1)} reshape(bf16[256,2048]{1,0:T(8,128)(2,1)S(1)} %get-tuple-element.12) | data formatting | bytes 2097152 | tf_op jit(solution)/shard_map/jit(_where)/select_n | solution.py:171
  64.4 3.9 %pad_maximum_fusion = bf16[4,8,16,4,512]{4,3,2,1,0:T(4,128)(2,1)} fusion(bf16[2,8,16,4,512]{4,3,2,1,0:T(4,128)(2,1)} %select_n.51, bf16[2,8,16,4,512]{4,3,2,1,0:T(4,128)(2,1)S(1)} %select_n.49), kind=kLoop, calls=%fused_computation.4 | loop fusion | flops 1048576 | bytes 4194304 | tf_op jit(solution)/shard_map/concatenate | solution.py:172
  (33 shorter events, 0.3 us)
Async XLA Ops:
  0.0 3.3 %copy-start = (bf16[4,128,1024]{2,1,0:T(8,128)(2,1)S(1)}, bf16[4,128,1024]{2,1,0:T(8,128)(2,1)}, u32[]{:S(2)}) copy-start(bf16[4,128,1024]{2,1,0:T(8,128)(2,1)} %param.10) | copy-start | bytes 3145732
  0.0 3.3 %collective-permute-start = (bf16[1024,512]{1,0:T(8,128)(2,1)}, bf16[1024,512]{1,0:T(8,128)(2,1)S(1)}, u32[]{:S(2)}, u32[]{:S(2)}) collective-permute-start(bf16[1024,512]{1,0:T(8,128)(2,1)} %ip_a.1), channel_id=1, source_target_pairs={{0,1},{1,0},{2,3},{3,2},{4,5},{5,4},{6,7},{7,6},{8,9},{9,8},{10,11... | collective-permute-start | bytes 3145736 | tf_op jit(solution)/shard_map/ppermute | solution.py:67
  3.3 3.3 %copy-start.8 = (bf16[1024,512]{1,0:T(8,128)(2,1)}, bf16[1024,512]{1,0:T(8,128)(2,1)S(1)}, u32[]{:S(2)}) copy-start(bf16[1024,512]{1,0:T(8,128)(2,1)S(1)} %collective-permute-done.ip_b) | copy-start | bytes 3145732
  11.0 8.9 %copy-start.1 = (bf16[512,1024]{1,0:T(8,128)(2,1)S(1)}, bf16[512,1024]{1,0:T(8,128)(2,1)}, u32[]{:S(2)}) copy-start(bf16[512,1024]{1,0:T(8,128)(2,1)} %r_a.1) | copy-start | bytes 3145732
  11.0 9.6 %copy-start.4 = (bf16[18,512]{1,0:T(8,128)(2,1)S(1)}, bf16[18,512]{1,0:T(8,128)(2,1)}, u32[]{:S(2)}) copy-start(bf16[18,512]{1,0:T(8,128)(2,1)} %param.18) | copy-start | bytes 55300
  11.0 10.0 %copy-start.5 = (s32[4,8,16,4]{2,3,1,0:T(4,128)S(1)}, s32[4,8,16,4]{2,3,1,0:T(4,128)}, u32[]{:S(2)}) copy-start(s32[4,8,16,4]{2,3,1,0:T(4,128)} %param.12) | copy-start | bytes 24580
  11.0 11.1 %copy-start.6 = (f32[1024]{0:T(1024)S(1)}, f32[1024]{0:T(1024)}, u32[]{:S(2)}) copy-start(f32[1024]{0:T(1024)} %param.16) | copy-start | bytes 12292
  13.0 23.4 %all-to-all-start = ((bf16[8,32,1152]{2,1,0:T(8,128)(2,1)}), bf16[8,32,1152]{2,1,0:T(8,128)(2,1)S(1)}, u32[]{:S(2)}, u32[]{:S(2)}) async-start(bf16[8,32,1152]{2,1,0:T(8,128)(2,1)} %pad_maximum_fusion.1), calls=%async_computation | async-start | bytes 1179648 | tf_op jit(solution)/shard_map/all_to_all | solution.py:120
  19.9 17.8 %collective-permute-start.1 = (bf16[512,1024]{1,0:T(8,128)(2,1)S(1)}, bf16[512,1024]{1,0:T(8,128)(2,1)}, u32[]{:S(2)}, u32[]{:S(2)}) collective-permute-start(bf16[512,1024]{1,0:T(8,128)(2,1)S(1)} %copy-done.1), channel_id=1, source_target_pairs={{0,1},{1,0},{2,3},{3,2},{4,5},{5,4},{6,7},{7,6},{8,9},{9,8},{10,11... | collective-permute-start | bytes 3145736 | tf_op jit(solution)/shard_map/ppermute | solution.py:67
  20.1 17.6 %collective-permute-start.2 = (bf16[1024,512]{1,0:T(8,128)(2,1)}, bf16[1024,512]{1,0:T(8,128)(2,1)}, u32[]{:S(2)}, u32[]{:S(2)}) collective-permute-start(bf16[1024,512]{1,0:T(8,128)(2,1)} %wh_a.1), channel_id=1, source_target_pairs={{0,1},{1,0},{2,3},{3,2},{4,5},{5,4},{6,7},{7,6},{8,9},{9,8},{10,11... | collective-permute-start | bytes 3145736 | tf_op jit(solution)/shard_map/ppermute | solution.py:67
  20.5 17.3 %collective-permute-start.4 = (bf16[512,1024]{1,0:T(8,128)(2,1)}, bf16[512,1024]{1,0:T(8,128)(2,1)}, u32[]{:S(2)}, u32[]{:S(2)}) collective-permute-start(bf16[512,1024]{1,0:T(8,128)(2,1)} %wo_a.1), channel_id=1, source_target_pairs={{0,1},{1,0},{2,3},{3,2},{4,5},{5,4},{6,7},{7,6},{8,9},{9,8},{10,11... | collective-permute-start | bytes 3145736 | tf_op jit(solution)/shard_map/ppermute | solution.py:67
  20.6 5.1 %collective-permute-start.3 = (bf16[18,512]{1,0:T(8,128)(2,1)S(1)}, bf16[18,512]{1,0:T(8,128)(2,1)S(1)}, u32[]{:S(2)}, u32[]{:S(2)}) collective-permute-start(bf16[18,512]{1,0:T(8,128)(2,1)S(1)} %copy-done.4), channel_id=1, source_target_pairs={{0,1},{1,0},{2,3},{3,2},{4,5},{5,4},{6,7},{7,6},{8,9},{9,8},{10,11... | collective-permute-start | bytes 55304 | tf_op jit(solution)/shard_map/ppermute | solution.py:67
  36.7 0.7 copy-start.7
  37.0 1.2 %copy-start.2 = (bf16[512,1024]{1,0:T(8,128)(2,1)S(1)}, bf16[512,1024]{1,0:T(8,128)(2,1)}, u32[]{:S(2)}) copy-start(bf16[512,1024]{1,0:T(8,128)(2,1)} %r_a.1) | copy-start | bytes 3145732
  54.8 2.9 %collective-permute-start.5 = (bf16[256,2048]{1,0:T(8,128)(2,1)}, bf16[256,2048]{1,0:T(8,128)(2,1)S(1)}, u32[]{:S(2)}, u32[]{:S(2)}) collective-permute-start(bf16[256,2048]{1,0:T(8,128)(2,1)} %get-tuple-element.8), channel_id=1, source_target_pairs={{0,1},{1,0},{2,3},{3,2},{4,5},{5,4},{6,7},{7,6},{8,9},{9,8},{10,11... | collective-permute-start | bytes 3145736 | tf_op jit(solution)/shard_map/ppermute | solution.py:67
  57.7 1.0 %copy-start.3 = (bf16[256,2048]{1,0:T(8,128)(2,1)}, bf16[256,2048]{1,0:T(8,128)(2,1)S(1)}, u32[]{:S(2)}) copy-start(bf16[256,2048]{1,0:T(8,128)(2,1)S(1)} %collective-permute-done.5) | copy-start | bytes 3145732

commit v10 on v8

--- a/solution.py
+++ b/solution.py
@@ -179,7 +179,7 @@
     horizon, rows, _ = hot_ref.shape
     half = r_a.shape[0]
     width = 2 * half
-    tile = 128
+    tile = 256
     lead = side_ref[0] == 0
 
     def dot(a, b):

time: 62.7 us -> 60.3 us (0.962)
  Pallas kernels: 19.7 us -> 17.3 us
    pallas_call x1, Pallas kernels: 16.5 us -> 14.1 us  [imagine(): pl.pallas_call(_imagine_kernel, out_shape=(out, out), in_specs=[pl.BlockS...]
where the time goes in v10:
time: 60.3 us; the launch traced here: 59.9 us
  Pallas kernels  17.3 us (29%)
  waiting for transfers between devices  17.2 us (29%)
  starting transfers between devices  8.5 us (14%)
  other arithmetic  8.28 us (14%)
  local copies, waits for them, and re-layouts  5.07 us (8%)
  matrix products  3.28 us (5%)
    pallas_call x1, Pallas kernels, imagine(): pl.pallas_call(_imagine_kernel, out_shape=(out, out), in_specs=[pl.BlockS...  14.1 us
    all_to_all x1, waiting for transfers between devices, per_device(): got = lax.all_to_all(send, 'tm', split_axis=0, concat_axis=0, tiled=True)  10.6 us
    all_to_all x1, starting transfers between devices, per_device(): got = lax.all_to_all(send, 'tm', split_axis=0, concat_axis=0, tiled=True)  6.92 us
    ppermute x6, waiting for transfers between devices, partner(): return lax.ppermute(x, 'mp', swap)  6.62 us
    dot_general x1, matrix products, per_device(): jnp.dot(x.reshape(bh * steps, feat), ip, preferred_element_type=jnp.float32)  3.28 us
    pallas_call x1, Pallas kernels, local_scan(): pl.pallas_call(_scan_kernel, out_shape=jax.ShapeDtypeStruct(driven.shape,...  3.13 us
    concatenate x1, other arithmetic, per_device(): return jnp.concatenate([first_half, second_half], axis=0)  2.67 us
    ppermute x6, starting transfers between devices, partner(): return lax.ppermute(x, 'mp', swap)  1.58 us
  transfers between devices with their start and end apart: 7, of which 3 were waited for; matrix products, arithmetic and copies ran while one was open for 8% of the time, Pallas kernels for 0%

profile of v10, /device:TPU:0, one launch (start us, length us, event | category | flops | bytes accessed | tf_op | source)
XLA Modules:
  0.0 59.9 jit_solution(4152011470054805852)
XLA Ops:
  0.0 0.5 collective-permute-start
  0.5 0.8 %fusion.14 = (s32[2]{0:T(128)S(1)}, f32[2,128]{1,0:T(2,128)S(1)}) fusion(s32[4,128]{1,0:T(4,128)} %param.11, s32[]{:T(128)S(6)} %select_n.48), kind=kLoop, calls=%fused_computation.48 | loop fusion | flops 1278 | bytes 2060 | tf_op jit(solution)/shard_map/reduce_min | solution.py:102
  1.3 0.8 %fusion.19 = (f32[512]{0:T(512)S(1)}, f32[512]{0:T(512)S(1)}) fusion(f32[1024]{0:T(1024)} %param.14, s32[]{:T(128)S(6)} %select_n.49, s32[]{:T(128)S(6)} %select_n.50), kind=kLoop, calls=%fused_computation.58 | loop fusion | bytes 8200 | tf_op jit(solution)/shard_map/dynamic_slice | solution.py:79
  2.2 1.1 %broadcast_multiply_fusion.g_ref = f32[2,128,1024]{2,1,0:T(8,128)} fusion(f32[1024]{0:T(1024)S(1)} %get-tuple-element.19, f32[2,128]{1,0:T(2,128)S(1)} %get-tuple-element.23), kind=kLoop, calls=%fused_computation.17 | loop fusion | flops 262144 | bytes 1053696 | tf_op jit(solution)/shard_map/mul | solution.py:98
  3.3 0.0 collective-permute-done.ip_b
  3.3 3.3 %fusion.3.x_ref = f32[2,128,1024]{2,1,0:T(8,128)} fusion(bf16[1024,512]{1,0:T(8,128)(2,1)S(1)} %collective-permute-done.ip_b, bf16[1024,512]{1,0:T(8,128)(2,1)} %ip_a.1, f32[1024]{0:T(1024)S(1)} %get-tuple-element.18, bf16[4,128,1024]{2,1,0:T(8,128)(2,1)S(1)} %copy-done, s32[]{:T(128)S(6)} %select_n.48), kind=kOutput, calls=%fused_computation.5 | convolution fusion | flops 541327360 | bytes 3674116 | tf_op jit(solution)/shard_map/dot_general | solution.py:91
  6.6 3.1 %shard_map.100 = f32[2,128,1024]{2,1,0:T(8,128)} custom-call(f32[2,128,1024]{2,1,0:T(8,128)} %fusion.3.x_ref, f32[2,128,1024]{2,1,0:T(8,128)} %broadcast_multiply_fusion.g_ref), custom_call_target="tpu_custom_call" | custom-call | flops 524288 | bytes 3145728 | tf_op jit(solution)/shard_map/pallas_call | solution.py:27
  9.7 1.3 %convert_element_type.65 = bf16[2,128,1024]{2,1,0:T(8,128)(2,1)S(1)} convert(f32[2,128,1024]{2,1,0:T(8,128)} %shard_map.100) | non-fusion elementwise | flops 262144 | bytes 1572864 | tf_op jit(solution)/shard_map/convert_element_type | solution.py:115
  11.0 0.0 copy-start.1
  11.0 0.0 copy-start.3
  11.0 0.0 copy-start.4
  11.0 0.0 copy-start.5
  11.1 0.9 %slice.56 = f32[2,1,1024]{2,1,0:T(1,128)S(1)} slice(f32[2,128,1024]{2,1,0:T(8,128)} %shard_map.100), slice={[0:2], [127:128], [0:1024]} | slice | bytes 16384 | tf_op jit(solution)/shard_map/slice | solution.py:104
  12.1 0.1 concatenate.66
  12.2 0.9 %pad_maximum_fusion.1 = bf16[8,32,1152]{2,1,0:T(8,128)(2,1)} fusion(bf16[8,32,128]{2,1,0:T(8,128)(2,1)S(1)} %broadcast_in_dim.38, bf16[8,32,1024]{2,1,0:T(8,128)(2,1)S(1)} %bitcast.52), kind=kLoop, calls=%fused_computation.12 | loop fusion | flops 1179648 | bytes 1179648 | tf_op jit(solution)/shard_map/concatenate | solution.py:116
  13.0 6.9 %all-to-all-start = ((bf16[8,32,1152]{2,1,0:T(8,128)(2,1)}), bf16[8,32,1152]{2,1,0:T(8,128)(2,1)S(1)}, u32[]{:S(2)}, u32[]{:S(2)}) async-start(bf16[8,32,1152]{2,1,0:T(8,128)(2,1)} %pad_maximum_fusion.1), calls=%async_computation | async-start | bytes 1179648 | tf_op jit(solution)/shard_map/all_to_all | solution.py:120
  19.9 0.2 collective-permute-start.1
  20.1 0.4 collective-permute-start.2
  20.5 0.1 collective-permute-start.4
  20.7 0.4 collective-permute-start.3
  21.0 0.1 reshape.188
  21.1 0.5 add_convert_fusion
  21.7 0.1 broadcast_power_fusion
  21.8 0.2 fusion.8.hot_ref
  22.1 3.7 %collective-permute-done.3 = bf16[18,512]{1,0:T(8,128)(2,1)S(1)} collective-permute-done((bf16[18,512]{1,0:T(8,128)(2,1)S(1)}, bf16[18,512]{1,0:T(8,128)(2,1)S(1)}, u32[]{:S(2)}, u32[]{:S(2)}) %collective-permute-start.3) | collective-permute-done | bytes 18464 | tf_op jit(solution)/shard_map/ppermute | solution.py:67
  25.8 10.6 %all-to-all-done = bf16[8,32,1152]{2,1,0:T(8,128)(2,1)S(1)} async-done(((bf16[8,32,1152]{2,1,0:T(8,128)(2,1)}), bf16[8,32,1152]{2,1,0:T(8,128)(2,1)S(1)}, u32[]{:S(2)}, u32[]{:S(2)}) %all-to-all-start) | async-done | bytes 589856 | tf_op jit(solution)/shard_map/all_to_all | solution.py:120
  36.5 0.1 slice.65
  36.6 0.1 reshape.186
  36.6 0.1 slice.52
  36.7 0.1 broadcast_multiply_fusion.1
  36.8 0.1 pad_multiply_fusion
  37.0 0.1 slice.59
  37.1 0.0 copy-start.2
  37.1 0.1 slice_add_fusion
  37.2 0.1 copy-done.6
  37.3 0.1 broadcast_compare_fusion
  37.4 0.2 fusion.4
  37.6 0.1 copy.14
  37.7 0.0 collective-permute-done.1.r_b
  37.7 0.0 collective-permute-done.4.wo_b
  37.7 0.6 copy-done.2
  38.3 14.1 %shard_map.101 = (bf16[4,256,512]{2,1,0:T(8,128)(2,1)S(1)}, bf16[4,256,512]{2,1,0:T(8,128)(2,1)}) custom-call(s32[1]{0:T(128)} %bitcast.side_ref, f32[256,1024]{1,0:T(8,128)S(1)} %bitcast.45, bf16[4,256,128]{2,1,0:T(8,128)(2,1)S(1)} %fusion.8.hot_ref, f32[3,1024]{1,0:T(4,128)S(1)} %pad_maximum_fusion.2.vec_ref, bf16[512,1024]{1,0:T(8,128)(2,1)S(1)} %copy-done.2, ...), custom_call_target="tpu_custom_call" | custom-call | flops 8589934592 | bytes 16777216 | tf_op jit(solution)/shard_map/pallas_call | solution.py:223
  52.4 0.0 collective-permute-start.5
  52.4 2.9 %collective-permute-done.5 = bf16[4,256,512]{2,1,0:T(8,128)(2,1)S(1)} collective-permute-done((bf16[4,256,512]{2,1,0:T(8,128)(2,1)}, bf16[4,256,512]{2,1,0:T(8,128)(2,1)S(1)}, u32[]{:S(2)}, u32[]{:S(2)}) %collective-permute-start.5) | collective-permute-done | bytes 1048608 | tf_op jit(solution)/shard_map/ppermute | solution.py:67
  55.3 0.1 broadcast_select_fusion.1
  55.4 0.9 %copy.22 = bf16[4,2,8,16,512]{4,0,3,2,1:T(4,128)(2,1)S(1)} copy(bf16[4,2,8,16,512]{4,3,2,1,0:T(8,128)(2,1)S(1)} %bitcast.47) | data formatting | bytes 2097152 | tf_op jit(solution)/shard_map/jit(_where)/select_n | solution.py:171
  56.3 0.9 %copy.23 = bf16[4,2,8,16,512]{4,0,3,2,1:T(4,128)(2,1)S(1)} copy(bf16[4,2,8,16,512]{4,3,2,1,0:T(8,128)(2,1)S(1)} %bitcast.46) | data formatting | bytes 2097152 | tf_op jit(solution)/shard_map/jit(_where)/select_n | solution.py:170
  57.2 2.7 %pad_maximum_fusion = bf16[4,8,16,4,512]{4,3,2,1,0:T(4,128)(2,1)} fusion(bf16[2,8,16,4,512]{4,3,2,1,0:T(4,128)(2,1)S(1)} %bitcast.48, bf16[2,8,16,4,512]{4,3,2,1,0:T(4,128)(2,1)S(1)} %bitcast.49), kind=kLoop, calls=%fused_computation.4 | loop fusion | flops 1048576 | bytes 4194304 | tf_op jit(solution)/shard_map/concatenate | solution.py:172
  (31 shorter events, 0.3 us)
Async XLA Ops:
  0.0 3.3 %copy-start = (bf16[4,128,1024]{2,1,0:T(8,128)(2,1)S(1)}, bf16[4,128,1024]{2,1,0:T(8,128)(2,1)}, u32[]{:S(2)}) copy-start(bf16[4,128,1024]{2,1,0:T(8,128)(2,1)} %param.10) | copy-start | bytes 3145732
  0.0 3.3 %collective-permute-start = (bf16[1024,512]{1,0:T(8,128)(2,1)}, bf16[1024,512]{1,0:T(8,128)(2,1)S(1)}, u32[]{:S(2)}, u32[]{:S(2)}) collective-permute-start(bf16[1024,512]{1,0:T(8,128)(2,1)} %ip_a.1), channel_id=1, source_target_pairs={{0,1},{1,0},{2,3},{3,2},{4,5},{5,4},{6,7},{7,6},{8,9},{9,8},{10,11... | collective-permute-start | bytes 3145736 | tf_op jit(solution)/shard_map/ppermute | solution.py:67
  3.3 3.3 %copy-start.7 = (bf16[1024,512]{1,0:T(8,128)(2,1)}, bf16[1024,512]{1,0:T(8,128)(2,1)S(1)}, u32[]{:S(2)}) copy-start(bf16[1024,512]{1,0:T(8,128)(2,1)S(1)} %collective-permute-done.ip_b) | copy-start | bytes 3145732
  11.0 8.9 %copy-start.1 = (bf16[512,1024]{1,0:T(8,128)(2,1)S(1)}, bf16[512,1024]{1,0:T(8,128)(2,1)}, u32[]{:S(2)}) copy-start(bf16[512,1024]{1,0:T(8,128)(2,1)} %r_a.1) | copy-start | bytes 3145732
  11.0 9.6 %copy-start.3 = (bf16[18,512]{1,0:T(8,128)(2,1)S(1)}, bf16[18,512]{1,0:T(8,128)(2,1)}, u32[]{:S(2)}) copy-start(bf16[18,512]{1,0:T(8,128)(2,1)} %param.18) | copy-start | bytes 55300
  11.0 10.0 %copy-start.4 = (s32[4,8,16,4]{2,3,1,0:T(4,128)S(1)}, s32[4,8,16,4]{2,3,1,0:T(4,128)}, u32[]{:S(2)}) copy-start(s32[4,8,16,4]{2,3,1,0:T(4,128)} %param.12) | copy-start | bytes 24580
  11.0 11.0 %copy-start.5 = (f32[1024]{0:T(1024)S(1)}, f32[1024]{0:T(1024)}, u32[]{:S(2)}) copy-start(f32[1024]{0:T(1024)} %param.16) | copy-start | bytes 12292
  13.0 23.4 %all-to-all-start = ((bf16[8,32,1152]{2,1,0:T(8,128)(2,1)}), bf16[8,32,1152]{2,1,0:T(8,128)(2,1)S(1)}, u32[]{:S(2)}, u32[]{:S(2)}) async-start(bf16[8,32,1152]{2,1,0:T(8,128)(2,1)} %pad_maximum_fusion.1), calls=%async_computation | async-start | bytes 1179648 | tf_op jit(solution)/shard_map/all_to_all | solution.py:120
  19.9 17.8 %collective-permute-start.1 = (bf16[512,1024]{1,0:T(8,128)(2,1)S(1)}, bf16[512,1024]{1,0:T(8,128)(2,1)}, u32[]{:S(2)}, u32[]{:S(2)}) collective-permute-start(bf16[512,1024]{1,0:T(8,128)(2,1)S(1)} %copy-done.1), channel_id=1, source_target_pairs={{0,1},{1,0},{2,3},{3,2},{4,5},{5,4},{6,7},{7,6},{8,9},{9,8},{10,11... | collective-permute-start | bytes 3145736 | tf_op jit(solution)/shard_map/ppermute | solution.py:67
  20.1 17.6 %collective-permute-start.2 = (bf16[1024,512]{1,0:T(8,128)(2,1)}, bf16[1024,512]{1,0:T(8,128)(2,1)}, u32[]{:S(2)}, u32[]{:S(2)}) collective-permute-start(bf16[1024,512]{1,0:T(8,128)(2,1)} %wh_a.1), channel_id=1, source_target_pairs={{0,1},{1,0},{2,3},{3,2},{4,5},{5,4},{6,7},{7,6},{8,9},{9,8},{10,11... | collective-permute-start | bytes 3145736 | tf_op jit(solution)/shard_map/ppermute | solution.py:67
  20.5 17.2 %collective-permute-start.4 = (bf16[512,1024]{1,0:T(8,128)(2,1)}, bf16[512,1024]{1,0:T(8,128)(2,1)}, u32[]{:S(2)}, u32[]{:S(2)}) collective-permute-start(bf16[512,1024]{1,0:T(8,128)(2,1)} %wo_a.1), channel_id=1, source_target_pairs={{0,1},{1,0},{2,3},{3,2},{4,5},{5,4},{6,7},{7,6},{8,9},{9,8},{10,11... | collective-permute-start | bytes 3145736 | tf_op jit(solution)/shard_map/ppermute | solution.py:67
  20.7 5.1 %collective-permute-start.3 = (bf16[18,512]{1,0:T(8,128)(2,1)S(1)}, bf16[18,512]{1,0:T(8,128)(2,1)S(1)}, u32[]{:S(2)}, u32[]{:S(2)}) collective-permute-start(bf16[18,512]{1,0:T(8,128)(2,1)S(1)} %copy-done.3), channel_id=1, source_target_pairs={{0,1},{1,0},{2,3},{3,2},{4,5},{5,4},{6,7},{7,6},{8,9},{9,8},{10,11... | collective-permute-start | bytes 55304 | tf_op jit(solution)/shard_map/ppermute | solution.py:67
  36.7 0.6 copy-start.6
  37.1 1.2 %copy-start.2 = (bf16[512,1024]{1,0:T(8,128)(2,1)S(1)}, bf16[512,1024]{1,0:T(8,128)(2,1)}, u32[]{:S(2)}) copy-start(bf16[512,1024]{1,0:T(8,128)(2,1)} %r_a.1) | copy-start | bytes 3145732
  52.4 2.9 %collective-permute-start.5 = (bf16[4,256,512]{2,1,0:T(8,128)(2,1)}, bf16[4,256,512]{2,1,0:T(8,128)(2,1)S(1)}, u32[]{:S(2)}, u32[]{:S(2)}) collective-permute-start(bf16[4,256,512]{2,1,0:T(8,128)(2,1)} %get-tuple-element.8), channel_id=1, source_target_pairs={{0,1},{1,0},{2,3},{3,2},{4,5},{5,4},{6,7},{7,6},{8,9},{9,8},{10,11... | collective-permute-start | bytes 3145736 | tf_op jit(solution)/shard_map/ppermute | solution.py:67

commit v11 on v10

--- a/solution.py
+++ b/solution.py
@@ -67,11 +67,9 @@
         return lax.ppermute(x, "mp", swap)
 
     half = in_proj.shape[1]
-    ip_o = partner(in_proj)
-    r_o = partner(readout_w)
-    wh_o = partner(w_hidden)
-    wo_o = partner(w_out)
-    emb_o = partner(action_embed)
+    ip_o, r_o, wh_o, wo_o, emb_o = lax.optimization_barrier(
+        partner((in_proj, readout_w, w_hidden, w_out, action_embed))
+    )
     ip = jnp.concatenate([in_proj, ip_o], axis=1)
 
     rates = jnp.concatenate(

time: 60.3 us -> 66.6 us (1.10)
  waiting for transfers between devices: 17.2 us -> 21.9 us
  other arithmetic: 8.28 us -> 9.01 us
    all_to_all x1, waiting for transfers between devices: 10.6 us -> 15.6 us  [per_device(): got = lax.all_to_all(send, 'tm', split_axis=0, concat_axis=0, tiled=True)]
    select_n x1, other arithmetic: 0.14 us -> 1.36 us  [per_device(): first_half = jnp.where(m == 0, mine, theirs)]
  transfers between devices with their start and end apart: 7 -> 7, of which waited for: 3 -> 3; matrix products, arithmetic and copies ran while one was open for 8% -> 5% of each run, Pallas kernels for 0% -> 0%
where the time goes in v11:
time: 66.6 us; the launch traced here: 66.1 us
  waiting for transfers between devices  21.9 us (33%)
  Pallas kernels  17 us (26%)
  other arithmetic  9.01 us (14%)
  starting transfers between devices  8.71 us (13%)
  local copies, waits for them, and re-layouts  5.53 us (8%)
  matrix products  3.64 us (5%)
    all_to_all x1, waiting for transfers between devices, per_device(): got = lax.all_to_all(send, 'tm', split_axis=0, concat_axis=0, tiled=True)  15.6 us
    pallas_call x1, Pallas kernels, imagine(): pl.pallas_call(_imagine_kernel, out_shape=(out, out), in_specs=[pl.BlockS...  13.8 us
    all_to_all x1, starting transfers between devices, per_device(): got = lax.all_to_all(send, 'tm', split_axis=0, concat_axis=0, tiled=True)  7.19 us
    ppermute x6, waiting for transfers between devices, partner(): return lax.ppermute(x, 'mp', swap)  6.33 us
    dot_general x1, matrix products, per_device(): jnp.dot(x.reshape(bh * steps, feat), ip, preferred_element_type=jnp.float32)  3.64 us
    pallas_call x1, Pallas kernels, local_scan(): pl.pallas_call(_scan_kernel, out_shape=jax.ShapeDtypeStruct(driven.shape,...  3.15 us
    concatenate x1, other arithmetic, per_device(): return jnp.concatenate([first_half, second_half], axis=0)  2.67 us
    ppermute x6, starting transfers between devices, partner(): return lax.ppermute(x, 'mp', swap)  1.52 us
  transfers between devices with their start and end apart: 7, of which 3 were waited for; matrix products, arithmetic and copies ran while one was open for 5% of the time, Pallas kernels for 0%

profile of v11, /device:TPU:0, one launch (start us, length us, event | category | flops | bytes accessed | tf_op | source)
XLA Modules:
  0.0 66.1 jit_solution(503409201044079694)
XLA Ops:
  0.0 0.0 copy-start
  0.0 0.5 collective-permute-start
  0.5 0.1 collective-permute-start.1
  0.6 0.4 collective-permute-start.2
  1.0 0.1 collective-permute-start.3
  1.1 0.4 collective-permute-start.4
  1.5 0.8 %fusion.14 = (s32[2]{0:T(128)S(1)}, f32[2,128]{1,0:T(2,128)S(1)}) fusion(s32[4,128]{1,0:T(4,128)} %param.11, s32[]{:T(128)S(6)} %select_n.48), kind=kLoop, calls=%fused_computation.48 | loop fusion | flops 1278 | bytes 2060 | tf_op jit(solution)/shard_map/reduce_min | solution.py:100
  2.3 0.8 %fusion.19 = (f32[512]{0:T(512)S(1)}, f32[512]{0:T(512)S(1)}) fusion(f32[1024]{0:T(1024)} %param.14, s32[]{:T(128)S(6)} %select_n.49, s32[]{:T(128)S(6)} %select_n.50), kind=kLoop, calls=%fused_computation.58 | loop fusion | bytes 8200 | tf_op jit(solution)/shard_map/dynamic_slice | solution.py:77
  3.2 1.1 %broadcast_multiply_fusion.g_ref = f32[2,128,1024]{2,1,0:T(8,128)} fusion(f32[1024]{0:T(1024)S(1)} %get-tuple-element.29, f32[2,128]{1,0:T(2,128)S(1)} %get-tuple-element.33), kind=kLoop, calls=%fused_computation.17 | loop fusion | flops 262144 | bytes 1053696 | tf_op jit(solution)/shard_map/mul | solution.py:96
  4.3 3.3 %collective-permute-done.4 = bf16[18,512]{1,0:T(8,128)(2,1)S(1)} collective-permute-done((bf16[18,512]{1,0:T(8,128)(2,1)}, bf16[18,512]{1,0:T(8,128)(2,1)S(1)}, u32[]{:S(2)}, u32[]{:S(2)}) %collective-permute-start.4) | collective-permute-done | bytes 18464 | tf_op jit(solution)/shard_map/ppermute | solution.py:67
  7.6 0.0 collective-permute-done.ip_b
  7.6 0.0 collective-permute-done.1.r_b
  7.6 0.0 collective-permute-done.2.wh_b
  7.6 0.0 collective-permute-done.3.wo_b
  7.7 3.6 %fusion.3.x_ref = f32[2,128,1024]{2,1,0:T(8,128)} fusion(bf16[1024,512]{1,0:T(8,128)(2,1)S(1)} %collective-permute-done.ip_b, bf16[1024,512]{1,0:T(8,128)(2,1)} %ip_a.1, f32[1024]{0:T(1024)S(1)} %get-tuple-element.28, bf16[4,128,1024]{2,1,0:T(8,128)(2,1)S(1)} %copy-done, s32[]{:T(128)S(6)} %select_n.48), kind=kOutput, calls=%fused_computation.5 | convolution fusion | flops 541327360 | bytes 3674116 | tf_op jit(solution)/shard_map/dot_general | solution.py:89
  11.3 3.1 %shard_map.100 = f32[2,128,1024]{2,1,0:T(8,128)} custom-call(f32[2,128,1024]{2,1,0:T(8,128)} %fusion.3.x_ref, f32[2,128,1024]{2,1,0:T(8,128)} %broadcast_multiply_fusion.g_ref), custom_call_target="tpu_custom_call" | custom-call | flops 524288 | bytes 3145728 | tf_op jit(solution)/shard_map/pallas_call | solution.py:27
  14.5 1.3 %convert_element_type.65 = bf16[2,128,1024]{2,1,0:T(8,128)(2,1)S(1)} convert(f32[2,128,1024]{2,1,0:T(8,128)} %shard_map.100) | non-fusion elementwise | flops 262144 | bytes 1572864 | tf_op jit(solution)/shard_map/convert_element_type | solution.py:113
  15.8 0.0 copy-start.5
  15.8 0.0 copy-start.6
  15.8 0.0 copy-start.4
  15.8 0.9 %slice.56 = f32[2,1,1024]{2,1,0:T(1,128)S(1)} slice(f32[2,128,1024]{2,1,0:T(8,128)} %shard_map.100), slice={[0:2], [127:128], [0:1024]} | slice | bytes 16384 | tf_op jit(solution)/shard_map/slice | solution.py:102
  16.7 0.1 concatenate.66
  16.8 0.9 %pad_maximum_fusion.1 = bf16[8,32,1152]{2,1,0:T(8,128)(2,1)} fusion(bf16[8,32,128]{2,1,0:T(8,128)(2,1)S(1)} %broadcast_in_dim.38, bf16[8,32,1024]{2,1,0:T(8,128)(2,1)S(1)} %bitcast.51), kind=kLoop, calls=%fused_computation.12 | loop fusion | flops 1179648 | bytes 1179648 | tf_op jit(solution)/shard_map/concatenate | solution.py:114
  17.7 7.2 %all-to-all-start = ((bf16[8,32,1152]{2,1,0:T(8,128)(2,1)}), bf16[8,32,1152]{2,1,0:T(8,128)(2,1)S(1)}, u32[]{:S(2)}, u32[]{:S(2)}) async-start(bf16[8,32,1152]{2,1,0:T(8,128)(2,1)} %pad_maximum_fusion.1), calls=%async_computation | async-start | bytes 1179648 | tf_op jit(solution)/shard_map/all_to_all | solution.py:118
  24.9 0.1 reshape.188
  25.1 0.1 broadcast_power_fusion
  25.2 0.2 fusion.8.hot_ref
  25.5 15.6 %all-to-all-done = bf16[8,32,1152]{2,1,0:T(8,128)(2,1)S(1)} async-done(((bf16[8,32,1152]{2,1,0:T(8,128)(2,1)}), bf16[8,32,1152]{2,1,0:T(8,128)(2,1)S(1)}, u32[]{:S(2)}, u32[]{:S(2)}) %all-to-all-start) | async-done | bytes 589856 | tf_op jit(solution)/shard_map/all_to_all | solution.py:118
  41.1 0.1 slice.65
  41.3 0.1 reshape.186
  41.3 0.1 slice.52
  41.4 0.1 broadcast_multiply_fusion.1
  41.5 0.1 pad_multiply_fusion
  41.7 0.1 slice_add_fusion
  41.8 0.1 broadcast_compare_fusion
  41.8 0.1 slice.59
  41.9 0.0 copy-start.1
  41.9 0.2 fusion.4
  42.1 0.1 copy.14
  42.2 0.9 %copy-done.1 = bf16[512,1024]{1,0:T(8,128)(2,1)S(1)} copy-done((bf16[512,1024]{1,0:T(8,128)(2,1)S(1)}, bf16[512,1024]{1,0:T(8,128)(2,1)}, u32[]{:S(2)}) %copy-start.1) | copy-done | bytes 1048600
  43.1 0.3 copy-done.3
  43.4 13.8 %shard_map.101 = (bf16[4,256,512]{2,1,0:T(8,128)(2,1)S(1)}, bf16[4,256,512]{2,1,0:T(8,128)(2,1)}) custom-call(s32[1]{0:T(128)} %bitcast.side_ref, f32[256,1024]{1,0:T(8,128)S(1)} %bitcast.45, bf16[4,256,128]{2,1,0:T(8,128)(2,1)S(1)} %fusion.8.hot_ref, f32[3,1024]{1,0:T(4,128)S(1)} %pad_maximum_fusion.2.vec_ref, bf16[512,1024]{1,0:T(8,128)(2,1)S(1)} %copy-done.1, ...), custom_call_target="tpu_custom_call" | custom-call | flops 8589934592 | bytes 16777216 | tf_op jit(solution)/shard_map/pallas_call | solution.py:221
  57.3 0.0 collective-permute-start.5
  57.3 3.0 %collective-permute-done.5 = bf16[4,256,512]{2,1,0:T(8,128)(2,1)} collective-permute-done((bf16[4,256,512]{2,1,0:T(8,128)(2,1)}, bf16[4,256,512]{2,1,0:T(8,128)(2,1)}, u32[]{:S(2)}, u32[]{:S(2)}) %collective-permute-start.5) | collective-permute-done | bytes 1048608 | tf_op jit(solution)/shard_map/ppermute | solution.py:67
  60.3 1.4 %broadcast_select_fusion.1 = (bf16[4,256,512]{2,1,0:T(8,128)(2,1)S(1)}, bf16[4,256,512]{2,1,0:T(8,128)(2,1)S(1)}) fusion(bf16[4,256,512]{2,1,0:T(8,128)(2,1)S(1)} %get-tuple-element.17, bf16[4,256,512]{2,1,0:T(8,128)(2,1)} %collective-permute-done.5, pred[]{:T(512)S(6)} %eq.8), kind=kLoop, calls=%fused_computation.11 | loop fusion | flops 1048576 | bytes 4194305 | tf_op jit(solution)/shard_map/jit(_where)/select_n | solution.py:168
  61.6 0.9 %copy.22 = bf16[4,2,8,16,512]{4,0,3,2,1:T(4,128)(2,1)S(1)} copy(bf16[4,2,8,16,512]{4,3,2,1,0:T(8,128)(2,1)S(1)} %bitcast.47) | data formatting | bytes 2097152 | tf_op jit(solution)/shard_map/jit(_where)/select_n | solution.py:169
  62.5 0.9 %copy.23 = bf16[4,2,8,16,512]{4,0,3,2,1:T(4,128)(2,1)S(1)} copy(bf16[4,2,8,16,512]{4,3,2,1,0:T(8,128)(2,1)S(1)} %bitcast.46) | data formatting | bytes 2097152 | tf_op jit(solution)/shard_map/jit(_where)/select_n | solution.py:168
  63.4 2.7 %pad_maximum_fusion = bf16[4,8,16,4,512]{4,3,2,1,0:T(4,128)(2,1)} fusion(bf16[2,8,16,4,512]{4,3,2,1,0:T(4,128)(2,1)S(1)} %bitcast.48, bf16[2,8,16,4,512]{4,3,2,1,0:T(4,128)(2,1)S(1)} %bitcast.49), kind=kLoop, calls=%fused_computation.4 | loop fusion | flops 1048576 | bytes 4194304 | tf_op jit(solution)/shard_map/concatenate | solution.py:170
  (31 shorter events, 0.3 us)
Async XLA Ops:
  0.0 7.7 %copy-start = (bf16[4,128,1024]{2,1,0:T(8,128)(2,1)S(1)}, bf16[4,128,1024]{2,1,0:T(8,128)(2,1)}, u32[]{:S(2)}) copy-start(bf16[4,128,1024]{2,1,0:T(8,128)(2,1)} %param.10) | copy-start | bytes 3145732
  0.0 7.6 %collective-permute-start = (bf16[1024,512]{1,0:T(8,128)(2,1)}, bf16[1024,512]{1,0:T(8,128)(2,1)S(1)}, u32[]{:S(2)}, u32[]{:S(2)}) collective-permute-start(bf16[1024,512]{1,0:T(8,128)(2,1)} %ip_a.1), channel_id=1, source_target_pairs={{0,1},{1,0},{2,3},{3,2},{4,5},{5,4},{6,7},{7,6},{8,9},{9,8},{10,11... | collective-permute-start | bytes 3145736 | tf_op jit(solution)/shard_map/ppermute | solution.py:67
  0.5 7.1 %collective-permute-start.1 = (bf16[512,1024]{1,0:T(8,128)(2,1)}, bf16[512,1024]{1,0:T(8,128)(2,1)S(1)}, u32[]{:S(2)}, u32[]{:S(2)}) collective-permute-start(bf16[512,1024]{1,0:T(8,128)(2,1)} %r_a.1), channel_id=1, source_target_pairs={{0,1},{1,0},{2,3},{3,2},{4,5},{5,4},{6,7},{7,6},{8,9},{9,8},{10,11... | collective-permute-start | bytes 3145736 | tf_op jit(solution)/shard_map/ppermute | solution.py:67
  0.6 7.1 %collective-permute-start.2 = (bf16[1024,512]{1,0:T(8,128)(2,1)}, bf16[1024,512]{1,0:T(8,128)(2,1)}, u32[]{:S(2)}, u32[]{:S(2)}) collective-permute-start(bf16[1024,512]{1,0:T(8,128)(2,1)} %wh_a.1), channel_id=1, source_target_pairs={{0,1},{1,0},{2,3},{3,2},{4,5},{5,4},{6,7},{7,6},{8,9},{9,8},{10,11... | collective-permute-start | bytes 3145736 | tf_op jit(solution)/shard_map/ppermute | solution.py:67
  1.0 6.6 %collective-permute-start.3 = (bf16[512,1024]{1,0:T(8,128)(2,1)}, bf16[512,1024]{1,0:T(8,128)(2,1)}, u32[]{:S(2)}, u32[]{:S(2)}) collective-permute-start(bf16[512,1024]{1,0:T(8,128)(2,1)} %wo_a.1), channel_id=1, source_target_pairs={{0,1},{1,0},{2,3},{3,2},{4,5},{5,4},{6,7},{7,6},{8,9},{9,8},{10,11... | collective-permute-start | bytes 3145736 | tf_op jit(solution)/shard_map/ppermute | solution.py:67
  1.1 6.5 %collective-permute-start.4 = (bf16[18,512]{1,0:T(8,128)(2,1)}, bf16[18,512]{1,0:T(8,128)(2,1)S(1)}, u32[]{:S(2)}, u32[]{:S(2)}) collective-permute-start(bf16[18,512]{1,0:T(8,128)(2,1)} %param.18), channel_id=1, source_target_pairs={{0,1},{1,0},{2,3},{3,2},{4,5},{5,4},{6,7},{7,6},{8,9},{9,8},{10,11... | collective-permute-start | bytes 55304 | tf_op jit(solution)/shard_map/ppermute | solution.py:67
  7.6 3.7 %copy-start.7 = (bf16[1024,512]{1,0:T(8,128)(2,1)}, bf16[1024,512]{1,0:T(8,128)(2,1)S(1)}, u32[]{:S(2)}) copy-start(bf16[1024,512]{1,0:T(8,128)(2,1)S(1)} %collective-permute-done.ip_b) | copy-start | bytes 3145732
  7.6 3.7 %copy-start.2 = (bf16[512,1024]{1,0:T(8,128)(2,1)}, bf16[512,1024]{1,0:T(8,128)(2,1)S(1)}, u32[]{:S(2)}) copy-start(bf16[512,1024]{1,0:T(8,128)(2,1)S(1)} %collective-permute-done.1.r_b) | copy-start | bytes 3145732
  15.8 9.1 %copy-start.5 = (s32[4,8,16,4]{2,3,1,0:T(4,128)S(1)}, s32[4,8,16,4]{2,3,1,0:T(4,128)}, u32[]{:S(2)}) copy-start(s32[4,8,16,4]{2,3,1,0:T(4,128)} %param.12) | copy-start | bytes 24580
  15.8 9.3 %copy-start.6 = (f32[1024]{0:T(1024)S(1)}, f32[1024]{0:T(1024)}, u32[]{:S(2)}) copy-start(f32[1024]{0:T(1024)} %param.16) | copy-start | bytes 12292
  15.8 9.7 %copy-start.4 = (bf16[18,512]{1,0:T(8,128)(2,1)S(1)}, bf16[18,512]{1,0:T(8,128)(2,1)}, u32[]{:S(2)}) copy-start(bf16[18,512]{1,0:T(8,128)(2,1)} %param.18) | copy-start | bytes 55300
  17.7 23.4 %all-to-all-start = ((bf16[8,32,1152]{2,1,0:T(8,128)(2,1)}), bf16[8,32,1152]{2,1,0:T(8,128)(2,1)S(1)}, u32[]{:S(2)}, u32[]{:S(2)}) async-start(bf16[8,32,1152]{2,1,0:T(8,128)(2,1)} %pad_maximum_fusion.1), calls=%async_computation | async-start | bytes 1179648 | tf_op jit(solution)/shard_map/all_to_all | solution.py:118
  41.9 1.2 %copy-start.1 = (bf16[512,1024]{1,0:T(8,128)(2,1)S(1)}, bf16[512,1024]{1,0:T(8,128)(2,1)}, u32[]{:S(2)}) copy-start(bf16[512,1024]{1,0:T(8,128)(2,1)} %r_a.1) | copy-start | bytes 3145732
  41.9 1.5 %copy-start.3 = (bf16[512,1024]{1,0:T(8,128)(2,1)S(1)}, bf16[512,1024]{1,0:T(8,128)(2,1)}, u32[]{:S(2)}) copy-start(bf16[512,1024]{1,0:T(8,128)(2,1)} %copy-done.2) | copy-start | bytes 3145732
  57.3 3.0 %collective-permute-start.5 = (bf16[4,256,512]{2,1,0:T(8,128)(2,1)}, bf16[4,256,512]{2,1,0:T(8,128)(2,1)}, u32[]{:S(2)}, u32[]{:S(2)}) collective-permute-start(bf16[4,256,512]{2,1,0:T(8,128)(2,1)} %get-tuple-element.18), channel_id=1, source_target_pairs={{0,1},{1,0},{2,3},{3,2},{4,5},{5,4},{6,7},{7,6},{8,9},{9,8},{10,11... | collective-permute-start | bytes 3145736 | tf_op jit(solution)/shard_map/ppermute | solution.py:67
